TPU v7x, 128 devices: a whole 4x4x4 slice. The times are simulated.
128 devices in a mesh: dp: 32 (over x, z, core), tensor: 4 (over y).
Axes of the slice: x: 4, y: 4, z: 4, core: 2. Of those that a mesh axis runs over, the one named last changes fastest.
Arguments:
- hidden_in: bfloat16 [768, 4096], P('dp'), may hold values from -6 to 6
- queries: bfloat16 [768, 8192], P('dp', 'tensor'), may hold values from -150 to 150
- key_cache: bfloat16 [768, 4, 768, 128], P('dp', 'tensor'), may hold values from -5 to 5
- cached_value_rows: bfloat16 [768, 4, 768, 128], P('dp', 'tensor'), may hold values from -6 to 6
- cache_lengths: int32 [768], P('dp'), may hold values from 48 to 768, as said below
- out_weight: bfloat16 [8192, 4096], P('tensor', 'dp'), may hold values from -0.0625 to 0.0625
- expert_ids: int32 [768, 8], P('dp'), may hold values from 0 to 127, as said below
- route_probs: float32 [768, 8], P('dp'), may hold values from 0.05 to 1
- w_gate: bfloat16 [128, 4096, 768], P(('dp', 'tensor')), may hold values from -0.09375 to 0.09375
- w_up: bfloat16 [128, 4096, 768], P(('dp', 'tensor')), may hold values from -0.09375 to 0.09375
- w_down: bfloat16 [128, 768, 4096], P(('dp', 'tensor')), may hold values from -0.21875 to 0.21875
Outputs:
- layer_out: bfloat16 [768, 4096], P('dp', 'tensor')
Inputs may be any that keep to these rules, and one draw needn't show every extreme that they name: `expert_ids`: each row names 8 different experts; among the rows of one index of dp no expert is named more than 2 times, and one expert is named exactly 2 times in every such group of rows. Row r attends to cache positions 0 to cache_lengths[r] - 1; some row has all 768.
All inputs are finite; a program needn't handle non-finite values.
Results may differ from a plain program's by a relative error of at most 0.01.
Values may be sent and summed in bfloat16 or wider, within the bound.
No kernel may reach another device: no remote copies, remote signals or barrier semaphores. Data moves between devices by JAX's collectives and lax.ppermute only.
A program may use at most 128 MiB of HBM per device.

v0:
```python
import math

import jax
import jax.numpy as jnp
from jax import lax
from jax.sharding import PartitionSpec as P

CAP = 2


def residual_norm(hidden_rows, projected):
    residual = (hidden_rows.astype(jnp.float32) + projected.astype(jnp.float32)).astype(
        jnp.bfloat16
    )
    resid_f = residual.astype(jnp.float32)
    normed = (
        resid_f * lax.rsqrt(jnp.mean(resid_f * resid_f, axis=-1, keepdims=True) + 1e-06)
    ).astype(jnp.bfloat16)
    return (residual, normed)


def local(
    hidden_in,
    queries,
    key_cache,
    cached_value_rows,
    cache_lengths,
    out_weight,
    expert_ids,
    route_probs,
    w_gate,
    w_up,
    w_down,
):
    dp_count = lax.axis_size("dp")
    tp_count = lax.axis_size("tensor")
    tp_rank = lax.axis_index("tensor")
    rows_dev, kv_local, cache_len, head_dim = key_cache.shape
    groups = queries.shape[1] // (kv_local * head_dim)
    model_width = hidden_in.shape[1]
    col_block = model_width // dp_count
    query_head_count = queries.reshape(rows_dev, kv_local, groups, head_dim)
    scores = jnp.einsum(
        "rhgd,rhld->rhgl", query_head_count, key_cache, preferred_element_type=jnp.float32
    ) * (1.0 / math.sqrt(head_dim))
    valid_mask = (jnp.arange(cache_len, dtype=jnp.int32)[None, :] < cache_lengths[:, None])[
        :, None, None, :
    ]
    scores = jnp.where(valid_mask, scores, -jnp.inf)
    largest = jnp.max(scores, axis=-1, keepdims=True)
    exponent = jnp.exp(scores - largest)
    attn_probs = (exponent / jnp.sum(exponent, axis=-1, keepdims=True)).astype(jnp.bfloat16)
    attn_out = jnp.einsum(
        "rhgl,rhld->rhgd", attn_probs, cached_value_rows, preferred_element_type=jnp.float32
    ).astype(jnp.bfloat16)
    attn_out = attn_out.reshape(rows_dev, kv_local * groups * head_dim)
    partial_value = jnp.dot(
        lax.all_gather(attn_out, "dp", axis=0, tiled=True),
        out_weight,
        preferred_element_type=jnp.float32,
    )
    partial_value = partial_value.reshape(dp_count, rows_dev, col_block)
    summed = lax.psum(partial_value.astype(jnp.bfloat16), "tensor")
    arrived = lax.all_to_all(summed, "dp", split_axis=0, concat_axis=2, tiled=True)
    residual, normed = residual_norm(hidden_in, arrived.reshape(rows_dev, model_width))
    exp_dev = w_gate.shape[0]
    owned = (
        (jnp.arange(dp_count, dtype=jnp.int32)[:, None] * tp_count + tp_rank) * exp_dev
        + jnp.arange(exp_dev, dtype=jnp.int32)[None, :]
    ).reshape(-1)
    matches = expert_ids[:, :, None] == owned[None, None, :]
    assigned = jnp.sum(matches.astype(jnp.int32), axis=1)
    slot_rank = jnp.cumsum(assigned, axis=0) - assigned
    slot_hit = (slot_rank[:, :, None] == jnp.arange(CAP, dtype=jnp.int32)[None, None, :]) & (
        assigned[:, :, None] > 0
    )
    route_weights = route_probs / jnp.sum(route_probs, axis=-1, keepdims=True)
    owned_weight = jnp.sum(jnp.where(matches, route_weights[:, :, None], 0.0), axis=1)
    outgoing = jnp.einsum(
        "rmc,rd->mcd", slot_hit.astype(jnp.bfloat16), normed, preferred_element_type=jnp.float32
    ).astype(jnp.bfloat16)
    outgoing = outgoing.reshape(dp_count, exp_dev, CAP, model_width)
    arrived_slots = lax.all_to_all(outgoing, "dp", split_axis=0, concat_axis=0, tiled=True)
    gate_proj = jnp.einsum(
        "sjcd,jdf->sjcf", arrived_slots, w_gate, preferred_element_type=jnp.float32
    )
    up_proj = jnp.einsum("sjcd,jdf->sjcf", arrived_slots, w_up, preferred_element_type=jnp.float32)
    activated = (jax.nn.silu(gate_proj) * up_proj).astype(jnp.bfloat16)
    expert_out = jnp.einsum(
        "sjcf,jfd->sjcd", activated, w_down, preferred_element_type=jnp.float32
    ).astype(jnp.bfloat16)
    results = lax.all_to_all(expert_out, "dp", split_axis=0, concat_axis=0, tiled=True)
    combine_table = jnp.where(slot_hit, owned_weight[:, :, None], 0.0)
    mixture = jnp.einsum(
        "rmc,mcd->rd",
        combine_table,
        results.reshape(dp_count * exp_dev, CAP, model_width).astype(jnp.float32),
        precision=lax.Precision.HIGHEST,
    )
    mixture_own = lax.psum_scatter(
        mixture.astype(jnp.bfloat16), "tensor", scatter_dimension=1, tiled=True
    ).astype(jnp.float32)
    width_share = model_width // tp_count
    residual_own = lax.dynamic_slice_in_dim(residual, tp_rank * width_share, width_share, 1)
    return (residual_own.astype(jnp.float32) + mixture_own).astype(jnp.bfloat16)


def solution(mesh):
    placed = (
        P("dp", None),
        P("dp", "tensor"),
        P("dp", "tensor", None, None),
        P("dp", "tensor", None, None),
        P("dp"),
        P("tensor", "dp"),
        P("dp", None),
        P("dp", None),
        P(("dp", "tensor"), None, None),
        P(("dp", "tensor"), None, None),
        P(("dp", "tensor"), None, None),
    )
    return jax.shard_map(
        local, mesh=mesh, in_specs=placed, out_specs=P("dp", "tensor"), check_vma=False
    )
```

profile of v0, /device:TPU:1, one launch (start us, length us, event | category | flops | bytes accessed | tf_op | source)
XLA Modules:
  0.0 194.0 jit_solution(4893107147027439860)
XLA Ops:
  6.5 0.0 copy-start
  6.5 0.0 all-gather.2.cloned.1.call-start
  6.5 1.0 copy.29
  7.5 0.7 iota_compare_fusion
  8.2 3.8 %fusion.83 = (f32[24,16]{1,0:T(8,128)S(1)}, f32[24,16,768]{2,1,0:T(8,128)S(1)}) fusion(bf16[24,16,128]{2,1,0:T(8,128)(2,1)S(1)} %bitcast.114, bf16[24,1,768,128]{3,2,1,0:T(8,128)(2,1)} %param.13, pred[24,768]{1,0:T(8,128)(4,1)S(1)} %iota_compare_fusion), kind=kOutput, calls=%fused_computation.73 | convolution fusion | flops 76677888 | bytes 6016512 | tf_op jit(solution)/shard_map/sub | solution.py:51
  12.1 0.0 copy-start.3
  12.1 3.1 %fusion.39 = bf16[24,16,128]{2,1,0:T(8,128)(2,1)S(1)} fusion(bf16[24,1,768,128]{3,2,1,0:T(8,128)(2,1)} %param.14, f32[24,16,768]{2,1,0:T(8,128)S(1)} %get-tuple-element.8, f32[24,16]{1,0:T(8,128)S(1)} %get-tuple-element.7), kind=kOutput, calls=%fused_computation.27 | convolution fusion | flops 76136448 | bytes 5998080 | tf_op jit(solution)/shard_map/rhgl,rhld->rhgd/dot_general | solution.py:53
  15.2 0.0 copy-start.1
  15.3 0.7 copy.48
  15.9 0.0 all-gather.2.cloned.1.call-update
  15.9 0.0 all-reduce.2.cloned.1.call-start
  16.0 0.0 copy-done.3
  16.0 0.1 copy.23
  16.1 48.5 %all-gather.2.cloned.1.call-done = bf16[768,2048]{1,0:T(8,128)(2,1)} async-done(((bf16[24,2048]{1,0:T(8,128)(2,1)}), bf16[768,2048]{1,0:T(8,128)(2,1)}) %all-gather.2.cloned.1.call-update) | async-done | bytes 3145744 | tf_op jit(solution)/shard_map/all_gather | solution.py:58
  64.6 0.0 copy-done
  64.6 3.5 %convolution_convert_fusion.1 = bf16[768,128]{1,0:T(8,128)(2,1)} fusion(bf16[768,2048]{1,0:T(8,128)(2,1)} %all-gather.2.cloned.1.call-done, bf16[2048,128]{1,0:T(8,128)(2,1)S(1)} %copy-done), kind=kOutput, calls=%fused_computation.22 | convolution fusion | flops 402751488 | bytes 3866624 | tf_op jit(solution)/shard_map/dot_general | solution.py:57
  68.2 0.0 all-reduce.2.cloned.1.call-update
  68.2 0.1 fusion.67
  68.4 38.4 %all-reduce.2.cloned.1.call-done = bf16[32,24,128]{2,1,0:T(8,128)(2,1)} async-done(((bf16[32,24,128]{2,1,0:T(8,128)(2,1)}), bf16[32,24,128]{2,1,0:T(8,128)(2,1)}) %all-reduce.2.cloned.1.call-update) | async-done | bytes 196624 | tf_op jit(solution)/shard_map/psum | solution.py:63
  106.8 9.8 %all-to-all-start = ((bf16[32,24,128]{2,1,0:T(8,128)(2,1)}), bf16[32,24,128]{2,1,0:T(8,128)(2,1)S(1)}, u32[]{:S(2)}, u32[]{:S(2)}) async-start(bf16[32,24,128]{2,1,0:T(8,128)(2,1)} %all-reduce.2.cloned.1.call-done), calls=%async_computation | async-start | bytes 393216 | tf_op jit(solution)/shard_map/all_to_all | solution.py:64
  116.6 8.3 %all-to-all-done = bf16[32,24,128]{2,1,0:T(8,128)(2,1)S(1)} async-done(((bf16[32,24,128]{2,1,0:T(8,128)(2,1)}), bf16[32,24,128]{2,1,0:T(8,128)(2,1)S(1)}, u32[]{:S(2)}, u32[]{:S(2)}) %all-to-all-start) | async-done | bytes 196640 | tf_op jit(solution)/shard_map/all_to_all | solution.py:64
  124.9 0.1 copy.22
  125.0 0.0 copy-done.1
  125.0 0.3 fusion.56
  125.3 0.4 fusion.14
  125.7 0.5 copy.25
  126.3 15.1 %all_to_all.19 = bf16[32,1,2,4096]{3,2,1,0:T(2,128)(2,1)S(1)} all-to-all(bf16[32,1,2,4096]{3,2,1,0:T(2,128)(2,1)S(1)} %copy.25), channel_id=1, replica_groups=mesh['dp'=32,'tensor'=4] {'dp'}, dimensions={0} | all-to-all | bytes 1048576 | tf_op jit(solution)/shard_map/all_to_all | solution.py:83
  141.4 4.2 %fusion.27 = f32[32,1,2,768]{3,0,2,1:T(8,128)S(1)} fusion(bf16[1,4096,768]{2,1,0:T(8,128)(2,1)} %param.19, bf16[32,1,2,4096]{3,2,1,0:T(2,128)(2,1)S(1)} %all_to_all.19), kind=kOutput, calls=%fused_computation.23 | convolution fusion | flops 402653184 | bytes 7012352 | tf_op jit(solution)/shard_map/sjcd,jdf->sjcf/dot_general | solution.py:84
  145.6 0.0 copy-start.2
  145.6 7.6 %fusion.15 = bf16[32,1,2,4096]{3,0,2,1:T(8,128)(2,1)S(1)} fusion(bf16[1,768,4096]{2,1,0:T(8,128)(2,1)} %param.21, bf16[1,4096,768]{2,1,0:T(8,128)(2,1)} %param.20, bf16[32,1,2,4096]{3,2,1,0:T(2,128)(2,1)S(1)} %all_to_all.19, f32[32,1,2,768]{3,0,2,1:T(8,128)S(1)} %fusion.27), kind=kOutput, calls=%fused_computation.14 | convolution fusion | flops 805863424 | bytes 13828096 | tf_op jit(solution)/shard_map/sjcf,jfd->sjcd/dot_general | solution.py:89
  153.1 1.3 copy.27
  154.5 3.7 %all-to-all-start.2 = ((bf16[32,1,2,4096]{3,2,1,0:T(2,128)(2,1)}), bf16[32,1,2,4096]{3,2,1,0:T(2,128)(2,1)S(1)}, u32[]{:S(2)}, u32[]{:S(2)}) async-start(bf16[32,1,2,4096]{3,2,1,0:T(2,128)(2,1)} %copy.27), calls=%async_computation.2 | async-start | bytes 1048576 | tf_op jit(solution)/shard_map/all_to_all | solution.py:92
  158.2 0.0 reduce-scatter.2.cloned.1.call-start
  158.2 0.0 copy-done.2
  158.3 0.1 copy.24
  158.3 0.1 fusion.68
  158.5 11.2 %all-to-all-done.2 = bf16[32,1,2,4096]{3,2,1,0:T(2,128)(2,1)S(1)} async-done(((bf16[32,1,2,4096]{3,2,1,0:T(2,128)(2,1)}), bf16[32,1,2,4096]{3,2,1,0:T(2,128)(2,1)S(1)}, u32[]{:S(2)}, u32[]{:S(2)}) %all-to-all-start.2) | async-done | bytes 524320 | tf_op jit(solution)/shard_map/all_to_all | solution.py:92
  169.7 1.3 fusion.18
  171.0 0.0 reduce-scatter.2.cloned.1.call-update
  171.0 15.0 %reduce-scatter.2.cloned.1.call-done = bf16[24,1024]{1,0:T(8,128)(2,1)} async-done(((bf16[24,4096]{1,0:T(8,128)(2,1)}), bf16[24,1024]{1,0:T(8,128)(2,1)}) %reduce-scatter.2.cloned.1.call-update) | async-done | bytes 49168 | tf_op jit(solution)/shard_map/reduce_scatter | solution.py:100
  186.0 1.4 add_convert_fusion
  (8 shorter events, 0.1 us)
Async XLA Ops:
  6.5 58.1 %copy-start = (bf16[2048,128]{1,0:T(8,128)(2,1)S(1)}, bf16[2048,128]{1,0:T(8,128)(2,1)}, u32[]{:S(2)}) copy-start(bf16[2048,128]{1,0:T(8,128)(2,1)} %param.16) | copy-start | bytes 1572868
  6.5 58.1 %all-gather.2.cloned.1.call-start = ((), (), s32[]{:S(2)}) async-start(), calls=%async_computation.4 | async-start | bytes 3244032 | tf_op jit(solution)/shard_map/all_gather | solution.py:58
  12.1 3.9 %copy-start.3 = (s32[24,8]{0,1:T(8,128)S(1)}, s32[24,8]{0,1:T(8,128)}, u32[]{:S(2)}) copy-start(s32[24,8]{0,1:T(8,128)} %param.17) | copy-start | bytes 2308
  15.2 109.7 %copy-start.1 = (bf16[24,4096]{1,0:T(8,128)(2,1)S(1)}, bf16[24,4096]{1,0:T(8,128)(2,1)}, u32[]{:S(2)}) copy-start(bf16[24,4096]{1,0:T(8,128)(2,1)} %param.11) | copy-start | bytes 589828
  15.9 90.9 %all-reduce.2.cloned.1.call-start = ((), (), s32[]{:S(2)}) async-start(), calls=%async_computation.5 | async-start | bytes 393216 | tf_op jit(solution)/shard_map/psum | solution.py:63
  106.8 18.1 %all-to-all-start = ((bf16[32,24,128]{2,1,0:T(8,128)(2,1)}), bf16[32,24,128]{2,1,0:T(8,128)(2,1)S(1)}, u32[]{:S(2)}, u32[]{:S(2)}) async-start(bf16[32,24,128]{2,1,0:T(8,128)(2,1)} %all-reduce.2.cloned.1.call-done), calls=%async_computation | async-start | bytes 393216 | tf_op jit(solution)/shard_map/all_to_all | solution.py:64
  145.6 12.6 %copy-start.2 = (f32[24,8]{0,1:T(8,128)S(1)}, f32[24,8]{0,1:T(8,128)}, u32[]{:S(2)}) copy-start(f32[24,8]{0,1:T(8,128)} %param.18) | copy-start | bytes 2308
  154.5 15.2 %all-to-all-start.2 = ((bf16[32,1,2,4096]{3,2,1,0:T(2,128)(2,1)}), bf16[32,1,2,4096]{3,2,1,0:T(2,128)(2,1)S(1)}, u32[]{:S(2)}, u32[]{:S(2)}) async-start(bf16[32,1,2,4096]{3,2,1,0:T(2,128)(2,1)} %copy.27), calls=%async_computation.2 | async-start | bytes 1048576 | tf_op jit(solution)/shard_map/all_to_all | solution.py:92
  158.2 27.8 %reduce-scatter.2.cloned.1.call-start = ((), (), s32[]{:S(2)}) async-start(), calls=%async_computation.6 | async-start | bytes 245760 | tf_op jit(solution)/shard_map/reduce_scatter | solution.py:100
Sparse Core Ops, SparseCore 0:
  16.1 48.5 all-gather.1
  68.3 38.4 all-reduce.1
  171.1 14.8 reduce-scatter.1
where the time goes:
time: 196 us; the launch traced here: 194 us
  waiting for transfers between devices  122 us (62%)
  matrix products  23.9 us (12%)
  blocking collectives  15.1 us (8%)
  starting transfers between devices  13.5 us (7%)
  between operations  13.3 us (7%)
  local copies, waits for them, and re-layouts  3.74 us (2%)
  other arithmetic  2.88 us (1%)
    all_gather x1, waiting for transfers between devices, local(): lax.all_gather(attn_out, 'dp', axis=0, tiled=True)  48.5 us
    psum x1, waiting for transfers between devices, local(): summed = lax.psum(partial_value.astype(jnp.bfloat16), 'tensor')  38.4 us
    all_to_all x1, blocking collectives, local(): lax.all_to_all(outgoing, 'dp', split_axis=0, concat_axis=0, tiled=True)  15.1 us
    reduce_scatter x1, waiting for transfers between devices, local(): lax.psum_scatter(mixture.astype(jnp.bfloat16), 'tensor', scatter_dimensio...  15 us
    all_to_all x1, waiting for transfers between devices, local(): lax.all_to_all(expert_out, 'dp', split_axis=0, concat_axis=0, tiled=True)  11.2 us
    all_to_all x1, starting transfers between devices, local(): lax.all_to_all(summed, 'dp', split_axis=0, concat_axis=2, tiled=True)  9.77 us
    all_to_all x1, waiting for transfers between devices, local(): lax.all_to_all(summed, 'dp', split_axis=0, concat_axis=2, tiled=True)  8.29 us
    dot_general x1, matrix products, local(): jnp.einsum('sjcf,jfd->sjcd', activated, w_down, preferred_element_type=jn...  7.55 us
  transfers between devices with their start and end apart: 5, of which 5 were waited for; matrix products, arithmetic and copies ran while one was open for 0% of the time, Pallas kernels for 0%

commit v1 on v0

v1 whole, which is shorter than its diff:
```python
import math

import jax
import jax.numpy as jnp
import numpy as np
from jax import lax
from jax.sharding import Mesh, PartitionSpec as P

CAP = 2
DP = ("x", "z", "c")
ALL = ("x", "z", "c", "tensor")


def residual_norm(hidden_rows, projected):
    residual = (hidden_rows.astype(jnp.float32) + projected.astype(jnp.float32)).astype(
        jnp.bfloat16
    )
    resid_f = residual.astype(jnp.float32)
    normed = (
        resid_f * lax.rsqrt(jnp.mean(resid_f * resid_f, axis=-1, keepdims=True) + 1e-06)
    ).astype(jnp.bfloat16)
    return (residual, normed)


def local(
    hidden_in,
    queries,
    key_cache,
    cached_value_rows,
    cache_lengths,
    out_weight,
    expert_ids,
    route_probs,
    w_gate,
    w_up,
    w_down,
):
    n_xz = lax.axis_size("x") * lax.axis_size("z")
    n_c = lax.axis_size("c")
    dp_count = n_xz * n_c
    tp_count = lax.axis_size("tensor")
    tp_rank = lax.axis_index("tensor")
    c_rank = lax.axis_index("c")
    rows_dev, kv_local, cache_len, head_dim = key_cache.shape
    groups = queries.shape[1] // (kv_local * head_dim)
    model_width = hidden_in.shape[1]
    col_block = model_width // dp_count
    n_all = dp_count * tp_count

    query_head_count = queries.reshape(rows_dev, kv_local, groups, head_dim)
    scores = jnp.einsum(
        "rhgd,rhld->rhgl", query_head_count, key_cache, preferred_element_type=jnp.float32
    ) * (1.0 / math.sqrt(head_dim))
    valid_mask = (jnp.arange(cache_len, dtype=jnp.int32)[None, :] < cache_lengths[:, None])[
        :, None, None, :
    ]
    scores = jnp.where(valid_mask, scores, -jnp.inf)
    largest = jnp.max(scores, axis=-1, keepdims=True)
    exponent = jnp.exp(scores - largest)
    attn_probs = (exponent / jnp.sum(exponent, axis=-1, keepdims=True)).astype(jnp.bfloat16)
    attn_out = jnp.einsum(
        "rhgl,rhld->rhgd", attn_probs, cached_value_rows, preferred_element_type=jnp.float32
    ).astype(jnp.bfloat16)
    attn_out = attn_out.reshape(rows_dev, kv_local * groups * head_dim)

    sent = jnp.broadcast_to(attn_out[None], (n_xz,) + attn_out.shape)
    mine = lax.all_to_all(sent, ("x", "z"), 0, 0, tiled=True)
    other = lax.ppermute(mine, "c", [(i, (i + 1) % n_c) for i in range(n_c)])
    part_mine = jnp.einsum("ird,dc->irc", mine, out_weight, preferred_element_type=jnp.float32)
    part_other = jnp.einsum("ird,dc->irc", other, out_weight, preferred_element_type=jnp.float32)
    slots = jnp.stack([part_mine, part_other], axis=1)
    slots = jnp.where(c_rank == 0, slots, slots[:, ::-1])
    partial_value = slots.reshape(dp_count, rows_dev, col_block).astype(jnp.bfloat16)

    sent = jnp.broadcast_to(partial_value[:, None], (dp_count, tp_count, rows_dev, col_block))
    got = lax.all_to_all(sent.reshape(n_all, rows_dev, col_block), ALL, 0, 0, tiled=True)
    projected = got.reshape(dp_count, tp_count, rows_dev, col_block).astype(jnp.float32).sum(1)
    projected = projected.transpose(1, 0, 2).reshape(rows_dev, model_width).astype(jnp.bfloat16)
    residual, normed = residual_norm(hidden_in, projected)

    exp_dev = w_gate.shape[0]
    n_exp = n_all * exp_dev
    matches = expert_ids[:, :, None] == jnp.arange(n_exp, dtype=jnp.int32)[None, None, :]
    assigned = jnp.sum(matches.astype(jnp.int32), axis=1)
    slot_rank = jnp.cumsum(assigned, axis=0) - assigned
    slot_hit = (slot_rank[:, :, None] == jnp.arange(CAP, dtype=jnp.int32)[None, None, :]) & (
        assigned[:, :, None] > 0
    )
    route_weights = route_probs / jnp.sum(route_probs, axis=-1, keepdims=True)
    all_weight = jnp.sum(jnp.where(matches, route_weights[:, :, None], 0.0), axis=1)

    hit_col = slot_hit.reshape(rows_dev, dp_count, tp_count, exp_dev, CAP)
    hit_col = lax.dynamic_index_in_dim(hit_col, tp_rank, axis=2, keepdims=False)
    outgoing = jnp.einsum(
        "rmjc,rd->mjcd", hit_col.astype(jnp.bfloat16), normed, preferred_element_type=jnp.float32
    ).astype(jnp.bfloat16)
    arrived_slots = lax.all_to_all(outgoing, DP, 0, 0, tiled=True)
    gate_proj = jnp.einsum(
        "sjcd,jdf->sjcf", arrived_slots, w_gate, preferred_element_type=jnp.float32
    )
    up_proj = jnp.einsum("sjcd,jdf->sjcf", arrived_slots, w_up, preferred_element_type=jnp.float32)
    activated = (jax.nn.silu(gate_proj) * up_proj).astype(jnp.bfloat16)
    expert_out = jnp.einsum(
        "sjcf,jfd->sjcd", activated, w_down, preferred_element_type=jnp.float32
    ).astype(jnp.bfloat16)

    width_share = model_width // tp_count
    back = expert_out.reshape(dp_count, exp_dev, CAP, tp_count, width_share)
    back = back.transpose(0, 3, 1, 2, 4).reshape(n_all, exp_dev * CAP, width_share)
    results = lax.all_to_all(back, ALL, 0, 0, tiled=True)
    combine_table = jnp.where(slot_hit, all_weight[:, :, None], 0.0)
    mixture = jnp.einsum(
        "rmc,mcd->rd",
        combine_table,
        results.reshape(n_exp, CAP, width_share).astype(jnp.float32),
        precision=lax.Precision.HIGHEST,
    )
    residual_own = lax.dynamic_slice_in_dim(residual, tp_rank * width_share, width_share, 1)
    return (residual_own.astype(jnp.float32) + mixture).astype(jnp.bfloat16)


def split_mesh(mesh):
    devices = np.asarray(mesh.devices)
    n_dp, n_t = devices.shape
    n_c = 2
    try:
        xs = sorted({d.coords[0] for d in devices.flat})
        n_x = len(xs)
    except Exception:
        n_x = 4
    n_z = n_dp // (n_x * n_c)
    return Mesh(devices.reshape(n_x, n_z, n_c, n_t), ALL)


def solution(mesh):
    fine = split_mesh(mesh)
    placed = (
        P(DP, None),
        P(DP, "tensor"),
        P(DP, "tensor", None, None),
        P(DP, "tensor", None, None),
        P(DP),
        P("tensor", DP),
        P(DP, None),
        P(DP, None),
        P(ALL, None, None),
        P(ALL, None, None),
        P(ALL, None, None),
    )
    return jax.shard_map(
        local, mesh=fine, in_specs=placed, out_specs=P(DP, "tensor"), check_vma=False
    )
```

time: 196 us -> 121 us (0.62)
  waiting for transfers between devices: 122 us -> 44.2 us
  blocking collectives: 15.1 us -> 29.8 us
  between operations: 13.3 us -> 0.22 us
  starting transfers between devices: 13.5 us -> 16.2 us
  local copies, waits for them, and re-layouts: 3.74 us -> 5.78 us
    all_gather x1 -> x0, waiting for transfers between devices: 48.5 us -> none  [local(): lax.all_gather(attn_out, 'dp', axis=0, tiled=True)]
    psum x1 -> x0, waiting for transfers between devices: 38.4 us -> none  [local(): summed = lax.psum(partial_value.astype(jnp.bfloat16), 'tensor')]
    all_to_all x2 -> x3, waiting for transfers between devices: 19.5 us -> 41.7 us  [the longest x1 16.3 us: local(): lax.all_to_all(sent.reshape(n_all, rows_dev, col_block), ALL, 0, 0, tiled...]
    reduce_scatter x1 -> x0, waiting for transfers between devices: 15 us -> none  [local(): lax.psum_scatter(mixture.astype(jnp.bfloat16), 'tensor', scatter_dimensio...]
    all_to_all x1, blocking collectives: 15.1 us -> 29.8 us  [local(): mine = lax.all_to_all(sent, ('x', 'z'), 0, 0, tiled=True)]
    ppermute x0 -> x1, waiting for transfers between devices: none -> 2.51 us  [local(): other = lax.ppermute(mine, 'c', [(i, (i + 1) % n_c) for i in range(n_c)])]
    ppermute x0 -> x1, starting transfers between devices: none -> 1.96 us  [local(): other = lax.ppermute(mine, 'c', [(i, (i + 1) % n_c) for i in range(n_c)])]
    dot_general x3 -> x4, matrix products: 5.17 us -> 3.94 us  [the longest x1 2 us: local(): jnp.einsum('ird,dc->irc', other, out_weight, preferred_element_type=jnp.f...]
  transfers between devices with their start and end apart: 5 -> 4, of which waited for: 5 -> 4; matrix products, arithmetic and copies ran while one was open for 0% -> 1% of each run, Pallas kernels for 0% -> 0%
where the time goes in v1:
time: 121 us; the launch traced here: 120 us
  waiting for transfers between devices  44.2 us (37%)
  blocking collectives  29.8 us (25%)
  matrix products  22.6 us (19%)
  starting transfers between devices  16.2 us (13%)
  local copies, waits for them, and re-layouts  5.78 us (5%)
  other arithmetic  1.44 us (1%)
    all_to_all x1, blocking collectives, local(): mine = lax.all_to_all(sent, ('x', 'z'), 0, 0, tiled=True)  29.8 us
    all_to_all x1, waiting for transfers between devices, local(): lax.all_to_all(sent.reshape(n_all, rows_dev, col_block), ALL, 0, 0, tiled...  16.3 us
    all_to_all x1, waiting for transfers between devices, local(): results = lax.all_to_all(back, ALL, 0, 0, tiled=True)  13.9 us
    all_to_all x1, waiting for transfers between devices, local(): arrived_slots = lax.all_to_all(outgoing, DP, 0, 0, tiled=True)  11.6 us
    dot_general x1, matrix products, local(): jnp.einsum('sjcf,jfd->sjcd', activated, w_down, preferred_element_type=jn...  7.55 us
    all_to_all x1, starting transfers between devices, local(): lax.all_to_all(sent.reshape(n_all, rows_dev, col_block), ALL, 0, 0, tiled...  6.33 us
    dot_general x1, matrix products, local(): jnp.einsum('sjcd,jdf->sjcf', arrived_slots, w_gate, preferred_element_typ...  4.18 us
    all_to_all x1, starting transfers between devices, local(): arrived_slots = lax.all_to_all(outgoing, DP, 0, 0, tiled=True)  3.97 us
  transfers between devices with their start and end apart: 4, of which 4 were waited for; matrix products, arithmetic and copies ran while one was open for 1% of the time, Pallas kernels for 0%

profile of v1, /device:TPU:1, one launch (start us, length us, event | category | flops | bytes accessed | tf_op | source)
XLA Modules:
  0.0 120.3 jit_solution(14470670761910713339)
XLA Ops:
  0.0 0.0 copy-start
  0.0 1.0 copy.51
  1.0 0.7 iota_compare_fusion.1
  1.7 3.8 %fusion.86 = (f32[24,16]{1,0:T(8,128)S(1)}, f32[24,16,768]{2,1,0:T(8,128)S(1)}) fusion(bf16[24,16,128]{2,1,0:T(8,128)(2,1)S(1)} %bitcast.141, bf16[24,1,768,128]{3,2,1,0:T(8,128)(2,1)} %param.13, pred[24,768]{1,0:T(8,128)(4,1)S(1)} %iota_compare_fusion.1), kind=kOutput, calls=%fused_computation.83 | convolution fusion | flops 76677888 | bytes 6016512 | tf_op jit(solution)/shard_map/sub | solution.py:59
  5.6 3.1 %fusion.38 = bf16[24,16,128]{2,1,0:T(8,128)(2,1)S(1)} fusion(bf16[24,1,768,128]{3,2,1,0:T(8,128)(2,1)} %param.14, f32[24,16,768]{2,1,0:T(8,128)S(1)} %get-tuple-element.8, f32[24,16]{1,0:T(8,128)S(1)} %get-tuple-element.7), kind=kOutput, calls=%fused_computation.26 | convolution fusion | flops 76136448 | bytes 5998080 | tf_op jit(solution)/shard_map/rhgl,rhld->rhgd/dot_general | solution.py:61
  8.7 0.2 broadcast_in_dim.66
  8.9 0.0 copy-start.3
  8.9 29.8 %all_to_all.20 = bf16[16,24,2048]{2,1,0:T(8,128)(2,1)S(1)} all-to-all(bf16[16,24,2048]{2,1,0:T(8,128)(2,1)S(1)} %broadcast_in_dim.66), channel_id=1, replica_groups=mesh['x'=4,'z'=4,'c'=2,'tensor'=4] {'x','z'}, dimensions={0} | all-to-all | bytes 3145728 | tf_op jit(solution)/shard_map/all_to_all | solution.py:67
  38.7 2.0 %collective-permute-start = (bf16[16,24,2048]{2,1,0:T(8,128)(2,1)S(1)}, bf16[16,24,2048]{2,1,0:T(8,128)(2,1)}, u32[]{:S(2)}, u32[]{:S(2)}) collective-permute-start(bf16[16,24,2048]{2,1,0:T(8,128)(2,1)S(1)} %all_to_all.20), channel_id=1, source_target_pairs={{0,4},{4,0},{1,5},{5,1},{2,6},{6,2},{3,7},{7,3},{8,12},{12,8},{9,1... | collective-permute-start | bytes 4718600 | tf_op jit(solution)/shard_map/ppermute | solution.py:68
  40.6 0.0 copy-done.3
  40.7 0.1 copy.39
  40.7 0.0 copy-done
  40.7 0.6 convolution_bitcast_fusion.1
  41.3 2.5 %collective-permute-done = bf16[16,24,2048]{2,1,0:T(8,128)(2,1)} collective-permute-done((bf16[16,24,2048]{2,1,0:T(8,128)(2,1)S(1)}, bf16[16,24,2048]{2,1,0:T(8,128)(2,1)}, u32[]{:S(2)}, u32[]{:S(2)}) %collective-permute-start) | collective-permute-done | bytes 1572896 | tf_op jit(solution)/shard_map/ppermute | solution.py:68
  43.8 2.0 %convolution_bitcast_fusion = bf16[16,1,24,128]{3,2,0,1:T(8,128)(2,1)S(1)} fusion(bf16[16,24,2048]{2,1,0:T(8,128)(2,1)} %collective-permute-done, bf16[2048,128]{1,0:T(8,128)(2,1)S(1)} %copy-done), kind=kOutput, calls=%fused_computation.22 | convolution fusion | flops 201326592 | bytes 2195456 | tf_op jit(solution)/shard_map/ird,dc->irc/dot_general | solution.py:70
  45.9 1.0 broadcast_in_dim.67
  46.9 0.0 copy-start.1
  46.9 6.3 %all-to-all-start.1 = ((bf16[128,24,128]{2,1,0:T(8,128)(2,1)}), bf16[128,24,128]{2,1,0:T(8,128)(2,1)S(1)}, u32[]{:S(2)}, u32[]{:S(2)}) async-start(bf16[128,24,128]{2,1,0:T(8,128)(2,1)} %bitcast.6), calls=%async_computation.1 | async-start | bytes 1572864 | tf_op jit(solution)/shard_map/all_to_all | solution.py:76
  53.3 0.1 convert_reduce_fusion
  53.4 0.1 copy.43
  53.5 0.1 copy.42
  53.6 0.1 copy.44
  53.7 0.1 copy.45
  53.9 16.3 %all-to-all-done.1 = bf16[128,24,128]{2,1,0:T(8,128)(2,1)S(1)} async-done(((bf16[128,24,128]{2,1,0:T(8,128)(2,1)}), bf16[128,24,128]{2,1,0:T(8,128)(2,1)S(1)}, u32[]{:S(2)}, u32[]{:S(2)}) %all-to-all-start.1) | async-done | bytes 786464 | tf_op jit(solution)/shard_map/all_to_all | solution.py:76
  70.2 0.1 bitcast_reduce_fusion
  70.3 0.0 copy-done.1
  70.3 0.0 copy-start.2
  70.3 0.2 fusion.58
  70.5 0.4 fusion.14
  70.9 1.3 %copy.46 = bf16[32,1,2,4096]{3,2,1,0:T(2,128)(2,1)} copy(bf16[32,1,2,4096]{3,0,2,1:T(8,128)(2,1)S(1)} %fusion.14) | data formatting | bytes 1048576 | tf_op jit(solution)/shard_map/convert_element_type | solution.py:96
  72.2 4.0 %all-to-all-start.2 = ((bf16[32,1,2,4096]{3,2,1,0:T(2,128)(2,1)}), bf16[32,1,2,4096]{3,2,1,0:T(2,128)(2,1)S(1)}, u32[]{:S(2)}, u32[]{:S(2)}) async-start(bf16[32,1,2,4096]{3,2,1,0:T(2,128)(2,1)} %copy.46), calls=%async_computation.2 | async-start | bytes 1048576 | tf_op jit(solution)/shard_map/all_to_all | solution.py:97
  76.2 0.0 copy-done.2
  76.2 11.6 %all-to-all-done.2 = bf16[32,1,2,4096]{3,2,1,0:T(2,128)(2,1)S(1)} async-done(((bf16[32,1,2,4096]{3,2,1,0:T(2,128)(2,1)}), bf16[32,1,2,4096]{3,2,1,0:T(2,128)(2,1)S(1)}, u32[]{:S(2)}, u32[]{:S(2)}) %all-to-all-start.2) | async-done | bytes 524320 | tf_op jit(solution)/shard_map/all_to_all | solution.py:97
  87.8 4.2 %fusion.26 = f32[32,1,2,768]{3,0,2,1:T(8,128)S(1)} fusion(bf16[1,4096,768]{2,1,0:T(8,128)(2,1)} %param.19, bf16[32,1,2,4096]{3,2,1,0:T(2,128)(2,1)S(1)} %all-to-all-done.2), kind=kOutput, calls=%fused_computation.20 | convolution fusion | flops 402653184 | bytes 7012352 | tf_op jit(solution)/shard_map/sjcd,jdf->sjcf/dot_general | solution.py:98
  92.0 7.5 %fusion.15 = bf16[32,1,2,4096]{3,0,2,1:T(8,128)(2,1)S(1)} fusion(bf16[1,768,4096]{2,1,0:T(8,128)(2,1)} %param.21, bf16[1,4096,768]{2,1,0:T(8,128)(2,1)} %param.20, bf16[32,1,2,4096]{3,2,1,0:T(2,128)(2,1)S(1)} %all-to-all-done.2, f32[32,1,2,768]{3,0,2,1:T(8,128)S(1)} %fusion.26), kind=kOutput, calls=%fused_computation.14 | convolution fusion | flops 805863424 | bytes 13828096 | tf_op jit(solution)/shard_map/sjcf,jfd->sjcd/dot_general | solution.py:103
  99.5 0.4 reshape.152
  99.9 1.3 %copy.48 = bf16[32,4,1,2,1024]{4,3,1,0,2:T(2,128)(2,1)} copy(bf16[32,4,1,2,1024]{4,1,0,3,2:T(4,128)(2,1)S(1)} %bitcast.136) | data formatting | bytes 1048576 | tf_op jit(solution)/shard_map/transpose | solution.py:109
  101.2 3.9 %all-to-all-start.3 = ((bf16[128,2,1024]{2,1,0:T(2,128)(2,1)}), bf16[128,2,1024]{2,1,0:T(2,128)(2,1)S(1)}, u32[]{:S(2)}, u32[]{:S(2)}) async-start(bf16[128,2,1024]{2,1,0:T(2,128)(2,1)} %bitcast.37), calls=%async_computation.3 | async-start | bytes 1048576 | tf_op jit(solution)/shard_map/all_to_all | solution.py:110
  105.2 0.1 copy.41
  105.3 0.1 select_reduce_fusion
  105.4 13.9 %all-to-all-done.3 = bf16[128,2,1024]{2,1,0:T(2,128)(2,1)S(1)} async-done(((bf16[128,2,1024]{2,1,0:T(2,128)(2,1)}), bf16[128,2,1024]{2,1,0:T(2,128)(2,1)S(1)}, u32[]{:S(2)}, u32[]{:S(2)}) %all-to-all-start.3) | async-done | bytes 524320 | tf_op jit(solution)/shard_map/all_to_all | solution.py:110
  119.3 1.0 fusion.45
  (14 shorter events, 0.3 us)
Async XLA Ops:
  0.0 40.7 %copy-start = (bf16[2048,128]{1,0:T(8,128)(2,1)S(1)}, bf16[2048,128]{1,0:T(8,128)(2,1)}, u32[]{:S(2)}) copy-start(bf16[2048,128]{1,0:T(8,128)(2,1)} %param.16) | copy-start | bytes 1572868
  8.9 31.7 %copy-start.3 = (s32[24,8]{0,1:T(8,128)S(1)}, s32[24,8]{0,1:T(8,128)}, u32[]{:S(2)}) copy-start(s32[24,8]{0,1:T(8,128)} %param.17) | copy-start | bytes 2308
  38.7 5.1 %collective-permute-start = (bf16[16,24,2048]{2,1,0:T(8,128)(2,1)S(1)}, bf16[16,24,2048]{2,1,0:T(8,128)(2,1)}, u32[]{:S(2)}, u32[]{:S(2)}) collective-permute-start(bf16[16,24,2048]{2,1,0:T(8,128)(2,1)S(1)} %all_to_all.20), channel_id=1, source_target_pairs={{0,4},{4,0},{1,5},{5,1},{2,6},{6,2},{3,7},{7,3},{8,12},{12,8},{9,1... | collective-permute-start | bytes 4718600 | tf_op jit(solution)/shard_map/ppermute | solution.py:68
  46.9 23.4 %copy-start.1 = (bf16[24,4096]{1,0:T(8,128)(2,1)S(1)}, bf16[24,4096]{1,0:T(8,128)(2,1)}, u32[]{:S(2)}) copy-start(bf16[24,4096]{1,0:T(8,128)(2,1)} %param.11) | copy-start | bytes 589828
  46.9 23.3 %all-to-all-start.1 = ((bf16[128,24,128]{2,1,0:T(8,128)(2,1)}), bf16[128,24,128]{2,1,0:T(8,128)(2,1)S(1)}, u32[]{:S(2)}, u32[]{:S(2)}) async-start(bf16[128,24,128]{2,1,0:T(8,128)(2,1)} %bitcast.6), calls=%async_computation.1 | async-start | bytes 1572864 | tf_op jit(solution)/shard_map/all_to_all | solution.py:76
  70.3 5.9 %copy-start.2 = (f32[24,8]{0,1:T(8,128)S(1)}, f32[24,8]{0,1:T(8,128)}, u32[]{:S(2)}) copy-start(f32[24,8]{0,1:T(8,128)} %param.18) | copy-start | bytes 2308
  72.2 15.6 %all-to-all-start.2 = ((bf16[32,1,2,4096]{3,2,1,0:T(2,128)(2,1)}), bf16[32,1,2,4096]{3,2,1,0:T(2,128)(2,1)S(1)}, u32[]{:S(2)}, u32[]{:S(2)}) async-start(bf16[32,1,2,4096]{3,2,1,0:T(2,128)(2,1)} %copy.46), calls=%async_computation.2 | async-start | bytes 1048576 | tf_op jit(solution)/shard_map/all_to_all | solution.py:97
  101.2 18.0 %all-to-all-start.3 = ((bf16[128,2,1024]{2,1,0:T(2,128)(2,1)}), bf16[128,2,1024]{2,1,0:T(2,128)(2,1)S(1)}, u32[]{:S(2)}, u32[]{:S(2)}) async-start(bf16[128,2,1024]{2,1,0:T(2,128)(2,1)} %bitcast.37), calls=%async_computation.3 | async-start | bytes 1048576 | tf_op jit(solution)/shard_map/all_to_all | solution.py:110

commit v2 on v1

--- a/solution.py
+++ b/solution.py
@@ -4,6 +4,8 @@
 import jax.numpy as jnp
 import numpy as np
 from jax import lax
+from jax.experimental import pallas as pl
+from jax.experimental.pallas import tpu as pltpu
 from jax.sharding import Mesh, PartitionSpec as P
 
 CAP = 2
@@ -20,6 +22,34 @@
         resid_f * lax.rsqrt(jnp.mean(resid_f * resid_f, axis=-1, keepdims=True) + 1e-06)
     ).astype(jnp.bfloat16)
     return (residual, normed)
+
+
+def ffn_kernel(x_ref, wg_ref, wu_ref, wd_ref, o_ref):
+    x = x_ref[...]
+    gate = jnp.dot(x, wg_ref[...], preferred_element_type=jnp.float32)
+    up = jnp.dot(x, wu_ref[...], preferred_element_type=jnp.float32)
+    activated = (gate / (1.0 + jnp.exp(-gate)) * up).astype(jnp.bfloat16)
+    o_ref[...] = jnp.dot(activated, wd_ref[...], preferred_element_type=jnp.float32).astype(
+        o_ref.dtype
+    )
+
+
+def expert_ffn(x, wg, wu, wd):
+    rows, width = x.shape
+    ff = wg.shape[1]
+    vmem = pl.BlockSpec(memory_space=pltpu.VMEM)
+    return pl.pallas_call(
+        ffn_kernel,
+        out_shape=jax.ShapeDtypeStruct((rows, width), jnp.bfloat16),
+        in_specs=[vmem] * 4,
+        out_specs=vmem,
+        compiler_params=pltpu.CompilerParams(vmem_limit_bytes=56 * 1024 * 1024),
+        cost_estimate=pl.CostEstimate(
+            flops=6 * rows * width * ff,
+            transcendentals=rows * ff,
+            bytes_accessed=2 * (3 * width * ff + 2 * rows * width),
+        ),
+    )(x, wg, wu, wd)
 
 
 def local(
@@ -95,14 +125,15 @@
         "rmjc,rd->mjcd", hit_col.astype(jnp.bfloat16), normed, preferred_element_type=jnp.float32
     ).astype(jnp.bfloat16)
     arrived_slots = lax.all_to_all(outgoing, DP, 0, 0, tiled=True)
-    gate_proj = jnp.einsum(
-        "sjcd,jdf->sjcf", arrived_slots, w_gate, preferred_element_type=jnp.float32
+    expert_out = jnp.stack(
+        [
+            expert_ffn(
+                arrived_slots[:, j].reshape(dp_count * CAP, model_width), w_gate[j], w_up[j], w_down[j]
+            ).reshape(dp_count, CAP, model_width)
+            for j in range(exp_dev)
+        ],
+        axis=1,
     )
-    up_proj = jnp.einsum("sjcd,jdf->sjcf", arrived_slots, w_up, preferred_element_type=jnp.float32)
-    activated = (jax.nn.silu(gate_proj) * up_proj).astype(jnp.bfloat16)
-    expert_out = jnp.einsum(
-        "sjcf,jfd->sjcd", activated, w_down, preferred_element_type=jnp.float32
-    ).astype(jnp.bfloat16)
 
     width_share = model_width // tp_count
     back = expert_out.reshape(dp_count, exp_dev, CAP, tp_count, width_share)

time: 121 us -> 122 us (level)
  matrix products: 22.6 us -> 10.9 us
  Pallas kernels: 0 us -> 10.8 us
  local copies, waits for them, and re-layouts: 5.78 us -> 7.81 us
    dot_general x2 -> x0, matrix products: 11.7 us -> none  [the longest x1 7.55 us: local(): jnp.einsum('sjcf,jfd->sjcd', activated, w_down, preferred_element_type=jn...]
    pallas_call x0 -> x1, Pallas kernels: none -> 10.8 us  [expert_ffn(): pl.pallas_call(ffn_kernel, out_shape=jax.ShapeDtypeStruct((rows, width),...]
    another operation x0 -> x2, local copies, waits for them, and re-layouts: none -> 2.42 us  [the longest x1 1.43 us: local(): back = expert_out.reshape(dp_count, exp_dev, CAP, tp_count, width_share)]
where the time goes in v2:
time: 122 us; the launch traced here: 121 us
  waiting for transfers between devices  44.2 us (36%)
  blocking collectives  29.8 us (24%)
  starting transfers between devices  16.2 us (13%)
  matrix products  10.9 us (9%)
  Pallas kernels  10.8 us (9%)
  local copies, waits for them, and re-layouts  7.81 us (6%)
  other arithmetic  1.44 us (1%)
    all_to_all x1, blocking collectives, local(): mine = lax.all_to_all(sent, ('x', 'z'), 0, 0, tiled=True)  29.8 us
    all_to_all x1, waiting for transfers between devices, local(): lax.all_to_all(sent.reshape(n_all, rows_dev, col_block), ALL, 0, 0, tiled...  16.3 us
    all_to_all x1, waiting for transfers between devices, local(): results = lax.all_to_all(back, ALL, 0, 0, tiled=True)  13.9 us
    all_to_all x1, waiting for transfers between devices, local(): arrived_slots = lax.all_to_all(outgoing, DP, 0, 0, tiled=True)  11.6 us
    pallas_call x1, Pallas kernels, expert_ffn(): pl.pallas_call(ffn_kernel, out_shape=jax.ShapeDtypeStruct((rows, width),...  10.8 us
    all_to_all x1, starting transfers between devices, local(): lax.all_to_all(sent.reshape(n_all, rows_dev, col_block), ALL, 0, 0, tiled...  6.33 us
    all_to_all x1, starting transfers between devices, local(): arrived_slots = lax.all_to_all(outgoing, DP, 0, 0, tiled=True)  3.97 us
    all_to_all x1, starting transfers between devices, local(): results = lax.all_to_all(back, ALL, 0, 0, tiled=True)  3.93 us
  transfers between devices with their start and end apart: 4, of which 4 were waited for; matrix products, arithmetic and copies ran while one was open for 1% of the time, Pallas kernels for 0%

profile of v2, /device:TPU:1, one launch (start us, length us, event | category | flops | bytes accessed | tf_op | source)
XLA Modules:
  0.0 121.3 jit_solution(2161826616892927878)
XLA Ops:
  0.0 0.0 copy-start
  0.0 1.0 copy.53
  1.0 0.7 iota_compare_fusion.1
  1.7 3.8 %fusion.44 = (f32[24,16]{1,0:T(8,128)S(1)}, f32[24,16,768]{2,1,0:T(8,128)S(1)}) fusion(bf16[24,16,128]{2,1,0:T(8,128)(2,1)S(1)} %bitcast.79, bf16[24,1,768,128]{3,2,1,0:T(8,128)(2,1)} %param.13, pred[24,768]{1,0:T(8,128)(4,1)S(1)} %iota_compare_fusion.1), kind=kOutput, calls=%fused_computation.59 | convolution fusion | flops 76677888 | bytes 6016512 | tf_op jit(solution)/shard_map/sub | solution.py:89
  5.6 3.1 %fusion.14 = bf16[24,16,128]{2,1,0:T(8,128)(2,1)S(1)} fusion(bf16[24,1,768,128]{3,2,1,0:T(8,128)(2,1)} %param.14, f32[24,16,768]{2,1,0:T(8,128)S(1)} %get-tuple-element.8, f32[24,16]{1,0:T(8,128)S(1)} %get-tuple-element.7), kind=kOutput, calls=%fused_computation.14 | convolution fusion | flops 76136448 | bytes 5998080 | tf_op jit(solution)/shard_map/rhgl,rhld->rhgd/dot_general | solution.py:91
  8.7 0.2 broadcast_in_dim.66
  8.9 0.0 copy-start.3
  8.9 29.8 %all_to_all.20 = bf16[16,24,2048]{2,1,0:T(8,128)(2,1)S(1)} all-to-all(bf16[16,24,2048]{2,1,0:T(8,128)(2,1)S(1)} %broadcast_in_dim.66), channel_id=1, replica_groups=mesh['x'=4,'z'=4,'c'=2,'tensor'=4] {'x','z'}, dimensions={0} | all-to-all | bytes 3145728 | tf_op jit(solution)/shard_map/all_to_all | solution.py:97
  38.7 2.0 %collective-permute-start = (bf16[16,24,2048]{2,1,0:T(8,128)(2,1)S(1)}, bf16[16,24,2048]{2,1,0:T(8,128)(2,1)}, u32[]{:S(2)}, u32[]{:S(2)}) collective-permute-start(bf16[16,24,2048]{2,1,0:T(8,128)(2,1)S(1)} %all_to_all.20), channel_id=1, source_target_pairs={{0,4},{4,0},{1,5},{5,1},{2,6},{6,2},{3,7},{7,3},{8,12},{12,8},{9,1... | collective-permute-start | bytes 4718600 | tf_op jit(solution)/shard_map/ppermute | solution.py:98
  40.6 0.0 copy-done.3
  40.7 0.1 copy.42
  40.7 0.0 copy-done
  40.7 0.6 convolution_bitcast_fusion.1
  41.3 2.5 %collective-permute-done = bf16[16,24,2048]{2,1,0:T(8,128)(2,1)} collective-permute-done((bf16[16,24,2048]{2,1,0:T(8,128)(2,1)S(1)}, bf16[16,24,2048]{2,1,0:T(8,128)(2,1)}, u32[]{:S(2)}, u32[]{:S(2)}) %collective-permute-start) | collective-permute-done | bytes 1572896 | tf_op jit(solution)/shard_map/ppermute | solution.py:98
  43.8 2.0 %convolution_bitcast_fusion = bf16[16,1,24,128]{3,2,0,1:T(8,128)(2,1)S(1)} fusion(bf16[16,24,2048]{2,1,0:T(8,128)(2,1)} %collective-permute-done, bf16[2048,128]{1,0:T(8,128)(2,1)S(1)} %copy-done), kind=kOutput, calls=%fused_computation.12 | convolution fusion | flops 201326592 | bytes 2195456 | tf_op jit(solution)/shard_map/ird,dc->irc/dot_general | solution.py:100
  45.9 1.0 broadcast_in_dim.67
  46.9 0.0 copy-start.1
  46.9 6.3 %all-to-all-start.1 = ((bf16[128,24,128]{2,1,0:T(8,128)(2,1)}), bf16[128,24,128]{2,1,0:T(8,128)(2,1)S(1)}, u32[]{:S(2)}, u32[]{:S(2)}) async-start(bf16[128,24,128]{2,1,0:T(8,128)(2,1)} %bitcast.6), calls=%async_computation.1 | async-start | bytes 1572864 | tf_op jit(solution)/shard_map/all_to_all | solution.py:106
  53.3 0.1 convert_reduce_fusion
  53.4 0.1 copy.46
  53.5 0.1 copy.45
  53.6 0.1 copy.47
  53.7 0.1 copy.48
  53.9 16.3 %all-to-all-done.1 = bf16[128,24,128]{2,1,0:T(8,128)(2,1)S(1)} async-done(((bf16[128,24,128]{2,1,0:T(8,128)(2,1)}), bf16[128,24,128]{2,1,0:T(8,128)(2,1)S(1)}, u32[]{:S(2)}, u32[]{:S(2)}) %all-to-all-start.1) | async-done | bytes 786464 | tf_op jit(solution)/shard_map/all_to_all | solution.py:106
  70.2 0.1 bitcast_reduce_fusion
  70.3 0.0 copy-done.1
  70.3 0.0 copy-start.2
  70.3 0.2 fusion.23
  70.5 0.4 fusion.5
  70.9 1.3 %copy.49 = bf16[32,1,2,4096]{3,2,1,0:T(2,128)(2,1)} copy(bf16[32,1,2,4096]{3,0,2,1:T(8,128)(2,1)S(1)} %fusion.5) | data formatting | bytes 1048576 | tf_op jit(solution)/shard_map/convert_element_type | solution.py:126
  72.2 4.0 %all-to-all-start.2 = ((bf16[32,1,2,4096]{3,2,1,0:T(2,128)(2,1)}), bf16[32,1,2,4096]{3,2,1,0:T(2,128)(2,1)S(1)}, u32[]{:S(2)}, u32[]{:S(2)}) async-start(bf16[32,1,2,4096]{3,2,1,0:T(2,128)(2,1)} %copy.49), calls=%async_computation.2 | async-start | bytes 1048576 | tf_op jit(solution)/shard_map/all_to_all | solution.py:127
  76.2 0.0 copy-done.2
  76.2 11.6 %all-to-all-done.2 = bf16[32,1,2,4096]{3,2,1,0:T(2,128)(2,1)S(1)} async-done(((bf16[32,1,2,4096]{3,2,1,0:T(2,128)(2,1)}), bf16[32,1,2,4096]{3,2,1,0:T(2,128)(2,1)S(1)}, u32[]{:S(2)}, u32[]{:S(2)}) %all-to-all-start.2) | async-done | bytes 524320 | tf_op jit(solution)/shard_map/all_to_all | solution.py:127
  87.8 1.0 reshape_squeeze.3.x_ref
  88.8 10.8 %shard_map.109 = bf16[64,4096]{1,0:T(8,128)(2,1)} custom-call(bf16[64,4096]{1,0:T(8,128)(2,1)} %reshape_squeeze.3.x_ref, bf16[4096,768]{1,0:T(8,128)(2,1)} %bitcast.71, bf16[4096,768]{1,0:T(8,128)(2,1)} %bitcast.72, bf16[768,4096]{1,0:T(8,128)(2,1)} %bitcast.73), custom_call_target="tpu_custom_call" | custom-call | flops 1207959552 | bytes 19922944 | tf_op jit(solution)/shard_map/pallas_call | solution.py:41
  99.6 1.4 %reshape_stack_reshape.3 = bf16[32,1,2,4,1024]{4,3,2,0,1:T(4,128)(2,1)S(1)} reshape(bf16[64,4096]{1,0:T(8,128)(2,1)} %shard_map.109) | data formatting | bytes 1048576 | tf_op jit(solution)/shard_map/reshape;stack;reshape | solution.py:139
  101.0 1.3 %copy.50 = bf16[32,4,1,2,1024]{4,3,1,0,2:T(2,128)(2,1)} copy(bf16[32,4,1,2,1024]{4,1,3,0,2:T(4,128)(2,1)S(1)} %bitcast.74) | data formatting | bytes 1048576 | tf_op jit(solution)/shard_map/transpose | solution.py:140
  102.3 3.9 %all-to-all-start.3 = ((bf16[128,2,1024]{2,1,0:T(2,128)(2,1)}), bf16[128,2,1024]{2,1,0:T(2,128)(2,1)S(1)}, u32[]{:S(2)}, u32[]{:S(2)}) async-start(bf16[128,2,1024]{2,1,0:T(2,128)(2,1)} %bitcast.21), calls=%async_computation.3 | async-start | bytes 1048576 | tf_op jit(solution)/shard_map/all_to_all | solution.py:141
  106.3 0.1 copy.44
  106.3 0.1 select_reduce_fusion
  106.5 13.9 %all-to-all-done.3 = bf16[128,2,1024]{2,1,0:T(2,128)(2,1)S(1)} async-done(((bf16[128,2,1024]{2,1,0:T(2,128)(2,1)}), bf16[128,2,1024]{2,1,0:T(2,128)(2,1)S(1)}, u32[]{:S(2)}, u32[]{:S(2)}) %all-to-all-start.3) | async-done | bytes 524320 | tf_op jit(solution)/shard_map/all_to_all | solution.py:141
  120.4 1.0 fusion.18
  (14 shorter events, 0.3 us)
Async XLA Ops:
  0.0 40.7 %copy-start = (bf16[2048,128]{1,0:T(8,128)(2,1)S(1)}, bf16[2048,128]{1,0:T(8,128)(2,1)}, u32[]{:S(2)}) copy-start(bf16[2048,128]{1,0:T(8,128)(2,1)} %param.16) | copy-start | bytes 1572868
  8.9 31.7 %copy-start.3 = (s32[24,8]{0,1:T(8,128)S(1)}, s32[24,8]{0,1:T(8,128)}, u32[]{:S(2)}) copy-start(s32[24,8]{0,1:T(8,128)} %param.17) | copy-start | bytes 2308
  38.7 5.1 %collective-permute-start = (bf16[16,24,2048]{2,1,0:T(8,128)(2,1)S(1)}, bf16[16,24,2048]{2,1,0:T(8,128)(2,1)}, u32[]{:S(2)}, u32[]{:S(2)}) collective-permute-start(bf16[16,24,2048]{2,1,0:T(8,128)(2,1)S(1)} %all_to_all.20), channel_id=1, source_target_pairs={{0,4},{4,0},{1,5},{5,1},{2,6},{6,2},{3,7},{7,3},{8,12},{12,8},{9,1... | collective-permute-start | bytes 4718600 | tf_op jit(solution)/shard_map/ppermute | solution.py:98
  46.9 23.4 %copy-start.1 = (bf16[24,4096]{1,0:T(8,128)(2,1)S(1)}, bf16[24,4096]{1,0:T(8,128)(2,1)}, u32[]{:S(2)}) copy-start(bf16[24,4096]{1,0:T(8,128)(2,1)} %param.11) | copy-start | bytes 589828
  46.9 23.3 %all-to-all-start.1 = ((bf16[128,24,128]{2,1,0:T(8,128)(2,1)}), bf16[128,24,128]{2,1,0:T(8,128)(2,1)S(1)}, u32[]{:S(2)}, u32[]{:S(2)}) async-start(bf16[128,24,128]{2,1,0:T(8,128)(2,1)} %bitcast.6), calls=%async_computation.1 | async-start | bytes 1572864 | tf_op jit(solution)/shard_map/all_to_all | solution.py:106
  70.3 5.9 %copy-start.2 = (f32[24,8]{0,1:T(8,128)S(1)}, f32[24,8]{0,1:T(8,128)}, u32[]{:S(2)}) copy-start(f32[24,8]{0,1:T(8,128)} %param.18) | copy-start | bytes 2308
  72.2 15.6 %all-to-all-start.2 = ((bf16[32,1,2,4096]{3,2,1,0:T(2,128)(2,1)}), bf16[32,1,2,4096]{3,2,1,0:T(2,128)(2,1)S(1)}, u32[]{:S(2)}, u32[]{:S(2)}) async-start(bf16[32,1,2,4096]{3,2,1,0:T(2,128)(2,1)} %copy.49), calls=%async_computation.2 | async-start | bytes 1048576 | tf_op jit(solution)/shard_map/all_to_all | solution.py:127
  102.3 18.0 %all-to-all-start.3 = ((bf16[128,2,1024]{2,1,0:T(2,128)(2,1)}), bf16[128,2,1024]{2,1,0:T(2,128)(2,1)S(1)}, u32[]{:S(2)}, u32[]{:S(2)}) async-start(bf16[128,2,1024]{2,1,0:T(2,128)(2,1)} %bitcast.21), calls=%async_computation.3 | async-start | bytes 1048576 | tf_op jit(solution)/shard_map/all_to_all | solution.py:141

commit v3 on v1

--- a/solution.py
+++ b/solution.py
@@ -48,28 +48,35 @@
     n_all = dp_count * tp_count
 
     query_head_count = queries.reshape(rows_dev, kv_local, groups, head_dim)
-    scores = jnp.einsum(
-        "rhgd,rhld->rhgl", query_head_count, key_cache, preferred_element_type=jnp.float32
-    ) * (1.0 / math.sqrt(head_dim))
     valid_mask = (jnp.arange(cache_len, dtype=jnp.int32)[None, :] < cache_lengths[:, None])[
         :, None, None, :
     ]
-    scores = jnp.where(valid_mask, scores, -jnp.inf)
-    largest = jnp.max(scores, axis=-1, keepdims=True)
-    exponent = jnp.exp(scores - largest)
-    attn_probs = (exponent / jnp.sum(exponent, axis=-1, keepdims=True)).astype(jnp.bfloat16)
-    attn_out = jnp.einsum(
-        "rhgl,rhld->rhgd", attn_probs, cached_value_rows, preferred_element_type=jnp.float32
-    ).astype(jnp.bfloat16)
-    attn_out = attn_out.reshape(rows_dev, kv_local * groups * head_dim)
-
-    sent = jnp.broadcast_to(attn_out[None], (n_xz,) + attn_out.shape)
-    mine = lax.all_to_all(sent, ("x", "z"), 0, 0, tiled=True)
-    other = lax.ppermute(mine, "c", [(i, (i + 1) % n_c) for i in range(n_c)])
-    part_mine = jnp.einsum("ird,dc->irc", mine, out_weight, preferred_element_type=jnp.float32)
-    part_other = jnp.einsum("ird,dc->irc", other, out_weight, preferred_element_type=jnp.float32)
-    slots = jnp.stack([part_mine, part_other], axis=1)
-    slots = jnp.where(c_rank == 0, slots, slots[:, ::-1])
+    n_chunks = 2
+    per_chunk = groups // n_chunks
+    weight_rows = out_weight.reshape(kv_local, groups, head_dim, col_block)
+    partial_f = None
+    for k in range(n_chunks):
+        q_k = query_head_count[:, :, k * per_chunk : (k + 1) * per_chunk]
+        scores = jnp.einsum(
+            "rhgd,rhld->rhgl", q_k, key_cache, preferred_element_type=jnp.float32
+        ) * (1.0 / math.sqrt(head_dim))
+        scores = jnp.where(valid_mask, scores, -jnp.inf)
+        largest = jnp.max(scores, axis=-1, keepdims=True)
+        exponent = jnp.exp(scores - largest)
+        attn_probs = (exponent / jnp.sum(exponent, axis=-1, keepdims=True)).astype(jnp.bfloat16)
+        attn_out = jnp.einsum(
+            "rhgl,rhld->rhgd", attn_probs, cached_value_rows, preferred_element_type=jnp.float32
+        ).astype(jnp.bfloat16)
+        attn_out = attn_out.reshape(rows_dev, kv_local * per_chunk * head_dim)
+        w_k = weight_rows[:, k * per_chunk : (k + 1) * per_chunk].reshape(-1, col_block)
+        sent = jnp.broadcast_to(attn_out[None], (n_xz,) + attn_out.shape)
+        mine = lax.all_to_all(sent, ("x", "z"), 0, 0, tiled=True)
+        other = lax.ppermute(mine, "c", [(i, (i + 1) % n_c) for i in range(n_c)])
+        part_mine = jnp.einsum("ird,dc->irc", mine, w_k, preferred_element_type=jnp.float32)
+        part_other = jnp.einsum("ird,dc->irc", other, w_k, preferred_element_type=jnp.float32)
+        part = jnp.stack([part_mine, part_other], axis=1)
+        partial_f = part if partial_f is None else partial_f + part
+    slots = jnp.where(c_rank == 0, partial_f, partial_f[:, ::-1])
     partial_value = slots.reshape(dp_count, rows_dev, col_block).astype(jnp.bfloat16)
 
     sent = jnp.broadcast_to(partial_value[:, None], (dp_count, tp_count, rows_dev, col_block))

time: 121 us -> 128 us (1.058)
  blocking collectives: 29.8 us -> 0 us
  starting transfers between devices: 16.2 us -> 31.7 us
  waiting for transfers between devices: 44.2 us -> 57.2 us
  matrix products: 22.6 us -> 28.5 us
  local copies, waits for them, and re-layouts: 5.78 us -> 8.56 us
    all_to_all x1 -> x0, blocking collectives: 29.8 us -> none  [local(): mine = lax.all_to_all(sent, ('x', 'z'), 0, 0, tiled=True)]
    all_to_all x0 -> x2, waiting for transfers between devices: none -> 15.4 us  [local(): mine = lax.all_to_all(sent, ('x', 'z'), 0, 0, tiled=True)]
    all_to_all x0 -> x2, starting transfers between devices: none -> 12.3 us  [local(): mine = lax.all_to_all(sent, ('x', 'z'), 0, 0, tiled=True)]
    sub x1 -> x2, matrix products: 3.84 us -> 7.67 us  [local(): exponent = jnp.exp(scores - largest)]
    ppermute x1 -> x2, starting transfers between devices: 1.96 us -> 5.63 us  [local(): other = lax.ppermute(mine, 'c', [(i, (i + 1) % n_c) for i in range(n_c)])]
    dot_general x1 -> x2, matrix products: 3.13 us -> 6.24 us  [local(): jnp.einsum('rhgl,rhld->rhgd', attn_probs, cached_value_rows, preferred_el...]
    ppermute x1 -> x2, waiting for transfers between devices: 2.51 us -> 0.01 us  [local(): other = lax.ppermute(mine, 'c', [(i, (i + 1) % n_c) for i in range(n_c)])]
    broadcast_in_dim x1 -> x2, local copies, waits for them, and re-layouts: 0.17 us -> 1.94 us  [local(): sent = jnp.broadcast_to(attn_out[None], (n_xz,) + attn_out.shape)]
  transfers between devices with their start and end apart: 4 -> 7, of which waited for: 4 -> 5; matrix products, arithmetic and copies ran while one was open for 1% -> 8% of each run, Pallas kernels for 0% -> 0%
where the time goes in v3:
time: 128 us
  waiting for transfers between devices  57.2 us (45%)
  starting transfers between devices  31.7 us (25%)
  matrix products  28.5 us (22%)
  local copies, waits for them, and re-layouts  8.56 us (7%)
  other arithmetic  1.46 us (1%)
    all_to_all x1, waiting for transfers between devices, local(): lax.all_to_all(sent.reshape(n_all, rows_dev, col_block), ALL, 0, 0, tiled...  16.3 us
    all_to_all x2, waiting for transfers between devices, local(): mine = lax.all_to_all(sent, ('x', 'z'), 0, 0, tiled=True)  15.4 us
    all_to_all x1, waiting for transfers between devices, local(): results = lax.all_to_all(back, ALL, 0, 0, tiled=True)  13.9 us
    all_to_all x2, starting transfers between devices, local(): mine = lax.all_to_all(sent, ('x', 'z'), 0, 0, tiled=True)  12.3 us
    all_to_all x1, waiting for transfers between devices, local(): arrived_slots = lax.all_to_all(outgoing, DP, 0, 0, tiled=True)  11.6 us
    sub x2, matrix products, local(): exponent = jnp.exp(scores - largest)  7.67 us
    dot_general x1, matrix products, local(): jnp.einsum('sjcf,jfd->sjcd', activated, w_down, preferred_element_type=jn...  7.55 us
    dot_general x2, matrix products, local(): jnp.einsum('rhgl,rhld->rhgd', attn_probs, cached_value_rows, preferred_el...  6.24 us
  transfers between devices with their start and end apart: 7, of which 5 were waited for; matrix products, arithmetic and copies ran while one was open for 8% of the time, Pallas kernels for 0%

profile of v3, /device:TPU:1, one launch (start us, length us, event | category | flops | bytes accessed | tf_op | source)
XLA Modules:
  0.0 127.6 jit_solution(7017973563662323635)
XLA Ops:
  0.0 0.7 iota_compare_fusion.1
  0.7 0.9 copy.51
  1.7 3.8 %fusion.102 = (f32[24,8]{1,0:T(8,128)S(1)}, f32[24,8,768]{2,1,0:T(8,128)S(1)}) fusion(bf16[24,1,768,128]{3,2,1,0:T(8,128)(2,1)} %param.13, pred[24,768]{1,0:T(8,128)(4,1)S(1)} %iota_compare_fusion.1, bf16[24,1,16,128]{3,2,0,1:T(8,128)(2,1)S(1)} %bitcast.184), kind=kOutput, calls=%fused_computation.99 | convolution fusion | flops 38339328 | bytes 5376768 | tf_op jit(solution)/shard_map/sub | solution.py:65
  5.5 3.1 %fusion.56 = bf16[24,8,128]{2,1,0:T(8,128)(2,1)S(1)} fusion(bf16[24,1,768,128]{3,2,1,0:T(8,128)(2,1)} %param.14, f32[24,8,768]{2,1,0:T(8,128)S(1)} %get-tuple-element.10, f32[24,8]{1,0:T(8,128)S(1)} %get-tuple-element.9), kind=kOutput, calls=%fused_computation.40 | convolution fusion | flops 38068224 | bytes 5358336 | tf_op jit(solution)/shard_map/rhgl,rhld->rhgd/dot_general | solution.py:67
  8.6 1.0 broadcast_in_dim.79
  9.6 8.4 %all-to-all-start = ((bf16[16,24,1024]{2,1,0:T(8,128)(2,1)}), bf16[16,24,1024]{2,1,0:T(8,128)(2,1)S(1)}, u32[]{:S(2)}, u32[]{:S(2)}) async-start(bf16[16,24,1024]{2,1,0:T(8,128)(2,1)} %broadcast_in_dim.79), calls=%async_computation | async-start | bytes 1572864 | tf_op jit(solution)/shard_map/all_to_all | solution.py:73
  18.0 3.8 %fusion.103 = (f32[24,8]{1,0:T(8,128)S(1)}, f32[24,8,768]{2,1,0:T(8,128)S(1)}) fusion(bf16[24,1,768,128]{3,2,1,0:T(8,128)(2,1)} %param.13, pred[24,768]{1,0:T(8,128)(4,1)S(1)} %iota_compare_fusion.1, bf16[24,1,16,128]{3,2,0,1:T(8,128)(2,1)S(1)} %bitcast.185), kind=kOutput, calls=%fused_computation.100 | convolution fusion | flops 38339328 | bytes 5376768 | tf_op jit(solution)/shard_map/sub | solution.py:65
  21.9 3.1 %fusion.59 = bf16[24,8,128]{2,1,0:T(8,128)(2,1)S(1)} fusion(bf16[24,1,768,128]{3,2,1,0:T(8,128)(2,1)} %param.14, f32[24,8,768]{2,1,0:T(8,128)S(1)} %get-tuple-element.12, f32[24,8]{1,0:T(8,128)S(1)} %get-tuple-element.11), kind=kOutput, calls=%fused_computation.41 | convolution fusion | flops 38068224 | bytes 5358336 | tf_op jit(solution)/shard_map/rhgl,rhld->rhgd/dot_general | solution.py:67
  25.0 5.8 %all-to-all-done = bf16[16,24,1024]{2,1,0:T(8,128)(2,1)S(1)} async-done(((bf16[16,24,1024]{2,1,0:T(8,128)(2,1)}), bf16[16,24,1024]{2,1,0:T(8,128)(2,1)S(1)}, u32[]{:S(2)}, u32[]{:S(2)}) %all-to-all-start) | async-done | bytes 786464 | tf_op jit(solution)/shard_map/all_to_all | solution.py:73
  30.8 1.0 broadcast_in_dim.81
  31.8 3.9 %all-to-all-start.1 = ((bf16[16,24,1024]{2,1,0:T(8,128)(2,1)}), bf16[16,24,1024]{2,1,0:T(8,128)(2,1)S(1)}, u32[]{:S(2)}, u32[]{:S(2)}) async-start(bf16[16,24,1024]{2,1,0:T(8,128)(2,1)} %broadcast_in_dim.81), calls=%async_computation.1 | async-start | bytes 1572864 | tf_op jit(solution)/shard_map/all_to_all | solution.py:73
  35.7 2.4 %collective-permute-start = (bf16[16,24,1024]{2,1,0:T(8,128)(2,1)S(1)}, bf16[16,24,1024]{2,1,0:T(8,128)(2,1)S(1)}, u32[]{:S(2)}, u32[]{:S(2)}) collective-permute-start(bf16[16,24,1024]{2,1,0:T(8,128)(2,1)S(1)} %all-to-all-done), channel_id=1, source_target_pairs={{0,4},{4,0},{1,5},{5,1},{2,6},{6,2},{3,7},{7,3},{8,12},{12,8},{9,1... | collective-permute-start | bytes 2359304 | tf_op jit(solution)/shard_map/ppermute | solution.py:74
  38.1 9.6 %all-to-all-done.1 = bf16[16,24,1024]{2,1,0:T(8,128)(2,1)S(1)} async-done(((bf16[16,24,1024]{2,1,0:T(8,128)(2,1)}), bf16[16,24,1024]{2,1,0:T(8,128)(2,1)S(1)}, u32[]{:S(2)}, u32[]{:S(2)}) %all-to-all-start.1) | async-done | bytes 786464 | tf_op jit(solution)/shard_map/all_to_all | solution.py:73
  47.7 3.3 %collective-permute-start.1 = (bf16[16,24,1024]{2,1,0:T(8,128)(2,1)S(1)}, bf16[16,24,1024]{2,1,0:T(8,128)(2,1)S(1)}, u32[]{:S(2)}, u32[]{:S(2)}) collective-permute-start(bf16[16,24,1024]{2,1,0:T(8,128)(2,1)S(1)} %all-to-all-done.1), channel_id=1, source_target_pairs={{0,4},{4,0},{1,5},{5,1},{2,6},{6,2},{3,7},{7,3},{8,12},{12,8},{9,1... | collective-permute-start | bytes 2359304 | tf_op jit(solution)/shard_map/ppermute | solution.py:74
  51.0 0.1 copy.39
  51.0 1.1 fusion.101
  52.1 0.4 convolution_bitcast_fusion.3
  52.5 0.0 copy-start
  52.5 0.4 convolution_bitcast_fusion.1
  52.9 0.0 collective-permute-done
  52.9 0.4 convolution_bitcast_fusion.2
  53.3 0.0 collective-permute-done.1
  53.3 0.4 convolution_bitcast_fusion
  53.7 0.0 copy-start.1
  53.8 1.0 broadcast_in_dim.82
  54.8 5.8 %all-to-all-start.2 = ((bf16[128,24,128]{2,1,0:T(8,128)(2,1)}), bf16[128,24,128]{2,1,0:T(8,128)(2,1)S(1)}, u32[]{:S(2)}, u32[]{:S(2)}) async-start(bf16[128,24,128]{2,1,0:T(8,128)(2,1)} %bitcast.16), calls=%async_computation.2 | async-start | bytes 1572864 | tf_op jit(solution)/shard_map/all_to_all | solution.py:83
  60.6 0.1 convert_reduce_fusion
  60.7 0.1 copy.43
  60.8 0.1 copy.42
  61.0 0.1 copy.44
  61.1 0.1 copy.45
  61.2 16.3 %all-to-all-done.2 = bf16[128,24,128]{2,1,0:T(8,128)(2,1)S(1)} async-done(((bf16[128,24,128]{2,1,0:T(8,128)(2,1)}), bf16[128,24,128]{2,1,0:T(8,128)(2,1)S(1)}, u32[]{:S(2)}, u32[]{:S(2)}) %all-to-all-start.2) | async-done | bytes 786464 | tf_op jit(solution)/shard_map/all_to_all | solution.py:83
  77.5 0.1 bitcast_reduce_fusion
  77.6 0.0 copy-done
  77.6 0.2 fusion.71
  77.8 0.4 fusion.19
  78.2 1.3 %copy.46 = bf16[32,1,2,4096]{3,2,1,0:T(2,128)(2,1)} copy(bf16[32,1,2,4096]{3,0,2,1:T(8,128)(2,1)S(1)} %fusion.19) | data formatting | bytes 1048576 | tf_op jit(solution)/shard_map/convert_element_type | solution.py:103
  79.6 4.0 %all-to-all-start.3 = ((bf16[32,1,2,4096]{3,2,1,0:T(2,128)(2,1)}), bf16[32,1,2,4096]{3,2,1,0:T(2,128)(2,1)S(1)}, u32[]{:S(2)}, u32[]{:S(2)}) async-start(bf16[32,1,2,4096]{3,2,1,0:T(2,128)(2,1)} %copy.46), calls=%async_computation.3 | async-start | bytes 1048576 | tf_op jit(solution)/shard_map/all_to_all | solution.py:104
  83.6 11.6 %all-to-all-done.3 = bf16[32,1,2,4096]{3,2,1,0:T(2,128)(2,1)S(1)} async-done(((bf16[32,1,2,4096]{3,2,1,0:T(2,128)(2,1)}), bf16[32,1,2,4096]{3,2,1,0:T(2,128)(2,1)S(1)}, u32[]{:S(2)}, u32[]{:S(2)}) %all-to-all-start.3) | async-done | bytes 524320 | tf_op jit(solution)/shard_map/all_to_all | solution.py:104
  95.1 4.2 %fusion.39 = f32[32,1,2,768]{3,0,2,1:T(8,128)S(1)} fusion(bf16[1,4096,768]{2,1,0:T(8,128)(2,1)} %param.19, bf16[32,1,2,4096]{3,2,1,0:T(2,128)(2,1)S(1)} %all-to-all-done.3), kind=kOutput, calls=%fused_computation.28 | convolution fusion | flops 402653184 | bytes 7012352 | tf_op jit(solution)/shard_map/sjcd,jdf->sjcf/dot_general | solution.py:105
  99.3 7.5 %fusion.20 = bf16[32,1,2,4096]{3,0,2,1:T(8,128)(2,1)S(1)} fusion(bf16[1,768,4096]{2,1,0:T(8,128)(2,1)} %param.21, bf16[1,4096,768]{2,1,0:T(8,128)(2,1)} %param.20, bf16[32,1,2,4096]{3,2,1,0:T(2,128)(2,1)S(1)} %all-to-all-done.3, f32[32,1,2,768]{3,0,2,1:T(8,128)S(1)} %fusion.39), kind=kOutput, calls=%fused_computation.19 | convolution fusion | flops 805863424 | bytes 13828096 | tf_op jit(solution)/shard_map/sjcf,jfd->sjcd/dot_general | solution.py:110
  106.9 0.4 reshape.195
  107.2 1.3 %copy.48 = bf16[32,4,1,2,1024]{4,3,1,0,2:T(2,128)(2,1)} copy(bf16[32,4,1,2,1024]{4,1,0,3,2:T(4,128)(2,1)S(1)} %bitcast.179) | data formatting | bytes 1048576 | tf_op jit(solution)/shard_map/transpose | solution.py:116
  108.6 3.9 %all-to-all-start.4 = ((bf16[128,2,1024]{2,1,0:T(2,128)(2,1)}), bf16[128,2,1024]{2,1,0:T(2,128)(2,1)S(1)}, u32[]{:S(2)}, u32[]{:S(2)}) async-start(bf16[128,2,1024]{2,1,0:T(2,128)(2,1)} %bitcast.47), calls=%async_computation.4 | async-start | bytes 1048576 | tf_op jit(solution)/shard_map/all_to_all | solution.py:117
  112.5 0.1 copy.41
  112.6 0.1 select_reduce_fusion
  112.7 13.9 %all-to-all-done.4 = bf16[128,2,1024]{2,1,0:T(2,128)(2,1)S(1)} async-done(((bf16[128,2,1024]{2,1,0:T(2,128)(2,1)}), bf16[128,2,1024]{2,1,0:T(2,128)(2,1)S(1)}, u32[]{:S(2)}, u32[]{:S(2)}) %all-to-all-start.4) | async-done | bytes 524320 | tf_op jit(solution)/shard_map/all_to_all | solution.py:117
  126.6 1.0 fusion.55
  (18 shorter events, 0.3 us)
Async XLA Ops:
  9.6 21.2 %all-to-all-start = ((bf16[16,24,1024]{2,1,0:T(8,128)(2,1)}), bf16[16,24,1024]{2,1,0:T(8,128)(2,1)S(1)}, u32[]{:S(2)}, u32[]{:S(2)}) async-start(bf16[16,24,1024]{2,1,0:T(8,128)(2,1)} %broadcast_in_dim.79), calls=%async_computation | async-start | bytes 1572864 | tf_op jit(solution)/shard_map/all_to_all | solution.py:73
  21.9 29.1 %copy-start.2 = (s32[24,8]{0,1:T(8,128)S(1)}, s32[24,8]{0,1:T(8,128)}, u32[]{:S(2)}) copy-start(s32[24,8]{0,1:T(8,128)} %param.17) | copy-start | bytes 2308
  31.8 15.9 %all-to-all-start.1 = ((bf16[16,24,1024]{2,1,0:T(8,128)(2,1)}), bf16[16,24,1024]{2,1,0:T(8,128)(2,1)S(1)}, u32[]{:S(2)}, u32[]{:S(2)}) async-start(bf16[16,24,1024]{2,1,0:T(8,128)(2,1)} %broadcast_in_dim.81), calls=%async_computation.1 | async-start | bytes 1572864 | tf_op jit(solution)/shard_map/all_to_all | solution.py:73
  35.7 17.2 %collective-permute-start = (bf16[16,24,1024]{2,1,0:T(8,128)(2,1)S(1)}, bf16[16,24,1024]{2,1,0:T(8,128)(2,1)S(1)}, u32[]{:S(2)}, u32[]{:S(2)}) collective-permute-start(bf16[16,24,1024]{2,1,0:T(8,128)(2,1)S(1)} %all-to-all-done), channel_id=1, source_target_pairs={{0,4},{4,0},{1,5},{5,1},{2,6},{6,2},{3,7},{7,3},{8,12},{12,8},{9,1... | collective-permute-start | bytes 2359304 | tf_op jit(solution)/shard_map/ppermute | solution.py:74
  47.7 5.6 %collective-permute-start.1 = (bf16[16,24,1024]{2,1,0:T(8,128)(2,1)S(1)}, bf16[16,24,1024]{2,1,0:T(8,128)(2,1)S(1)}, u32[]{:S(2)}, u32[]{:S(2)}) collective-permute-start(bf16[16,24,1024]{2,1,0:T(8,128)(2,1)S(1)} %all-to-all-done.1), channel_id=1, source_target_pairs={{0,4},{4,0},{1,5},{5,1},{2,6},{6,2},{3,7},{7,3},{8,12},{12,8},{9,1... | collective-permute-start | bytes 2359304 | tf_op jit(solution)/shard_map/ppermute | solution.py:74
  52.5 25.2 %copy-start = (bf16[24,4096]{1,0:T(8,128)(2,1)S(1)}, bf16[24,4096]{1,0:T(8,128)(2,1)}, u32[]{:S(2)}) copy-start(bf16[24,4096]{1,0:T(8,128)(2,1)} %param.11) | copy-start | bytes 589828
  53.7 29.9 %copy-start.1 = (f32[24,8]{0,1:T(8,128)S(1)}, f32[24,8]{0,1:T(8,128)}, u32[]{:S(2)}) copy-start(f32[24,8]{0,1:T(8,128)} %param.18) | copy-start | bytes 2308
  54.8 22.7 %all-to-all-start.2 = ((bf16[128,24,128]{2,1,0:T(8,128)(2,1)}), bf16[128,24,128]{2,1,0:T(8,128)(2,1)S(1)}, u32[]{:S(2)}, u32[]{:S(2)}) async-start(bf16[128,24,128]{2,1,0:T(8,128)(2,1)} %bitcast.16), calls=%async_computation.2 | async-start | bytes 1572864 | tf_op jit(solution)/shard_map/all_to_all | solution.py:83
  79.6 15.6 %all-to-all-start.3 = ((bf16[32,1,2,4096]{3,2,1,0:T(2,128)(2,1)}), bf16[32,1,2,4096]{3,2,1,0:T(2,128)(2,1)S(1)}, u32[]{:S(2)}, u32[]{:S(2)}) async-start(bf16[32,1,2,4096]{3,2,1,0:T(2,128)(2,1)} %copy.46), calls=%async_computation.3 | async-start | bytes 1048576 | tf_op jit(solution)/shard_map/all_to_all | solution.py:104
  108.6 18.0 %all-to-all-start.4 = ((bf16[128,2,1024]{2,1,0:T(2,128)(2,1)}), bf16[128,2,1024]{2,1,0:T(2,128)(2,1)S(1)}, u32[]{:S(2)}, u32[]{:S(2)}) async-start(bf16[128,2,1024]{2,1,0:T(2,128)(2,1)} %bitcast.47), calls=%async_computation.4 | async-start | bytes 1048576 | tf_op jit(solution)/shard_map/all_to_all | solution.py:117

commit v4 on v1

--- a/solution.py
+++ b/solution.py
@@ -1,9 +1,12 @@
+import functools
 import math
 
 import jax
 import jax.numpy as jnp
 import numpy as np
 from jax import lax
+from jax.experimental import pallas as pl
+from jax.experimental.pallas import tpu as pltpu
 from jax.sharding import Mesh, PartitionSpec as P
 
 CAP = 2
@@ -20,6 +23,55 @@
         resid_f * lax.rsqrt(jnp.mean(resid_f * resid_f, axis=-1, keepdims=True) + 1e-06)
     ).astype(jnp.bfloat16)
     return (residual, normed)
+
+
+def attention_kernel(len_ref, q_ref, k_ref, v_ref, o_ref, *, block_rows, scale):
+    base = pl.program_id(0) * block_rows
+    for r in range(block_rows):
+        q = q_ref[r]
+        k = k_ref[r, 0]
+        v = v_ref[r, 0]
+        scores = (
+            lax.dot_general(q, k, (((1,), (1,)), ((), ())), preferred_element_type=jnp.float32)
+            * scale
+        )
+        position = lax.broadcasted_iota(jnp.int32, scores.shape, 1)
+        scores = jnp.where(position < len_ref[base + r], scores, -jnp.inf)
+        largest = jnp.max(scores, axis=-1, keepdims=True)
+        exponent = jnp.exp(scores - largest)
+        probs = (exponent / jnp.sum(exponent, axis=-1, keepdims=True)).astype(jnp.bfloat16)
+        o_ref[r] = jnp.dot(probs, v, preferred_element_type=jnp.float32).astype(o_ref.dtype)
+
+
+def attention(queries, key_cache, cached_value_rows, cache_lengths, block_rows=4):
+    rows, kv_local, cache_len, head_dim = key_cache.shape
+    assert kv_local == 1
+    heads = queries.shape[1] // head_dim
+    q = queries.reshape(rows, heads, head_dim)
+    kernel = functools.partial(
+        attention_kernel, block_rows=block_rows, scale=1.0 / math.sqrt(head_dim)
+    )
+    grid_spec = pltpu.PrefetchScalarGridSpec(
+        num_scalar_prefetch=1,
+        grid=(rows // block_rows,),
+        in_specs=[
+            pl.BlockSpec((block_rows, heads, head_dim), lambda i, n: (i, 0, 0)),
+            pl.BlockSpec((block_rows, 1, cache_len, head_dim), lambda i, n: (i, 0, 0, 0)),
+            pl.BlockSpec((block_rows, 1, cache_len, head_dim), lambda i, n: (i, 0, 0, 0)),
+        ],
+        out_specs=pl.BlockSpec((block_rows, heads, head_dim), lambda i, n: (i, 0, 0)),
+    )
+    out = pl.pallas_call(
+        kernel,
+        grid_spec=grid_spec,
+        out_shape=jax.ShapeDtypeStruct((rows, heads, head_dim), jnp.bfloat16),
+        cost_estimate=pl.CostEstimate(
+            flops=4 * rows * heads * cache_len * head_dim,
+            transcendentals=rows * heads * cache_len,
+            bytes_accessed=2 * (2 * rows * cache_len * head_dim + 2 * rows * heads * head_dim),
+        ),
+    )(cache_lengths, q, key_cache, cached_value_rows)
+    return out.reshape(rows, heads * head_dim)
 
 
 def local(
@@ -47,21 +99,7 @@
     col_block = model_width // dp_count
     n_all = dp_count * tp_count
 
-    query_head_count = queries.reshape(rows_dev, kv_local, groups, head_dim)
-    scores = jnp.einsum(
-        "rhgd,rhld->rhgl", query_head_count, key_cache, preferred_element_type=jnp.float32
-    ) * (1.0 / math.sqrt(head_dim))
-    valid_mask = (jnp.arange(cache_len, dtype=jnp.int32)[None, :] < cache_lengths[:, None])[
-        :, None, None, :
-    ]
-    scores = jnp.where(valid_mask, scores, -jnp.inf)
-    largest = jnp.max(scores, axis=-1, keepdims=True)
-    exponent = jnp.exp(scores - largest)
-    attn_probs = (exponent / jnp.sum(exponent, axis=-1, keepdims=True)).astype(jnp.bfloat16)
-    attn_out = jnp.einsum(
-        "rhgl,rhld->rhgd", attn_probs, cached_value_rows, preferred_element_type=jnp.float32
-    ).astype(jnp.bfloat16)
-    attn_out = attn_out.reshape(rows_dev, kv_local * groups * head_dim)
+    attn_out = attention(queries, key_cache, cached_value_rows, cache_lengths)
 
     sent = jnp.broadcast_to(attn_out[None], (n_xz,) + attn_out.shape)
     mine = lax.all_to_all(sent, ("x", "z"), 0, 0, tiled=True)

time: 121 us -> 127 us (1.050)
  Pallas kernels: 0 us -> 12.6 us
  matrix products: 22.6 us -> 15.7 us
  local copies, waits for them, and re-layouts: 5.78 us -> 7.28 us
    pallas_call x0 -> x1, Pallas kernels: none -> 12.6 us  [attention(): pl.pallas_call(kernel, grid_spec=grid_spec, out_shape=jax.ShapeDtypeStruc...]
    sub x1 -> x0, matrix products: 3.84 us -> none  [local(): exponent = jnp.exp(scores - largest)]
    dot_general x1 -> x0, matrix products: 3.13 us -> none  [local(): jnp.einsum('rhgl,rhld->rhgd', attn_probs, cached_value_rows, preferred_el...]
    unnamed x11, local copies, waits for them, and re-layouts: 1.09 us -> 2.6 us
where the time goes in v4:
time: 127 us
  waiting for transfers between devices  44.2 us (35%)
  blocking collectives  29.9 us (24%)
  starting transfers between devices  16.2 us (13%)
  matrix products  15.7 us (12%)
  Pallas kernels  12.6 us (10%)
  local copies, waits for them, and re-layouts  7.28 us (6%)
    all_to_all x1, blocking collectives, local(): mine = lax.all_to_all(sent, ('x', 'z'), 0, 0, tiled=True)  29.9 us
    all_to_all x1, waiting for transfers between devices, local(): lax.all_to_all(sent.reshape(n_all, rows_dev, col_block), ALL, 0, 0, tiled...  16.3 us
    all_to_all x1, waiting for transfers between devices, local(): results = lax.all_to_all(back, ALL, 0, 0, tiled=True)  13.9 us
    pallas_call x1, Pallas kernels, attention(): pl.pallas_call(kernel, grid_spec=grid_spec, out_shape=jax.ShapeDtypeStruc...  12.6 us
    all_to_all x1, waiting for transfers between devices, local(): arrived_slots = lax.all_to_all(outgoing, DP, 0, 0, tiled=True)  11.6 us
    dot_general x1, matrix products, local(): jnp.einsum('sjcf,jfd->sjcd', activated, w_down, preferred_element_type=jn...  7.55 us
    all_to_all x1, starting transfers between devices, local(): lax.all_to_all(sent.reshape(n_all, rows_dev, col_block), ALL, 0, 0, tiled...  6.33 us
    dot_general x1, matrix products, local(): jnp.einsum('sjcd,jdf->sjcf', arrived_slots, w_gate, preferred_element_typ...  4.17 us
  transfers between devices with their start and end apart: 4, of which 4 were waited for; matrix products, arithmetic and copies ran while one was open for 1% of the time, Pallas kernels for 0%

profile of v4, /device:TPU:1, one launch (start us, length us, event | category | flops | bytes accessed | tf_op | source)
XLA Modules:
  0.0 126.8 jit_solution(13506430325630557286)
XLA Ops:
  0.0 0.0 copy-start
  0.0 1.6 %copy.51 = bf16[3,8,16,128]{3,2,1,0:T(8,128)(2,1)} copy(bf16[3,8,16,128]{3,1,2,0:T(8,128)(2,1)} %bitcast.131) | data formatting | bytes 196608
  1.6 0.0 copy-start.3
  1.6 12.6 %shard_map.109 = bf16[24,16,128]{2,1,0:T(8,128)(2,1)} custom-call(s32[24]{0:T(128)} %len_ref.1, bf16[24,16,128]{2,1,0:T(8,128)(2,1)} %bitcast.126, bf16[24,1,768,128]{3,2,1,0:T(8,128)(2,1)} %k_ref.1, bf16[24,1,768,128]{3,2,1,0:T(8,128)(2,1)} %v_ref.1), custom_call_target="tpu_custom_call" | custom-call | flops 150994944 | bytes 9633792 | tf_op jit(solution)/shard_map/pallas_call | solution.py:64
  14.2 0.9 copy.67
  15.1 0.2 broadcast_in_dim.27
  15.3 0.0 copy-start.1
  15.3 29.9 %all_to_all.20 = bf16[16,24,2048]{2,1,0:T(8,128)(2,1)S(1)} all-to-all(bf16[16,24,2048]{2,1,0:T(8,128)(2,1)S(1)} %broadcast_in_dim.27), channel_id=1, replica_groups=mesh['x'=4,'z'=4,'c'=2,'tensor'=4] {'x','z'}, dimensions={0} | all-to-all | bytes 3145728 | tf_op jit(solution)/shard_map/all_to_all | solution.py:105
  45.2 2.0 %collective-permute-start = (bf16[16,24,2048]{2,1,0:T(8,128)(2,1)S(1)}, bf16[16,24,2048]{2,1,0:T(8,128)(2,1)}, u32[]{:S(2)}, u32[]{:S(2)}) collective-permute-start(bf16[16,24,2048]{2,1,0:T(8,128)(2,1)S(1)} %all_to_all.20), channel_id=1, source_target_pairs={{0,4},{4,0},{1,5},{5,1},{2,6},{6,2},{3,7},{7,3},{8,12},{12,8},{9,1... | collective-permute-start | bytes 4718600 | tf_op jit(solution)/shard_map/ppermute | solution.py:106
  47.2 0.0 copy-done.3
  47.2 0.1 copy.39
  47.3 0.0 copy-done
  47.3 0.0 copy-start.2
  47.3 0.6 convolution_bitcast_fusion.1
  47.9 2.5 %collective-permute-done = bf16[16,24,2048]{2,1,0:T(8,128)(2,1)} collective-permute-done((bf16[16,24,2048]{2,1,0:T(8,128)(2,1)S(1)}, bf16[16,24,2048]{2,1,0:T(8,128)(2,1)}, u32[]{:S(2)}, u32[]{:S(2)}) %collective-permute-start) | collective-permute-done | bytes 1572896 | tf_op jit(solution)/shard_map/ppermute | solution.py:106
  50.4 2.0 %convolution_bitcast_fusion = bf16[16,1,24,128]{3,2,0,1:T(8,128)(2,1)S(1)} fusion(bf16[16,24,2048]{2,1,0:T(8,128)(2,1)} %collective-permute-done, bf16[2048,128]{1,0:T(8,128)(2,1)S(1)} %copy-done), kind=kOutput, calls=%fused_computation.12 | convolution fusion | flops 201326592 | bytes 2195456 | tf_op jit(solution)/shard_map/ird,dc->irc/dot_general | solution.py:108
  52.5 1.0 broadcast_in_dim.48
  53.5 6.3 %all-to-all-start.1 = ((bf16[128,24,128]{2,1,0:T(8,128)(2,1)}), bf16[128,24,128]{2,1,0:T(8,128)(2,1)S(1)}, u32[]{:S(2)}, u32[]{:S(2)}) async-start(bf16[128,24,128]{2,1,0:T(8,128)(2,1)} %bitcast.4), calls=%async_computation.1 | async-start | bytes 1572864 | tf_op jit(solution)/shard_map/all_to_all | solution.py:114
  59.8 0.1 convert_reduce_fusion
  59.9 0.1 copy.43
  60.0 0.1 copy.42
  60.2 0.1 copy.44
  60.3 0.1 copy.45
  60.4 16.3 %all-to-all-done.1 = bf16[128,24,128]{2,1,0:T(8,128)(2,1)S(1)} async-done(((bf16[128,24,128]{2,1,0:T(8,128)(2,1)}), bf16[128,24,128]{2,1,0:T(8,128)(2,1)S(1)}, u32[]{:S(2)}, u32[]{:S(2)}) %all-to-all-start.1) | async-done | bytes 786464 | tf_op jit(solution)/shard_map/all_to_all | solution.py:114
  76.7 0.1 bitcast_reduce_fusion
  76.8 0.0 copy-done.1
  76.8 0.2 fusion.41
  77.0 0.4 fusion.9
  77.4 1.3 %copy.46 = bf16[32,1,2,4096]{3,2,1,0:T(2,128)(2,1)} copy(bf16[32,1,2,4096]{3,0,2,1:T(8,128)(2,1)S(1)} %fusion.9) | data formatting | bytes 1048576 | tf_op jit(solution)/shard_map/convert_element_type | solution.py:134
  78.7 4.0 %all-to-all-start.2 = ((bf16[32,1,2,4096]{3,2,1,0:T(2,128)(2,1)}), bf16[32,1,2,4096]{3,2,1,0:T(2,128)(2,1)S(1)}, u32[]{:S(2)}, u32[]{:S(2)}) async-start(bf16[32,1,2,4096]{3,2,1,0:T(2,128)(2,1)} %copy.46), calls=%async_computation.2 | async-start | bytes 1048576 | tf_op jit(solution)/shard_map/all_to_all | solution.py:135
  82.7 0.0 copy-done.2
  82.8 11.6 %all-to-all-done.2 = bf16[32,1,2,4096]{3,2,1,0:T(2,128)(2,1)S(1)} async-done(((bf16[32,1,2,4096]{3,2,1,0:T(2,128)(2,1)}), bf16[32,1,2,4096]{3,2,1,0:T(2,128)(2,1)S(1)}, u32[]{:S(2)}, u32[]{:S(2)}) %all-to-all-start.2) | async-done | bytes 524320 | tf_op jit(solution)/shard_map/all_to_all | solution.py:135
  94.3 4.2 %fusion.13 = f32[32,1,2,768]{3,0,2,1:T(8,128)S(1)} fusion(bf16[1,4096,768]{2,1,0:T(8,128)(2,1)} %param.19, bf16[32,1,2,4096]{3,2,1,0:T(2,128)(2,1)S(1)} %all-to-all-done.2), kind=kOutput, calls=%fused_computation.10 | convolution fusion | flops 402653184 | bytes 7012352 | tf_op jit(solution)/shard_map/sjcd,jdf->sjcf/dot_general | solution.py:136
  98.5 7.5 %fusion.10 = bf16[32,1,2,4096]{3,0,2,1:T(8,128)(2,1)S(1)} fusion(bf16[1,768,4096]{2,1,0:T(8,128)(2,1)} %param.21, bf16[1,4096,768]{2,1,0:T(8,128)(2,1)} %param.20, bf16[32,1,2,4096]{3,2,1,0:T(2,128)(2,1)S(1)} %all-to-all-done.2, f32[32,1,2,768]{3,0,2,1:T(8,128)S(1)} %fusion.13), kind=kOutput, calls=%fused_computation.9 | convolution fusion | flops 805863424 | bytes 13828096 | tf_op jit(solution)/shard_map/sjcf,jfd->sjcd/dot_general | solution.py:141
  106.0 0.4 reshape.101
  106.4 1.3 %copy.48 = bf16[32,4,1,2,1024]{4,3,1,0,2:T(2,128)(2,1)} copy(bf16[32,4,1,2,1024]{4,1,0,3,2:T(4,128)(2,1)S(1)} %bitcast.121) | data formatting | bytes 1048576 | tf_op jit(solution)/shard_map/transpose | solution.py:147
  107.8 3.9 %all-to-all-start.3 = ((bf16[128,2,1024]{2,1,0:T(2,128)(2,1)}), bf16[128,2,1024]{2,1,0:T(2,128)(2,1)S(1)}, u32[]{:S(2)}, u32[]{:S(2)}) async-start(bf16[128,2,1024]{2,1,0:T(2,128)(2,1)} %bitcast.35), calls=%async_computation.3 | async-start | bytes 1048576 | tf_op jit(solution)/shard_map/all_to_all | solution.py:148
  111.7 0.1 copy.41
  111.8 0.1 select_reduce_fusion
  111.9 13.9 %all-to-all-done.3 = bf16[128,2,1024]{2,1,0:T(2,128)(2,1)S(1)} async-done(((bf16[128,2,1024]{2,1,0:T(2,128)(2,1)}), bf16[128,2,1024]{2,1,0:T(2,128)(2,1)S(1)}, u32[]{:S(2)}, u32[]{:S(2)}) %all-to-all-start.3) | async-done | bytes 524320 | tf_op jit(solution)/shard_map/all_to_all | solution.py:148
  125.8 1.0 fusion.29
  (13 shorter events, 0.2 us)
Async XLA Ops:
  0.0 47.3 %copy-start = (bf16[2048,128]{1,0:T(8,128)(2,1)S(1)}, bf16[2048,128]{1,0:T(8,128)(2,1)}, u32[]{:S(2)}) copy-start(bf16[2048,128]{1,0:T(8,128)(2,1)} %param.16) | copy-start | bytes 1572868
  1.6 45.6 %copy-start.3 = (s32[24,8]{0,1:T(8,128)S(1)}, s32[24,8]{0,1:T(8,128)}, u32[]{:S(2)}) copy-start(s32[24,8]{0,1:T(8,128)} %param.17) | copy-start | bytes 2308
  15.3 61.5 %copy-start.1 = (bf16[24,4096]{1,0:T(8,128)(2,1)S(1)}, bf16[24,4096]{1,0:T(8,128)(2,1)}, u32[]{:S(2)}) copy-start(bf16[24,4096]{1,0:T(8,128)(2,1)} %param.11) | copy-start | bytes 589828
  45.2 5.1 %collective-permute-start = (bf16[16,24,2048]{2,1,0:T(8,128)(2,1)S(1)}, bf16[16,24,2048]{2,1,0:T(8,128)(2,1)}, u32[]{:S(2)}, u32[]{:S(2)}) collective-permute-start(bf16[16,24,2048]{2,1,0:T(8,128)(2,1)S(1)} %all_to_all.20), channel_id=1, source_target_pairs={{0,4},{4,0},{1,5},{5,1},{2,6},{6,2},{3,7},{7,3},{8,12},{12,8},{9,1... | collective-permute-start | bytes 4718600 | tf_op jit(solution)/shard_map/ppermute | solution.py:106
  47.3 35.5 %copy-start.2 = (f32[24,8]{0,1:T(8,128)S(1)}, f32[24,8]{0,1:T(8,128)}, u32[]{:S(2)}) copy-start(f32[24,8]{0,1:T(8,128)} %param.18) | copy-start | bytes 2308
  53.5 23.3 %all-to-all-start.1 = ((bf16[128,24,128]{2,1,0:T(8,128)(2,1)}), bf16[128,24,128]{2,1,0:T(8,128)(2,1)S(1)}, u32[]{:S(2)}, u32[]{:S(2)}) async-start(bf16[128,24,128]{2,1,0:T(8,128)(2,1)} %bitcast.4), calls=%async_computation.1 | async-start | bytes 1572864 | tf_op jit(solution)/shard_map/all_to_all | solution.py:114
  78.7 15.6 %all-to-all-start.2 = ((bf16[32,1,2,4096]{3,2,1,0:T(2,128)(2,1)}), bf16[32,1,2,4096]{3,2,1,0:T(2,128)(2,1)S(1)}, u32[]{:S(2)}, u32[]{:S(2)}) async-start(bf16[32,1,2,4096]{3,2,1,0:T(2,128)(2,1)} %copy.46), calls=%async_computation.2 | async-start | bytes 1048576 | tf_op jit(solution)/shard_map/all_to_all | solution.py:135
  107.8 18.0 %all-to-all-start.3 = ((bf16[128,2,1024]{2,1,0:T(2,128)(2,1)}), bf16[128,2,1024]{2,1,0:T(2,128)(2,1)S(1)}, u32[]{:S(2)}, u32[]{:S(2)}) async-start(bf16[128,2,1024]{2,1,0:T(2,128)(2,1)} %bitcast.35), calls=%async_computation.3 | async-start | bytes 1048576 | tf_op jit(solution)/shard_map/all_to_all | solution.py:148

commit v5 on v2

--- a/solution.py
+++ b/solution.py
@@ -24,26 +24,40 @@
     return (residual, normed)
 
 
-def ffn_kernel(x_ref, wg_ref, wu_ref, wd_ref, o_ref):
+def ffn_kernel(x_ref, wg_ref, wu_ref, wd_ref, o_ref, acc_ref):
+    step = pl.program_id(0)
+
+    @pl.when(step == 0)
+    def _():
+        acc_ref[...] = jnp.zeros_like(acc_ref)
+
     x = x_ref[...]
     gate = jnp.dot(x, wg_ref[...], preferred_element_type=jnp.float32)
     up = jnp.dot(x, wu_ref[...], preferred_element_type=jnp.float32)
     activated = (gate / (1.0 + jnp.exp(-gate)) * up).astype(jnp.bfloat16)
-    o_ref[...] = jnp.dot(activated, wd_ref[...], preferred_element_type=jnp.float32).astype(
-        o_ref.dtype
-    )
+    acc_ref[...] += jnp.dot(activated, wd_ref[...], preferred_element_type=jnp.float32)
+
+    @pl.when(step == pl.num_programs(0) - 1)
+    def _():
+        o_ref[...] = acc_ref[...].astype(o_ref.dtype)
 
 
-def expert_ffn(x, wg, wu, wd):
+def expert_ffn(x, wg, wu, wd, chunk=128):
     rows, width = x.shape
     ff = wg.shape[1]
-    vmem = pl.BlockSpec(memory_space=pltpu.VMEM)
     return pl.pallas_call(
         ffn_kernel,
+        grid=(ff // chunk,),
+        in_specs=[
+            pl.BlockSpec((rows, width), lambda f: (0, 0)),
+            pl.BlockSpec((width, chunk), lambda f: (0, f)),
+            pl.BlockSpec((width, chunk), lambda f: (0, f)),
+            pl.BlockSpec((chunk, width), lambda f: (f, 0)),
+        ],
+        out_specs=pl.BlockSpec((rows, width), lambda f: (0, 0)),
         out_shape=jax.ShapeDtypeStruct((rows, width), jnp.bfloat16),
-        in_specs=[vmem] * 4,
-        out_specs=vmem,
-        compiler_params=pltpu.CompilerParams(vmem_limit_bytes=56 * 1024 * 1024),
+        scratch_shapes=[pltpu.VMEM((rows, width), jnp.float32)],
+        compiler_params=pltpu.CompilerParams(vmem_limit_bytes=40 * 1024 * 1024),
         cost_estimate=pl.CostEstimate(
             flops=6 * rows * width * ff,
             transcendentals=rows * ff,
@@ -125,15 +139,10 @@
         "rmjc,rd->mjcd", hit_col.astype(jnp.bfloat16), normed, preferred_element_type=jnp.float32
     ).astype(jnp.bfloat16)
     arrived_slots = lax.all_to_all(outgoing, DP, 0, 0, tiled=True)
-    expert_out = jnp.stack(
-        [
-            expert_ffn(
-                arrived_slots[:, j].reshape(dp_count * CAP, model_width), w_gate[j], w_up[j], w_down[j]
-            ).reshape(dp_count, CAP, model_width)
-            for j in range(exp_dev)
-        ],
-        axis=1,
-    )
+    assert exp_dev == 1
+    expert_out = expert_ffn(
+        arrived_slots.reshape(dp_count * CAP, model_width), w_gate[0], w_up[0], w_down[0]
+    ).reshape(dp_count, exp_dev, CAP, model_width)
 
     width_share = model_width // tp_count
     back = expert_out.reshape(dp_count, exp_dev, CAP, tp_count, width_share)

time: 122 us -> 123 us (level)
  local copies, waits for them, and re-layouts: 7.81 us -> 11.5 us
  Pallas kernels: 10.8 us -> 8.26 us
    unnamed x11 -> x15, local copies, waits for them, and re-layouts: 1.1 us -> 6.66 us
    pallas_call x1, Pallas kernels: 10.8 us -> 8.26 us  [expert_ffn(): pl.pallas_call(ffn_kernel, grid=(ff // chunk,), in_specs=[pl.BlockSpec((r...]
where the time goes in v5:
time: 123 us
  waiting for transfers between devices  44.2 us (36%)
  blocking collectives  29.8 us (24%)
  starting transfers between devices  16.2 us (13%)
  local copies, waits for them, and re-layouts  11.5 us (9%)
  matrix products  10.9 us (9%)
  Pallas kernels  8.26 us (7%)
  other arithmetic  1.44 us (1%)
    all_to_all x1, blocking collectives, local(): mine = lax.all_to_all(sent, ('x', 'z'), 0, 0, tiled=True)  29.8 us
    all_to_all x1, waiting for transfers between devices, local(): lax.all_to_all(sent.reshape(n_all, rows_dev, col_block), ALL, 0, 0, tiled...  16.3 us
    all_to_all x1, waiting for transfers between devices, local(): results = lax.all_to_all(back, ALL, 0, 0, tiled=True)  13.9 us
    all_to_all x1, waiting for transfers between devices, local(): arrived_slots = lax.all_to_all(outgoing, DP, 0, 0, tiled=True)  11.6 us
    pallas_call x1, Pallas kernels, expert_ffn(): pl.pallas_call(ffn_kernel, grid=(ff // chunk,), in_specs=[pl.BlockSpec((r...  8.26 us
    unnamed x15, local copies, waits for them, and re-layouts  6.66 us
    all_to_all x1, starting transfers between devices, local(): lax.all_to_all(sent.reshape(n_all, rows_dev, col_block), ALL, 0, 0, tiled...  6.33 us
    all_to_all x1, starting transfers between devices, local(): arrived_slots = lax.all_to_all(outgoing, DP, 0, 0, tiled=True)  3.97 us
  transfers between devices with their start and end apart: 4, of which 4 were waited for; matrix products, arithmetic and copies ran while one was open for 1% of the time, Pallas kernels for 0%

profile of v5, /device:TPU:1, one launch (start us, length us, event | category | flops | bytes accessed | tf_op | source)
XLA Modules:
  0.0 122.6 jit_solution(6579414930568089599)
XLA Ops:
  0.0 0.0 copy-start
  0.0 1.0 copy.53
  1.0 0.7 iota_compare_fusion.1
  1.7 3.8 %fusion.44 = (f32[24,16]{1,0:T(8,128)S(1)}, f32[24,16,768]{2,1,0:T(8,128)S(1)}) fusion(bf16[24,16,128]{2,1,0:T(8,128)(2,1)S(1)} %bitcast.79, bf16[24,1,768,128]{3,2,1,0:T(8,128)(2,1)} %param.13, pred[24,768]{1,0:T(8,128)(4,1)S(1)} %iota_compare_fusion.1), kind=kOutput, calls=%fused_computation.59 | convolution fusion | flops 76677888 | bytes 6016512 | tf_op jit(solution)/shard_map/sub | solution.py:103
  5.6 3.1 %fusion.14 = bf16[24,16,128]{2,1,0:T(8,128)(2,1)S(1)} fusion(bf16[24,1,768,128]{3,2,1,0:T(8,128)(2,1)} %param.14, f32[24,16,768]{2,1,0:T(8,128)S(1)} %get-tuple-element.8, f32[24,16]{1,0:T(8,128)S(1)} %get-tuple-element.7), kind=kOutput, calls=%fused_computation.14 | convolution fusion | flops 76136448 | bytes 5998080 | tf_op jit(solution)/shard_map/rhgl,rhld->rhgd/dot_general | solution.py:105
  8.7 0.2 broadcast_in_dim.66
  8.9 0.0 copy-start.5
  8.9 29.8 %all_to_all.20 = bf16[16,24,2048]{2,1,0:T(8,128)(2,1)S(1)} all-to-all(bf16[16,24,2048]{2,1,0:T(8,128)(2,1)S(1)} %broadcast_in_dim.66), channel_id=1, replica_groups=mesh['x'=4,'z'=4,'c'=2,'tensor'=4] {'x','z'}, dimensions={0} | all-to-all | bytes 3145728 | tf_op jit(solution)/shard_map/all_to_all | solution.py:111
  38.7 2.0 %collective-permute-start = (bf16[16,24,2048]{2,1,0:T(8,128)(2,1)S(1)}, bf16[16,24,2048]{2,1,0:T(8,128)(2,1)}, u32[]{:S(2)}, u32[]{:S(2)}) collective-permute-start(bf16[16,24,2048]{2,1,0:T(8,128)(2,1)S(1)} %all_to_all.20), channel_id=1, source_target_pairs={{0,4},{4,0},{1,5},{5,1},{2,6},{6,2},{3,7},{7,3},{8,12},{12,8},{9,1... | collective-permute-start | bytes 4718600 | tf_op jit(solution)/shard_map/ppermute | solution.py:112
  40.6 0.0 copy-done.5
  40.7 0.1 copy.42
  40.7 0.0 copy-done
  40.7 0.6 convolution_bitcast_fusion.1
  41.3 2.5 %collective-permute-done = bf16[16,24,2048]{2,1,0:T(8,128)(2,1)} collective-permute-done((bf16[16,24,2048]{2,1,0:T(8,128)(2,1)S(1)}, bf16[16,24,2048]{2,1,0:T(8,128)(2,1)}, u32[]{:S(2)}, u32[]{:S(2)}) %collective-permute-start) | collective-permute-done | bytes 1572896 | tf_op jit(solution)/shard_map/ppermute | solution.py:112
  43.8 2.0 %convolution_bitcast_fusion = bf16[16,1,24,128]{3,2,0,1:T(8,128)(2,1)S(1)} fusion(bf16[16,24,2048]{2,1,0:T(8,128)(2,1)} %collective-permute-done, bf16[2048,128]{1,0:T(8,128)(2,1)S(1)} %copy-done), kind=kOutput, calls=%fused_computation.12 | convolution fusion | flops 201326592 | bytes 2195456 | tf_op jit(solution)/shard_map/ird,dc->irc/dot_general | solution.py:114
  45.9 1.0 broadcast_in_dim.67
  46.9 0.0 copy-start.3
  46.9 6.3 %all-to-all-start.1 = ((bf16[128,24,128]{2,1,0:T(8,128)(2,1)}), bf16[128,24,128]{2,1,0:T(8,128)(2,1)S(1)}, u32[]{:S(2)}, u32[]{:S(2)}) async-start(bf16[128,24,128]{2,1,0:T(8,128)(2,1)} %bitcast.6), calls=%async_computation.1 | async-start | bytes 1572864 | tf_op jit(solution)/shard_map/all_to_all | solution.py:120
  53.3 0.1 convert_reduce_fusion
  53.4 0.1 copy.46
  53.5 0.1 copy.45
  53.6 0.1 copy.47
  53.7 0.1 copy.48
  53.9 16.3 %all-to-all-done.1 = bf16[128,24,128]{2,1,0:T(8,128)(2,1)S(1)} async-done(((bf16[128,24,128]{2,1,0:T(8,128)(2,1)}), bf16[128,24,128]{2,1,0:T(8,128)(2,1)S(1)}, u32[]{:S(2)}, u32[]{:S(2)}) %all-to-all-start.1) | async-done | bytes 786464 | tf_op jit(solution)/shard_map/all_to_all | solution.py:120
  70.2 0.1 bitcast_reduce_fusion
  70.3 0.0 copy-done.3
  70.3 0.0 copy-start.4
  70.3 0.2 fusion.23
  70.5 0.4 fusion.5
  70.9 1.3 %copy.49 = bf16[32,1,2,4096]{3,2,1,0:T(2,128)(2,1)} copy(bf16[32,1,2,4096]{3,0,2,1:T(8,128)(2,1)S(1)} %fusion.5) | data formatting | bytes 1048576 | tf_op jit(solution)/shard_map/convert_element_type | solution.py:140
  72.2 4.0 %all-to-all-start.2 = ((bf16[32,1,2,4096]{3,2,1,0:T(2,128)(2,1)}), bf16[32,1,2,4096]{3,2,1,0:T(2,128)(2,1)S(1)}, u32[]{:S(2)}, u32[]{:S(2)}) async-start(bf16[32,1,2,4096]{3,2,1,0:T(2,128)(2,1)} %copy.49), calls=%async_computation.2 | async-start | bytes 1048576 | tf_op jit(solution)/shard_map/all_to_all | solution.py:141
  76.2 0.0 copy-done.4
  76.2 11.6 %all-to-all-done.2 = bf16[32,1,2,4096]{3,2,1,0:T(2,128)(2,1)S(1)} async-done(((bf16[32,1,2,4096]{3,2,1,0:T(2,128)(2,1)}), bf16[32,1,2,4096]{3,2,1,0:T(2,128)(2,1)S(1)}, u32[]{:S(2)}, u32[]{:S(2)}) %all-to-all-start.2) | async-done | bytes 524320 | tf_op jit(solution)/shard_map/all_to_all | solution.py:141
  87.8 0.2 reshape.127.x_ref
  88.0 0.0 copy-start.1
  88.0 2.8 %copy-done.1 = bf16[1,4096,768]{2,1,0:T(8,128)(2,1)S(1)} copy-done((bf16[1,4096,768]{2,1,0:T(8,128)(2,1)S(1)}, bf16[1,4096,768]{2,1,0:T(8,128)(2,1)}, u32[]{:S(2)}) %copy-start.1) | copy-done | bytes 6291480
  90.8 0.0 copy-start.2
  90.8 2.8 %copy-done.2 = bf16[1,4096,768]{2,1,0:T(8,128)(2,1)S(1)} copy-done((bf16[1,4096,768]{2,1,0:T(8,128)(2,1)S(1)}, bf16[1,4096,768]{2,1,0:T(8,128)(2,1)}, u32[]{:S(2)}) %copy-start.2) | copy-done | bytes 6291480
  93.6 8.3 %shard_map.109 = bf16[64,4096]{1,0:T(8,128)(2,1)S(1)} custom-call(bf16[64,4096]{1,0:T(8,128)(2,1)S(1)} %reshape.127.x_ref, bf16[4096,768]{1,0:T(8,128)(2,1)S(1)} %bitcast.71, bf16[4096,768]{1,0:T(8,128)(2,1)S(1)} %bitcast.72, bf16[768,4096]{1,0:T(8,128)(2,1)} %bitcast.73), custom_call_target="tpu_custom_call" | custom-call | flops 1207959552 | bytes 19922944 | tf_op jit(solution)/shard_map/pallas_call | solution.py:48
  101.8 0.4 reshape_reshape.3
  102.2 1.3 %copy.50 = bf16[32,4,1,2,1024]{4,3,1,0,2:T(2,128)(2,1)} copy(bf16[32,4,1,2,1024]{4,1,3,0,2:T(4,128)(2,1)S(1)} %bitcast.74) | data formatting | bytes 1048576 | tf_op jit(solution)/shard_map/transpose | solution.py:149
  103.5 3.9 %all-to-all-start.3 = ((bf16[128,2,1024]{2,1,0:T(2,128)(2,1)}), bf16[128,2,1024]{2,1,0:T(2,128)(2,1)S(1)}, u32[]{:S(2)}, u32[]{:S(2)}) async-start(bf16[128,2,1024]{2,1,0:T(2,128)(2,1)} %bitcast.21), calls=%async_computation.3 | async-start | bytes 1048576 | tf_op jit(solution)/shard_map/all_to_all | solution.py:150
  107.5 0.1 copy.44
  107.6 0.1 select_reduce_fusion
  107.7 13.9 %all-to-all-done.3 = bf16[128,2,1024]{2,1,0:T(2,128)(2,1)S(1)} async-done(((bf16[128,2,1024]{2,1,0:T(2,128)(2,1)}), bf16[128,2,1024]{2,1,0:T(2,128)(2,1)S(1)}, u32[]{:S(2)}, u32[]{:S(2)}) %all-to-all-start.3) | async-done | bytes 524320 | tf_op jit(solution)/shard_map/all_to_all | solution.py:150
  121.6 1.0 fusion.18
  (14 shorter events, 0.3 us)
Async XLA Ops:
  0.0 40.7 %copy-start = (bf16[2048,128]{1,0:T(8,128)(2,1)S(1)}, bf16[2048,128]{1,0:T(8,128)(2,1)}, u32[]{:S(2)}) copy-start(bf16[2048,128]{1,0:T(8,128)(2,1)} %param.16) | copy-start | bytes 1572868
  8.9 31.7 %copy-start.5 = (s32[24,8]{0,1:T(8,128)S(1)}, s32[24,8]{0,1:T(8,128)}, u32[]{:S(2)}) copy-start(s32[24,8]{0,1:T(8,128)} %param.17) | copy-start | bytes 2308
  38.7 5.1 %collective-permute-start = (bf16[16,24,2048]{2,1,0:T(8,128)(2,1)S(1)}, bf16[16,24,2048]{2,1,0:T(8,128)(2,1)}, u32[]{:S(2)}, u32[]{:S(2)}) collective-permute-start(bf16[16,24,2048]{2,1,0:T(8,128)(2,1)S(1)} %all_to_all.20), channel_id=1, source_target_pairs={{0,4},{4,0},{1,5},{5,1},{2,6},{6,2},{3,7},{7,3},{8,12},{12,8},{9,1... | collective-permute-start | bytes 4718600 | tf_op jit(solution)/shard_map/ppermute | solution.py:112
  46.9 23.4 %copy-start.3 = (bf16[24,4096]{1,0:T(8,128)(2,1)S(1)}, bf16[24,4096]{1,0:T(8,128)(2,1)}, u32[]{:S(2)}) copy-start(bf16[24,4096]{1,0:T(8,128)(2,1)} %param.11) | copy-start | bytes 589828
  46.9 23.3 %all-to-all-start.1 = ((bf16[128,24,128]{2,1,0:T(8,128)(2,1)}), bf16[128,24,128]{2,1,0:T(8,128)(2,1)S(1)}, u32[]{:S(2)}, u32[]{:S(2)}) async-start(bf16[128,24,128]{2,1,0:T(8,128)(2,1)} %bitcast.6), calls=%async_computation.1 | async-start | bytes 1572864 | tf_op jit(solution)/shard_map/all_to_all | solution.py:120
  70.3 5.9 %copy-start.4 = (f32[24,8]{0,1:T(8,128)S(1)}, f32[24,8]{0,1:T(8,128)}, u32[]{:S(2)}) copy-start(f32[24,8]{0,1:T(8,128)} %param.18) | copy-start | bytes 2308
  72.2 15.6 %all-to-all-start.2 = ((bf16[32,1,2,4096]{3,2,1,0:T(2,128)(2,1)}), bf16[32,1,2,4096]{3,2,1,0:T(2,128)(2,1)S(1)}, u32[]{:S(2)}, u32[]{:S(2)}) async-start(bf16[32,1,2,4096]{3,2,1,0:T(2,128)(2,1)} %copy.49), calls=%async_computation.2 | async-start | bytes 1048576 | tf_op jit(solution)/shard_map/all_to_all | solution.py:141
  88.0 2.8 %copy-start.1 = (bf16[1,4096,768]{2,1,0:T(8,128)(2,1)S(1)}, bf16[1,4096,768]{2,1,0:T(8,128)(2,1)}, u32[]{:S(2)}) copy-start(bf16[1,4096,768]{2,1,0:T(8,128)(2,1)} %param.19) | copy-start | bytes 18874372
  90.8 2.8 %copy-start.2 = (bf16[1,4096,768]{2,1,0:T(8,128)(2,1)S(1)}, bf16[1,4096,768]{2,1,0:T(8,128)(2,1)}, u32[]{:S(2)}) copy-start(bf16[1,4096,768]{2,1,0:T(8,128)(2,1)} %param.20) | copy-start | bytes 18874372
  103.5 18.0 %all-to-all-start.3 = ((bf16[128,2,1024]{2,1,0:T(2,128)(2,1)}), bf16[128,2,1024]{2,1,0:T(2,128)(2,1)S(1)}, u32[]{:S(2)}, u32[]{:S(2)}) async-start(bf16[128,2,1024]{2,1,0:T(2,128)(2,1)} %bitcast.21), calls=%async_computation.3 | async-start | bytes 1048576 | tf_op jit(solution)/shard_map/all_to_all | solution.py:150

commit v6 on v5

--- a/solution.py
+++ b/solution.py
@@ -42,7 +42,7 @@
         o_ref[...] = acc_ref[...].astype(o_ref.dtype)
 
 
-def expert_ffn(x, wg, wu, wd, chunk=128):
+def expert_ffn(x, wg, wu, wd, chunk=256):
     rows, width = x.shape
     ff = wg.shape[1]
     return pl.pallas_call(
@@ -57,7 +57,7 @@
         out_specs=pl.BlockSpec((rows, width), lambda f: (0, 0)),
         out_shape=jax.ShapeDtypeStruct((rows, width), jnp.bfloat16),
         scratch_shapes=[pltpu.VMEM((rows, width), jnp.float32)],
-        compiler_params=pltpu.CompilerParams(vmem_limit_bytes=40 * 1024 * 1024),
+        compiler_params=pltpu.CompilerParams(vmem_limit_bytes=60 * 1024 * 1024),
         cost_estimate=pl.CostEstimate(
             flops=6 * rows * width * ff,
             transcendentals=rows * ff,

time: 123 us -> 121 us (0.984)
  local copies, waits for them, and re-layouts: 11.5 us -> 7.81 us
  Pallas kernels: 8.26 us -> 9.98 us
    unnamed x15 -> x11, local copies, waits for them, and re-layouts: 6.66 us -> 1.1 us
    pallas_call x1, Pallas kernels: 8.26 us -> 9.98 us  [expert_ffn(): pl.pallas_call(ffn_kernel, grid=(ff // chunk,), in_specs=[pl.BlockSpec((r...]
where the time goes in v6:
time: 121 us
  waiting for transfers between devices  44.2 us (37%)
  blocking collectives  29.8 us (25%)
  starting transfers between devices  16.2 us (13%)
  matrix products  10.9 us (9%)
  Pallas kernels  9.98 us (8%)
  local copies, waits for them, and re-layouts  7.81 us (6%)
  other arithmetic  1.44 us (1%)
    all_to_all x1, blocking collectives, local(): mine = lax.all_to_all(sent, ('x', 'z'), 0, 0, tiled=True)  29.8 us
    all_to_all x1, waiting for transfers between devices, local(): lax.all_to_all(sent.reshape(n_all, rows_dev, col_block), ALL, 0, 0, tiled...  16.3 us
    all_to_all x1, waiting for transfers between devices, local(): results = lax.all_to_all(back, ALL, 0, 0, tiled=True)  13.9 us
    all_to_all x1, waiting for transfers between devices, local(): arrived_slots = lax.all_to_all(outgoing, DP, 0, 0, tiled=True)  11.6 us
    pallas_call x1, Pallas kernels, expert_ffn(): pl.pallas_call(ffn_kernel, grid=(ff // chunk,), in_specs=[pl.BlockSpec((r...  9.98 us
    all_to_all x1, starting transfers between devices, local(): lax.all_to_all(sent.reshape(n_all, rows_dev, col_block), ALL, 0, 0, tiled...  6.33 us
    all_to_all x1, starting transfers between devices, local(): arrived_slots = lax.all_to_all(outgoing, DP, 0, 0, tiled=True)  3.97 us
    all_to_all x1, starting transfers between devices, local(): results = lax.all_to_all(back, ALL, 0, 0, tiled=True)  3.93 us
  transfers between devices with their start and end apart: 4, of which 4 were waited for; matrix products, arithmetic and copies ran while one was open for 1% of the time, Pallas kernels for 0%

profile of v6, /device:TPU:1, one launch (start us, length us, event | category | flops | bytes accessed | tf_op | source)
XLA Modules:
  0.0 120.5 jit_solution(13142128265841687317)
XLA Ops:
  0.0 0.0 copy-start
  0.0 1.0 copy.53
  1.0 0.7 iota_compare_fusion.1
  1.7 3.8 %fusion.44 = (f32[24,16]{1,0:T(8,128)S(1)}, f32[24,16,768]{2,1,0:T(8,128)S(1)}) fusion(bf16[24,16,128]{2,1,0:T(8,128)(2,1)S(1)} %bitcast.79, bf16[24,1,768,128]{3,2,1,0:T(8,128)(2,1)} %param.13, pred[24,768]{1,0:T(8,128)(4,1)S(1)} %iota_compare_fusion.1), kind=kOutput, calls=%fused_computation.59 | convolution fusion | flops 76677888 | bytes 6016512 | tf_op jit(solution)/shard_map/sub | solution.py:103
  5.6 3.1 %fusion.14 = bf16[24,16,128]{2,1,0:T(8,128)(2,1)S(1)} fusion(bf16[24,1,768,128]{3,2,1,0:T(8,128)(2,1)} %param.14, f32[24,16,768]{2,1,0:T(8,128)S(1)} %get-tuple-element.8, f32[24,16]{1,0:T(8,128)S(1)} %get-tuple-element.7), kind=kOutput, calls=%fused_computation.14 | convolution fusion | flops 76136448 | bytes 5998080 | tf_op jit(solution)/shard_map/rhgl,rhld->rhgd/dot_general | solution.py:105
  8.7 0.2 broadcast_in_dim.66
  8.9 0.0 copy-start.3
  8.9 29.8 %all_to_all.20 = bf16[16,24,2048]{2,1,0:T(8,128)(2,1)S(1)} all-to-all(bf16[16,24,2048]{2,1,0:T(8,128)(2,1)S(1)} %broadcast_in_dim.66), channel_id=1, replica_groups=mesh['x'=4,'z'=4,'c'=2,'tensor'=4] {'x','z'}, dimensions={0} | all-to-all | bytes 3145728 | tf_op jit(solution)/shard_map/all_to_all | solution.py:111
  38.7 2.0 %collective-permute-start = (bf16[16,24,2048]{2,1,0:T(8,128)(2,1)S(1)}, bf16[16,24,2048]{2,1,0:T(8,128)(2,1)}, u32[]{:S(2)}, u32[]{:S(2)}) collective-permute-start(bf16[16,24,2048]{2,1,0:T(8,128)(2,1)S(1)} %all_to_all.20), channel_id=1, source_target_pairs={{0,4},{4,0},{1,5},{5,1},{2,6},{6,2},{3,7},{7,3},{8,12},{12,8},{9,1... | collective-permute-start | bytes 4718600 | tf_op jit(solution)/shard_map/ppermute | solution.py:112
  40.6 0.0 copy-done.3
  40.7 0.1 copy.42
  40.7 0.0 copy-done
  40.7 0.6 convolution_bitcast_fusion.1
  41.3 2.5 %collective-permute-done = bf16[16,24,2048]{2,1,0:T(8,128)(2,1)} collective-permute-done((bf16[16,24,2048]{2,1,0:T(8,128)(2,1)S(1)}, bf16[16,24,2048]{2,1,0:T(8,128)(2,1)}, u32[]{:S(2)}, u32[]{:S(2)}) %collective-permute-start) | collective-permute-done | bytes 1572896 | tf_op jit(solution)/shard_map/ppermute | solution.py:112
  43.8 2.0 %convolution_bitcast_fusion = bf16[16,1,24,128]{3,2,0,1:T(8,128)(2,1)S(1)} fusion(bf16[16,24,2048]{2,1,0:T(8,128)(2,1)} %collective-permute-done, bf16[2048,128]{1,0:T(8,128)(2,1)S(1)} %copy-done), kind=kOutput, calls=%fused_computation.12 | convolution fusion | flops 201326592 | bytes 2195456 | tf_op jit(solution)/shard_map/ird,dc->irc/dot_general | solution.py:114
  45.9 1.0 broadcast_in_dim.67
  46.9 0.0 copy-start.1
  46.9 6.3 %all-to-all-start.1 = ((bf16[128,24,128]{2,1,0:T(8,128)(2,1)}), bf16[128,24,128]{2,1,0:T(8,128)(2,1)S(1)}, u32[]{:S(2)}, u32[]{:S(2)}) async-start(bf16[128,24,128]{2,1,0:T(8,128)(2,1)} %bitcast.6), calls=%async_computation.1 | async-start | bytes 1572864 | tf_op jit(solution)/shard_map/all_to_all | solution.py:120
  53.3 0.1 convert_reduce_fusion
  53.4 0.1 copy.46
  53.5 0.1 copy.45
  53.6 0.1 copy.47
  53.7 0.1 copy.48
  53.9 16.3 %all-to-all-done.1 = bf16[128,24,128]{2,1,0:T(8,128)(2,1)S(1)} async-done(((bf16[128,24,128]{2,1,0:T(8,128)(2,1)}), bf16[128,24,128]{2,1,0:T(8,128)(2,1)S(1)}, u32[]{:S(2)}, u32[]{:S(2)}) %all-to-all-start.1) | async-done | bytes 786464 | tf_op jit(solution)/shard_map/all_to_all | solution.py:120
  70.2 0.1 bitcast_reduce_fusion
  70.3 0.0 copy-done.1
  70.3 0.0 copy-start.2
  70.3 0.2 fusion.23
  70.5 0.4 fusion.5
  70.9 1.3 %copy.49 = bf16[32,1,2,4096]{3,2,1,0:T(2,128)(2,1)} copy(bf16[32,1,2,4096]{3,0,2,1:T(8,128)(2,1)S(1)} %fusion.5) | data formatting | bytes 1048576 | tf_op jit(solution)/shard_map/convert_element_type | solution.py:140
  72.2 4.0 %all-to-all-start.2 = ((bf16[32,1,2,4096]{3,2,1,0:T(2,128)(2,1)}), bf16[32,1,2,4096]{3,2,1,0:T(2,128)(2,1)S(1)}, u32[]{:S(2)}, u32[]{:S(2)}) async-start(bf16[32,1,2,4096]{3,2,1,0:T(2,128)(2,1)} %copy.49), calls=%async_computation.2 | async-start | bytes 1048576 | tf_op jit(solution)/shard_map/all_to_all | solution.py:141
  76.2 0.0 copy-done.2
  76.2 11.6 %all-to-all-done.2 = bf16[32,1,2,4096]{3,2,1,0:T(2,128)(2,1)S(1)} async-done(((bf16[32,1,2,4096]{3,2,1,0:T(2,128)(2,1)}), bf16[32,1,2,4096]{3,2,1,0:T(2,128)(2,1)S(1)}, u32[]{:S(2)}, u32[]{:S(2)}) %all-to-all-start.2) | async-done | bytes 524320 | tf_op jit(solution)/shard_map/all_to_all | solution.py:141
  87.8 1.0 reshape.127.x_ref
  88.8 10.0 %shard_map.109 = bf16[64,4096]{1,0:T(8,128)(2,1)} custom-call(bf16[64,4096]{1,0:T(8,128)(2,1)} %reshape.127.x_ref, bf16[4096,768]{1,0:T(8,128)(2,1)} %bitcast.71, bf16[4096,768]{1,0:T(8,128)(2,1)} %bitcast.72, bf16[768,4096]{1,0:T(8,128)(2,1)} %bitcast.73), custom_call_target="tpu_custom_call" | custom-call | flops 1207959552 | bytes 19922944 | tf_op jit(solution)/shard_map/pallas_call | solution.py:48
  98.8 1.4 %reshape_reshape.3 = bf16[32,1,2,4,1024]{4,3,2,0,1:T(4,128)(2,1)S(1)} reshape(bf16[64,4096]{1,0:T(8,128)(2,1)} %shard_map.109) | data formatting | bytes 1048576 | tf_op jit(solution)/shard_map/reshape;reshape | solution.py:148
  100.2 1.3 %copy.50 = bf16[32,4,1,2,1024]{4,3,1,0,2:T(2,128)(2,1)} copy(bf16[32,4,1,2,1024]{4,1,3,0,2:T(4,128)(2,1)S(1)} %bitcast.74) | data formatting | bytes 1048576 | tf_op jit(solution)/shard_map/transpose | solution.py:149
  101.5 3.9 %all-to-all-start.3 = ((bf16[128,2,1024]{2,1,0:T(2,128)(2,1)}), bf16[128,2,1024]{2,1,0:T(2,128)(2,1)S(1)}, u32[]{:S(2)}, u32[]{:S(2)}) async-start(bf16[128,2,1024]{2,1,0:T(2,128)(2,1)} %bitcast.21), calls=%async_computation.3 | async-start | bytes 1048576 | tf_op jit(solution)/shard_map/all_to_all | solution.py:150
  105.5 0.1 copy.44
  105.5 0.1 select_reduce_fusion
  105.7 13.9 %all-to-all-done.3 = bf16[128,2,1024]{2,1,0:T(2,128)(2,1)S(1)} async-done(((bf16[128,2,1024]{2,1,0:T(2,128)(2,1)}), bf16[128,2,1024]{2,1,0:T(2,128)(2,1)S(1)}, u32[]{:S(2)}, u32[]{:S(2)}) %all-to-all-start.3) | async-done | bytes 524320 | tf_op jit(solution)/shard_map/all_to_all | solution.py:150
  119.5 1.0 fusion.18
  (14 shorter events, 0.3 us)
Async XLA Ops:
  0.0 40.7 %copy-start = (bf16[2048,128]{1,0:T(8,128)(2,1)S(1)}, bf16[2048,128]{1,0:T(8,128)(2,1)}, u32[]{:S(2)}) copy-start(bf16[2048,128]{1,0:T(8,128)(2,1)} %param.16) | copy-start | bytes 1572868
  8.9 31.7 %copy-start.3 = (s32[24,8]{0,1:T(8,128)S(1)}, s32[24,8]{0,1:T(8,128)}, u32[]{:S(2)}) copy-start(s32[24,8]{0,1:T(8,128)} %param.17) | copy-start | bytes 2308
  38.7 5.1 %collective-permute-start = (bf16[16,24,2048]{2,1,0:T(8,128)(2,1)S(1)}, bf16[16,24,2048]{2,1,0:T(8,128)(2,1)}, u32[]{:S(2)}, u32[]{:S(2)}) collective-permute-start(bf16[16,24,2048]{2,1,0:T(8,128)(2,1)S(1)} %all_to_all.20), channel_id=1, source_target_pairs={{0,4},{4,0},{1,5},{5,1},{2,6},{6,2},{3,7},{7,3},{8,12},{12,8},{9,1... | collective-permute-start | bytes 4718600 | tf_op jit(solution)/shard_map/ppermute | solution.py:112
  46.9 23.4 %copy-start.1 = (bf16[24,4096]{1,0:T(8,128)(2,1)S(1)}, bf16[24,4096]{1,0:T(8,128)(2,1)}, u32[]{:S(2)}) copy-start(bf16[24,4096]{1,0:T(8,128)(2,1)} %param.11) | copy-start | bytes 589828
  46.9 23.3 %all-to-all-start.1 = ((bf16[128,24,128]{2,1,0:T(8,128)(2,1)}), bf16[128,24,128]{2,1,0:T(8,128)(2,1)S(1)}, u32[]{:S(2)}, u32[]{:S(2)}) async-start(bf16[128,24,128]{2,1,0:T(8,128)(2,1)} %bitcast.6), calls=%async_computation.1 | async-start | bytes 1572864 | tf_op jit(solution)/shard_map/all_to_all | solution.py:120
  70.3 5.9 %copy-start.2 = (f32[24,8]{0,1:T(8,128)S(1)}, f32[24,8]{0,1:T(8,128)}, u32[]{:S(2)}) copy-start(f32[24,8]{0,1:T(8,128)} %param.18) | copy-start | bytes 2308
  72.2 15.6 %all-to-all-start.2 = ((bf16[32,1,2,4096]{3,2,1,0:T(2,128)(2,1)}), bf16[32,1,2,4096]{3,2,1,0:T(2,128)(2,1)S(1)}, u32[]{:S(2)}, u32[]{:S(2)}) async-start(bf16[32,1,2,4096]{3,2,1,0:T(2,128)(2,1)} %copy.49), calls=%async_computation.2 | async-start | bytes 1048576 | tf_op jit(solution)/shard_map/all_to_all | solution.py:141
  101.5 18.0 %all-to-all-start.3 = ((bf16[128,2,1024]{2,1,0:T(2,128)(2,1)}), bf16[128,2,1024]{2,1,0:T(2,128)(2,1)S(1)}, u32[]{:S(2)}, u32[]{:S(2)}) async-start(bf16[128,2,1024]{2,1,0:T(2,128)(2,1)} %bitcast.21), calls=%async_computation.3 | async-start | bytes 1048576 | tf_op jit(solution)/shard_map/all_to_all | solution.py:150

commit v7 on v1

--- a/solution.py
+++ b/solution.py
@@ -63,18 +63,22 @@
     ).astype(jnp.bfloat16)
     attn_out = attn_out.reshape(rows_dev, kv_local * groups * head_dim)
 
+    w_other = lax.ppermute(out_weight, "c", [(i, (i + 1) % n_c) for i in range(n_c)])
+    w_lo = jnp.where(c_rank == 0, out_weight, w_other)
+    w_hi = jnp.where(c_rank == 0, w_other, out_weight)
+    w_pair = jnp.concatenate([w_lo, w_hi], axis=1)
     sent = jnp.broadcast_to(attn_out[None], (n_xz,) + attn_out.shape)
     mine = lax.all_to_all(sent, ("x", "z"), 0, 0, tiled=True)
-    other = lax.ppermute(mine, "c", [(i, (i + 1) % n_c) for i in range(n_c)])
-    part_mine = jnp.einsum("ird,dc->irc", mine, out_weight, preferred_element_type=jnp.float32)
-    part_other = jnp.einsum("ird,dc->irc", other, out_weight, preferred_element_type=jnp.float32)
-    slots = jnp.stack([part_mine, part_other], axis=1)
-    slots = jnp.where(c_rank == 0, slots, slots[:, ::-1])
-    partial_value = slots.reshape(dp_count, rows_dev, col_block).astype(jnp.bfloat16)
+    partial_value = jnp.einsum(
+        "ird,dc->irc", mine, w_pair, preferred_element_type=jnp.float32
+    ).astype(jnp.bfloat16)
 
-    sent = jnp.broadcast_to(partial_value[:, None], (dp_count, tp_count, rows_dev, col_block))
-    got = lax.all_to_all(sent.reshape(n_all, rows_dev, col_block), ALL, 0, 0, tiled=True)
-    projected = got.reshape(dp_count, tp_count, rows_dev, col_block).astype(jnp.float32).sum(1)
+    pair_cols = n_c * col_block
+    sent = jnp.broadcast_to(partial_value[:, None], (n_xz, tp_count, rows_dev, pair_cols))
+    got = lax.all_to_all(
+        sent.reshape(n_xz * tp_count, rows_dev, pair_cols), ("x", "z", "tensor"), 0, 0, tiled=True
+    )
+    projected = got.reshape(n_xz, tp_count, rows_dev, pair_cols).astype(jnp.float32).sum(1)
     projected = projected.transpose(1, 0, 2).reshape(rows_dev, model_width).astype(jnp.bfloat16)
     residual, normed = residual_norm(hidden_in, projected)
 

time: 121 us -> 118 us (0.975)
  blocking collectives: 29.8 us -> 0 us
  starting transfers between devices: 16.2 us -> 29.1 us
  waiting for transfers between devices: 44.2 us -> 57 us
    all_to_all x1 -> x0, blocking collectives: 29.8 us -> none  [local(): mine = lax.all_to_all(sent, ('x', 'z'), 0, 0, tiled=True)]
    all_to_all x1 -> x2, waiting for transfers between devices: 16.3 us -> 30 us  [the longest x1 17.3 us: local(): mine = lax.all_to_all(sent, ('x', 'z'), 0, 0, tiled=True)]
    all_to_all x1 -> x2, starting transfers between devices: 6.33 us -> 17.2 us  [the longest x1 8.83 us: local(): lax.all_to_all(sent.reshape(n_xz * tp_count, rows_dev, pair_cols), ('x',...]
    all_to_all x1, starting transfers between devices: 3.97 us -> 7.04 us  [local(): arrived_slots = lax.all_to_all(outgoing, DP, 0, 0, tiled=True)]
    dot_general x2 -> x1, matrix products: 2.57 us -> 1.66 us  [local(): jnp.einsum('ird,dc->irc', mine, w_pair, preferred_element_type=jnp.float32)]
  transfers between devices with their start and end apart: 4 -> 5, of which waited for: 4 -> 5; matrix products, arithmetic and copies ran while one was open for 1% -> 2% of each run, Pallas kernels for 0% -> 0%
where the time goes in v7:
time: 118 us; the launch traced here: 117 us
  waiting for transfers between devices  57 us (48%)
  starting transfers between devices  29.1 us (25%)
  matrix products  21.8 us (18%)
  local copies, waits for them, and re-layouts  6.84 us (6%)
  other arithmetic  2.28 us (2%)
    all_to_all x1, waiting for transfers between devices, local(): mine = lax.all_to_all(sent, ('x', 'z'), 0, 0, tiled=True)  17.3 us
    all_to_all x1, waiting for transfers between devices, local(): results = lax.all_to_all(back, ALL, 0, 0, tiled=True)  13.9 us
    all_to_all x1, waiting for transfers between devices, local(): lax.all_to_all(sent.reshape(n_xz * tp_count, rows_dev, pair_cols), ('x',...  12.7 us
    all_to_all x1, waiting for transfers between devices, local(): arrived_slots = lax.all_to_all(outgoing, DP, 0, 0, tiled=True)  11.7 us
    all_to_all x1, starting transfers between devices, local(): lax.all_to_all(sent.reshape(n_xz * tp_count, rows_dev, pair_cols), ('x',...  8.83 us
    all_to_all x1, starting transfers between devices, local(): mine = lax.all_to_all(sent, ('x', 'z'), 0, 0, tiled=True)  8.42 us
    dot_general x1, matrix products, local(): jnp.einsum('sjcf,jfd->sjcd', activated, w_down, preferred_element_type=jn...  7.55 us
    all_to_all x1, starting transfers between devices, local(): arrived_slots = lax.all_to_all(outgoing, DP, 0, 0, tiled=True)  7.04 us
  transfers between devices with their start and end apart: 5, of which 5 were waited for; matrix products, arithmetic and copies ran while one was open for 2% of the time, Pallas kernels for 0%

profile of v7, /device:TPU:1, one launch (start us, length us, event | category | flops | bytes accessed | tf_op | source)
XLA Modules:
  0.0 117.2 jit_solution(15043370240136276615)
XLA Ops:
  0.0 0.9 copy.48
  0.9 0.7 iota_compare_fusion.1
  1.7 3.8 %fusion.84 = (f32[24,16]{1,0:T(8,128)S(1)}, f32[24,16,768]{2,1,0:T(8,128)S(1)}) fusion(bf16[24,16,128]{2,1,0:T(8,128)(2,1)S(1)} %bitcast.128, bf16[24,1,768,128]{3,2,1,0:T(8,128)(2,1)} %param.13, pred[24,768]{1,0:T(8,128)(4,1)S(1)} %iota_compare_fusion.1), kind=kOutput, calls=%fused_computation.82 | convolution fusion | flops 76677888 | bytes 6016512 | tf_op jit(solution)/shard_map/sub | solution.py:59
  5.5 0.0 copy-start
  5.5 0.0 copy-start.3
  5.5 3.2 %fusion.38 = bf16[24,16,128]{2,1,0:T(8,128)(2,1)S(1)} fusion(bf16[24,1,768,128]{3,2,1,0:T(8,128)(2,1)} %param.14, f32[24,16,768]{2,1,0:T(8,128)S(1)} %get-tuple-element.10, f32[24,16]{1,0:T(8,128)S(1)} %get-tuple-element.9), kind=kOutput, calls=%fused_computation.25 | convolution fusion | flops 76136448 | bytes 5998080 | tf_op jit(solution)/shard_map/rhgl,rhld->rhgd/dot_general | solution.py:61
  8.7 1.3 %broadcast_in_dim.66 = bf16[16,24,2048]{2,1,0:T(8,128)(2,1)} broadcast(bf16[24,2048]{1,0:T(8,128)(2,1)S(1)} %bitcast.127), dimensions={1,2} | broadcast | bytes 1671168 | tf_op jit(solution)/shard_map/broadcast_in_dim | solution.py:70
  10.1 8.4 %all-to-all-start = ((bf16[16,24,2048]{2,1,0:T(8,128)(2,1)}), bf16[16,24,2048]{2,1,0:T(8,128)(2,1)S(1)}, u32[]{:S(2)}, u32[]{:S(2)}) async-start(bf16[16,24,2048]{2,1,0:T(8,128)(2,1)} %broadcast_in_dim.66), calls=%async_computation | async-start | bytes 3145728 | tf_op jit(solution)/shard_map/all_to_all | solution.py:71
  18.5 0.0 copy-done
  18.5 1.0 collective-permute-start
  19.5 0.0 copy-done.3
  19.5 0.1 copy.36
  19.6 1.5 %collective-permute-done = bf16[2048,128]{1,0:T(8,128)(2,1)S(1)} collective-permute-done((bf16[2048,128]{1,0:T(8,128)(2,1)S(1)}, bf16[2048,128]{1,0:T(8,128)(2,1)S(1)}, u32[]{:S(2)}, u32[]{:S(2)}) %collective-permute-start) | collective-permute-done | bytes 524320 | tf_op jit(solution)/shard_map/ppermute | solution.py:66
  21.1 0.9 broadcast_select_fusion.1
  22.0 17.3 %all-to-all-done = bf16[16,24,2048]{2,1,0:T(8,128)(2,1)S(1)} async-done(((bf16[16,24,2048]{2,1,0:T(8,128)(2,1)}), bf16[16,24,2048]{2,1,0:T(8,128)(2,1)S(1)}, u32[]{:S(2)}, u32[]{:S(2)}) %all-to-all-start) | async-done | bytes 1572896 | tf_op jit(solution)/shard_map/all_to_all | solution.py:71
  39.2 0.0 copy-start.1
  39.2 1.7 %convolution_convert_fusion.1 = bf16[16,24,256]{2,1,0:T(8,128)(2,1)S(1)} fusion(bf16[16,24,2048]{2,1,0:T(8,128)(2,1)S(1)} %all-to-all-done, bf16[2048,128]{1,0:T(8,128)(2,1)} %get-tuple-element.8, bf16[2048,128]{1,0:T(8,128)(2,1)S(1)} %get-tuple-element.7), kind=kOutput, calls=%fused_computation.20 | convolution fusion | flops 404848640 | bytes 2818048 | tf_op jit(solution)/shard_map/ird,dc->irc/dot_general | solution.py:72
  40.9 0.0 copy-start.2
  40.9 0.9 broadcast_in_dim.67
  41.8 8.8 %all-to-all-start.1 = ((bf16[64,24,256]{2,1,0:T(8,128)(2,1)}), bf16[64,24,256]{2,1,0:T(8,128)(2,1)S(1)}, u32[]{:S(2)}, u32[]{:S(2)}) async-start(bf16[64,24,256]{2,1,0:T(8,128)(2,1)} %bitcast.3), calls=%async_computation.1 | async-start | bytes 1572864 | tf_op jit(solution)/shard_map/all_to_all | solution.py:78
  50.7 0.1 convert_reduce_fusion
  50.8 0.1 copy.40
  50.9 0.1 copy.39
  51.0 0.1 copy.41
  51.2 0.1 copy.42
  51.3 12.7 %all-to-all-done.1 = bf16[64,24,256]{2,1,0:T(8,128)(2,1)S(1)} async-done(((bf16[64,24,256]{2,1,0:T(8,128)(2,1)}), bf16[64,24,256]{2,1,0:T(8,128)(2,1)S(1)}, u32[]{:S(2)}, u32[]{:S(2)}) %all-to-all-start.1) | async-done | bytes 786464 | tf_op jit(solution)/shard_map/all_to_all | solution.py:78
  64.0 0.1 bitcast_reduce_fusion
  64.2 0.0 copy-done.1
  64.2 0.2 fusion.58
  64.4 0.4 fusion.14
  64.8 1.3 %copy.43 = bf16[32,1,2,4096]{3,2,1,0:T(2,128)(2,1)} copy(bf16[32,1,2,4096]{3,0,2,1:T(8,128)(2,1)S(1)} %fusion.14) | data formatting | bytes 1048576 | tf_op jit(solution)/shard_map/convert_element_type | solution.py:100
  66.1 7.0 %all-to-all-start.2 = ((bf16[32,1,2,4096]{3,2,1,0:T(2,128)(2,1)}), bf16[32,1,2,4096]{3,2,1,0:T(2,128)(2,1)S(1)}, u32[]{:S(2)}, u32[]{:S(2)}) async-start(bf16[32,1,2,4096]{3,2,1,0:T(2,128)(2,1)} %copy.43), calls=%async_computation.2 | async-start | bytes 1048576 | tf_op jit(solution)/shard_map/all_to_all | solution.py:101
  73.1 0.0 copy-done.2
  73.2 11.7 %all-to-all-done.2 = bf16[32,1,2,4096]{3,2,1,0:T(2,128)(2,1)S(1)} async-done(((bf16[32,1,2,4096]{3,2,1,0:T(2,128)(2,1)}), bf16[32,1,2,4096]{3,2,1,0:T(2,128)(2,1)S(1)}, u32[]{:S(2)}, u32[]{:S(2)}) %all-to-all-start.2) | async-done | bytes 524320 | tf_op jit(solution)/shard_map/all_to_all | solution.py:101
  84.9 4.2 %fusion.26 = f32[32,1,2,768]{3,0,2,1:T(8,128)S(1)} fusion(bf16[1,4096,768]{2,1,0:T(8,128)(2,1)} %param.19, bf16[32,1,2,4096]{3,2,1,0:T(2,128)(2,1)S(1)} %all-to-all-done.2), kind=kOutput, calls=%fused_computation.21 | convolution fusion | flops 402653184 | bytes 7012352 | tf_op jit(solution)/shard_map/sjcd,jdf->sjcf/dot_general | solution.py:102
  89.0 7.5 %fusion.15 = bf16[32,1,2,4096]{3,0,2,1:T(8,128)(2,1)S(1)} fusion(bf16[1,768,4096]{2,1,0:T(8,128)(2,1)} %param.21, bf16[1,4096,768]{2,1,0:T(8,128)(2,1)} %param.20, bf16[32,1,2,4096]{3,2,1,0:T(2,128)(2,1)S(1)} %all-to-all-done.2, f32[32,1,2,768]{3,0,2,1:T(8,128)S(1)} %fusion.26), kind=kOutput, calls=%fused_computation.14 | convolution fusion | flops 805863424 | bytes 13828096 | tf_op jit(solution)/shard_map/sjcf,jfd->sjcd/dot_general | solution.py:107
  96.6 0.4 reshape.146
  97.0 1.3 %copy.45 = bf16[32,4,1,2,1024]{4,3,1,0,2:T(2,128)(2,1)} copy(bf16[32,4,1,2,1024]{4,1,0,3,2:T(4,128)(2,1)S(1)} %bitcast.123) | data formatting | bytes 1048576 | tf_op jit(solution)/shard_map/transpose | solution.py:113
  98.3 3.8 %all-to-all-start.3 = ((bf16[128,2,1024]{2,1,0:T(2,128)(2,1)}), bf16[128,2,1024]{2,1,0:T(2,128)(2,1)S(1)}, u32[]{:S(2)}, u32[]{:S(2)}) async-start(bf16[128,2,1024]{2,1,0:T(2,128)(2,1)} %bitcast.34), calls=%async_computation.3 | async-start | bytes 1048576 | tf_op jit(solution)/shard_map/all_to_all | solution.py:114
  102.1 0.1 copy.38
  102.2 0.1 select_reduce_fusion
  102.3 13.9 %all-to-all-done.3 = bf16[128,2,1024]{2,1,0:T(2,128)(2,1)S(1)} async-done(((bf16[128,2,1024]{2,1,0:T(2,128)(2,1)}), bf16[128,2,1024]{2,1,0:T(2,128)(2,1)S(1)}, u32[]{:S(2)}, u32[]{:S(2)}) %all-to-all-start.3) | async-done | bytes 524320 | tf_op jit(solution)/shard_map/all_to_all | solution.py:114
  116.2 1.0 fusion.45
  (13 shorter events, 0.2 us)
Async XLA Ops:
  5.5 13.0 %copy-start = (bf16[2048,128]{1,0:T(8,128)(2,1)S(1)}, bf16[2048,128]{1,0:T(8,128)(2,1)}, u32[]{:S(2)}) copy-start(bf16[2048,128]{1,0:T(8,128)(2,1)} %param.16) | copy-start | bytes 1572868
  5.5 14.0 %copy-start.3 = (s32[24,8]{0,1:T(8,128)S(1)}, s32[24,8]{0,1:T(8,128)}, u32[]{:S(2)}) copy-start(s32[24,8]{0,1:T(8,128)} %param.17) | copy-start | bytes 2308
  10.1 29.2 %all-to-all-start = ((bf16[16,24,2048]{2,1,0:T(8,128)(2,1)}), bf16[16,24,2048]{2,1,0:T(8,128)(2,1)S(1)}, u32[]{:S(2)}, u32[]{:S(2)}) async-start(bf16[16,24,2048]{2,1,0:T(8,128)(2,1)} %broadcast_in_dim.66), calls=%async_computation | async-start | bytes 3145728 | tf_op jit(solution)/shard_map/all_to_all | solution.py:71
  18.5 2.6 %collective-permute-start = (bf16[2048,128]{1,0:T(8,128)(2,1)S(1)}, bf16[2048,128]{1,0:T(8,128)(2,1)S(1)}, u32[]{:S(2)}, u32[]{:S(2)}) collective-permute-start(bf16[2048,128]{1,0:T(8,128)(2,1)S(1)} %copy-done), channel_id=1, source_target_pairs={{0,4},{4,0},{1,5},{5,1},{2,6},{6,2},{3,7},{7,3},{8,12},{12,8},{9,1... | collective-permute-start | bytes 1572872 | tf_op jit(solution)/shard_map/ppermute | solution.py:66
  39.2 25.0 %copy-start.1 = (bf16[24,4096]{1,0:T(8,128)(2,1)S(1)}, bf16[24,4096]{1,0:T(8,128)(2,1)}, u32[]{:S(2)}) copy-start(bf16[24,4096]{1,0:T(8,128)(2,1)} %param.11) | copy-start | bytes 589828
  40.9 32.2 %copy-start.2 = (f32[24,8]{0,1:T(8,128)S(1)}, f32[24,8]{0,1:T(8,128)}, u32[]{:S(2)}) copy-start(f32[24,8]{0,1:T(8,128)} %param.18) | copy-start | bytes 2308
  41.8 22.2 %all-to-all-start.1 = ((bf16[64,24,256]{2,1,0:T(8,128)(2,1)}), bf16[64,24,256]{2,1,0:T(8,128)(2,1)S(1)}, u32[]{:S(2)}, u32[]{:S(2)}) async-start(bf16[64,24,256]{2,1,0:T(8,128)(2,1)} %bitcast.3), calls=%async_computation.1 | async-start | bytes 1572864 | tf_op jit(solution)/shard_map/all_to_all | solution.py:78
  66.1 18.8 %all-to-all-start.2 = ((bf16[32,1,2,4096]{3,2,1,0:T(2,128)(2,1)}), bf16[32,1,2,4096]{3,2,1,0:T(2,128)(2,1)S(1)}, u32[]{:S(2)}, u32[]{:S(2)}) async-start(bf16[32,1,2,4096]{3,2,1,0:T(2,128)(2,1)} %copy.43), calls=%async_computation.2 | async-start | bytes 1048576 | tf_op jit(solution)/shard_map/all_to_all | solution.py:101
  98.3 17.9 %all-to-all-start.3 = ((bf16[128,2,1024]{2,1,0:T(2,128)(2,1)}), bf16[128,2,1024]{2,1,0:T(2,128)(2,1)S(1)}, u32[]{:S(2)}, u32[]{:S(2)}) async-start(bf16[128,2,1024]{2,1,0:T(2,128)(2,1)} %bitcast.34), calls=%async_computation.3 | async-start | bytes 1048576 | tf_op jit(solution)/shard_map/all_to_all | solution.py:114

commit v8 on v7

--- a/solution.py
+++ b/solution.py
@@ -4,6 +4,8 @@
 import jax.numpy as jnp
 import numpy as np
 from jax import lax
+from jax.experimental import pallas as pl
+from jax.experimental.pallas import tpu as pltpu
 from jax.sharding import Mesh, PartitionSpec as P
 
 CAP = 2
@@ -20,6 +22,52 @@
         resid_f * lax.rsqrt(jnp.mean(resid_f * resid_f, axis=-1, keepdims=True) + 1e-06)
     ).astype(jnp.bfloat16)
     return (residual, normed)
+
+
+def ffn_kernel(x_ref, wg_ref, wu_ref, wd_ref, o_ref, acc_ref):
+    step = pl.program_id(0)
+
+    @pl.when(step == 0)
+    def _():
+        acc_ref[...] = jnp.zeros_like(acc_ref)
+
+    wg = wg_ref[...]
+    wu = wu_ref[...]
+    wd = wd_ref[...]
+    for c in range(x_ref.shape[1]):
+        x = x_ref[:, c, :]
+        gate = jnp.dot(x, wg, preferred_element_type=jnp.float32)
+        up = jnp.dot(x, wu, preferred_element_type=jnp.float32)
+        activated = (gate / (1.0 + jnp.exp(-gate)) * up).astype(jnp.bfloat16)
+        acc_ref[:, c, :] += jnp.dot(activated, wd, preferred_element_type=jnp.float32)
+
+    @pl.when(step == pl.num_programs(0) - 1)
+    def _():
+        o_ref[...] = acc_ref[...].astype(o_ref.dtype)
+
+
+def expert_ffn(x, wg, wu, wd, chunk=256):
+    sources, slots, width = x.shape
+    ff = wg.shape[1]
+    return pl.pallas_call(
+        ffn_kernel,
+        grid=(ff // chunk,),
+        in_specs=[
+            pl.BlockSpec((sources, slots, width), lambda f: (0, 0, 0)),
+            pl.BlockSpec((width, chunk), lambda f: (0, f)),
+            pl.BlockSpec((width, chunk), lambda f: (0, f)),
+            pl.BlockSpec((chunk, width), lambda f: (f, 0)),
+        ],
+        out_specs=pl.BlockSpec((sources, slots, width), lambda f: (0, 0, 0)),
+        out_shape=jax.ShapeDtypeStruct((sources, slots, width), jnp.bfloat16),
+        scratch_shapes=[pltpu.VMEM((sources, slots, width), jnp.float32)],
+        compiler_params=pltpu.CompilerParams(vmem_limit_bytes=60 * 1024 * 1024),
+        cost_estimate=pl.CostEstimate(
+            flops=6 * sources * slots * width * ff,
+            transcendentals=sources * slots * ff,
+            bytes_accessed=2 * (3 * width * ff + 2 * sources * slots * width),
+        ),
+    )(x, wg, wu, wd)
 
 
 def local(
@@ -99,14 +147,10 @@
         "rmjc,rd->mjcd", hit_col.astype(jnp.bfloat16), normed, preferred_element_type=jnp.float32
     ).astype(jnp.bfloat16)
     arrived_slots = lax.all_to_all(outgoing, DP, 0, 0, tiled=True)
-    gate_proj = jnp.einsum(
-        "sjcd,jdf->sjcf", arrived_slots, w_gate, preferred_element_type=jnp.float32
-    )
-    up_proj = jnp.einsum("sjcd,jdf->sjcf", arrived_slots, w_up, preferred_element_type=jnp.float32)
-    activated = (jax.nn.silu(gate_proj) * up_proj).astype(jnp.bfloat16)
-    expert_out = jnp.einsum(
-        "sjcf,jfd->sjcd", activated, w_down, preferred_element_type=jnp.float32
-    ).astype(jnp.bfloat16)
+    assert exp_dev == 1
+    expert_out = expert_ffn(
+        arrived_slots.reshape(dp_count, CAP, model_width), w_gate[0], w_up[0], w_down[0]
+    ).reshape(dp_count, exp_dev, CAP, model_width)
 
     width_share = model_width // tp_count
     back = expert_out.reshape(dp_count, exp_dev, CAP, tp_count, width_share)

time: 118 us -> 121 us (1.025)
  Pallas kernels: 0 us -> 13.3 us
  matrix products: 21.8 us -> 10 us
  local copies, waits for them, and re-layouts: 6.84 us -> 8.61 us
    pallas_call x0 -> x1, Pallas kernels: none -> 13.3 us  [expert_ffn(): pl.pallas_call(ffn_kernel, grid=(ff // chunk,), in_specs=[pl.BlockSpec((s...]
    dot_general x2 -> x0, matrix products: 11.7 us -> none  [the longest x1 7.55 us: local(): jnp.einsum('sjcf,jfd->sjcd', activated, w_down, preferred_element_type=jn...]
    another operation x0 -> x1, local copies, waits for them, and re-layouts: none -> 1.37 us  [local(): back = expert_out.reshape(dp_count, exp_dev, CAP, tp_count, width_share)]
  transfers between devices with their start and end apart: 5 -> 5, of which waited for: 5 -> 5; matrix products, arithmetic and copies ran while one was open for 2% -> 1% of each run, Pallas kernels for 0% -> 0%
where the time goes in v8:
time: 121 us
  waiting for transfers between devices  57 us (47%)
  starting transfers between devices  29.3 us (24%)
  Pallas kernels  13.3 us (11%)
  matrix products  10 us (8%)
  local copies, waits for them, and re-layouts  8.61 us (7%)
  other arithmetic  2.27 us (2%)
    all_to_all x1, waiting for transfers between devices, local(): mine = lax.all_to_all(sent, ('x', 'z'), 0, 0, tiled=True)  17.3 us
    all_to_all x1, waiting for transfers between devices, local(): results = lax.all_to_all(back, ALL, 0, 0, tiled=True)  13.9 us
    pallas_call x1, Pallas kernels, expert_ffn(): pl.pallas_call(ffn_kernel, grid=(ff // chunk,), in_specs=[pl.BlockSpec((s...  13.3 us
    all_to_all x1, waiting for transfers between devices, local(): lax.all_to_all(sent.reshape(n_xz * tp_count, rows_dev, pair_cols), ('x',...  12.7 us
    all_to_all x1, waiting for transfers between devices, local(): arrived_slots = lax.all_to_all(outgoing, DP, 0, 0, tiled=True)  11.7 us
    all_to_all x1, starting transfers between devices, local(): lax.all_to_all(sent.reshape(n_xz * tp_count, rows_dev, pair_cols), ('x',...  8.83 us
    all_to_all x1, starting transfers between devices, local(): mine = lax.all_to_all(sent, ('x', 'z'), 0, 0, tiled=True)  8.55 us
    all_to_all x1, starting transfers between devices, local(): arrived_slots = lax.all_to_all(outgoing, DP, 0, 0, tiled=True)  7.04 us
  transfers between devices with their start and end apart: 5, of which 5 were waited for; matrix products, arithmetic and copies ran while one was open for 1% of the time, Pallas kernels for 0%

profile of v8, /device:TPU:1, one launch (start us, length us, event | category | flops | bytes accessed | tf_op | source)
XLA Modules:
  0.0 120.6 jit_solution(5879659928197756859)
XLA Ops:
  0.0 0.9 copy.50
  0.9 0.7 iota_compare_fusion.1
  1.7 3.9 %fusion.42 = (f32[24,16]{1,0:T(8,128)S(1)}, f32[24,16,768]{2,1,0:T(8,128)S(1)}) fusion(bf16[24,16,128]{2,1,0:T(8,128)(2,1)S(1)} %bitcast.68, bf16[24,1,768,128]{3,2,1,0:T(8,128)(2,1)} %param.13, pred[24,768]{1,0:T(8,128)(4,1)S(1)} %iota_compare_fusion.1), kind=kOutput, calls=%fused_computation.58 | convolution fusion | flops 76677888 | bytes 6016512 | tf_op jit(solution)/shard_map/sub | solution.py:107
  5.5 3.1 %fusion.14 = bf16[24,16,128]{2,1,0:T(8,128)(2,1)S(1)} fusion(bf16[24,1,768,128]{3,2,1,0:T(8,128)(2,1)} %param.14, f32[24,16,768]{2,1,0:T(8,128)S(1)} %get-tuple-element.10, f32[24,16]{1,0:T(8,128)S(1)} %get-tuple-element.9), kind=kOutput, calls=%fused_computation.13 | convolution fusion | flops 76136448 | bytes 5998080 | tf_op jit(solution)/shard_map/rhgl,rhld->rhgd/dot_general | solution.py:109
  8.7 1.3 %broadcast_in_dim.66 = bf16[16,24,2048]{2,1,0:T(8,128)(2,1)} broadcast(bf16[24,2048]{1,0:T(8,128)(2,1)S(1)} %bitcast.67), dimensions={1,2} | broadcast | bytes 1671168 | tf_op jit(solution)/shard_map/broadcast_in_dim | solution.py:118
  10.0 0.0 copy-start.1
  10.0 0.0 copy-start.4
  10.0 8.5 %all-to-all-start = ((bf16[16,24,2048]{2,1,0:T(8,128)(2,1)}), bf16[16,24,2048]{2,1,0:T(8,128)(2,1)S(1)}, u32[]{:S(2)}, u32[]{:S(2)}) async-start(bf16[16,24,2048]{2,1,0:T(8,128)(2,1)} %broadcast_in_dim.66), calls=%async_computation | async-start | bytes 3145728 | tf_op jit(solution)/shard_map/all_to_all | solution.py:119
  18.6 0.0 copy-done.1
  18.6 1.0 collective-permute-start
  19.6 0.0 copy-done.4
  19.6 0.1 copy.39
  19.7 1.5 %collective-permute-done = bf16[2048,128]{1,0:T(8,128)(2,1)S(1)} collective-permute-done((bf16[2048,128]{1,0:T(8,128)(2,1)S(1)}, bf16[2048,128]{1,0:T(8,128)(2,1)S(1)}, u32[]{:S(2)}, u32[]{:S(2)}) %collective-permute-start) | collective-permute-done | bytes 524320 | tf_op jit(solution)/shard_map/ppermute | solution.py:114
  21.2 0.9 broadcast_select_fusion.1
  22.1 17.3 %all-to-all-done = bf16[16,24,2048]{2,1,0:T(8,128)(2,1)S(1)} async-done(((bf16[16,24,2048]{2,1,0:T(8,128)(2,1)}), bf16[16,24,2048]{2,1,0:T(8,128)(2,1)S(1)}, u32[]{:S(2)}, u32[]{:S(2)}) %all-to-all-start) | async-done | bytes 1572896 | tf_op jit(solution)/shard_map/all_to_all | solution.py:119
  39.3 1.7 %convolution_convert_fusion.1 = bf16[16,24,256]{2,1,0:T(8,128)(2,1)S(1)} fusion(bf16[16,24,2048]{2,1,0:T(8,128)(2,1)S(1)} %all-to-all-done, bf16[2048,128]{1,0:T(8,128)(2,1)} %get-tuple-element.8, bf16[2048,128]{1,0:T(8,128)(2,1)S(1)} %get-tuple-element.7), kind=kOutput, calls=%fused_computation.12 | convolution fusion | flops 404848640 | bytes 2818048 | tf_op jit(solution)/shard_map/ird,dc->irc/dot_general | solution.py:120
  41.0 0.9 broadcast_in_dim.67
  41.9 8.8 %all-to-all-start.1 = ((bf16[64,24,256]{2,1,0:T(8,128)(2,1)}), bf16[64,24,256]{2,1,0:T(8,128)(2,1)S(1)}, u32[]{:S(2)}, u32[]{:S(2)}) async-start(bf16[64,24,256]{2,1,0:T(8,128)(2,1)} %bitcast.3), calls=%async_computation.1 | async-start | bytes 1572864 | tf_op jit(solution)/shard_map/all_to_all | solution.py:126
  50.8 0.0 copy-start.2
  50.8 0.1 convert_reduce_fusion
  50.9 0.1 copy.43
  51.0 0.1 copy.42
  51.1 0.1 copy.44
  51.3 0.1 copy.45
  51.4 12.7 %all-to-all-done.1 = bf16[64,24,256]{2,1,0:T(8,128)(2,1)S(1)} async-done(((bf16[64,24,256]{2,1,0:T(8,128)(2,1)}), bf16[64,24,256]{2,1,0:T(8,128)(2,1)S(1)}, u32[]{:S(2)}, u32[]{:S(2)}) %all-to-all-start.1) | async-done | bytes 786464 | tf_op jit(solution)/shard_map/all_to_all | solution.py:126
  64.1 0.1 bitcast_reduce_fusion
  64.3 0.0 copy-done.2
  64.3 0.2 fusion.23
  64.5 0.0 copy-start.3
  64.5 0.4 fusion.5
  64.8 1.3 %copy.46 = bf16[32,1,2,4096]{3,2,1,0:T(2,128)(2,1)} copy(bf16[32,1,2,4096]{3,0,2,1:T(8,128)(2,1)S(1)} %fusion.5) | data formatting | bytes 1048576 | tf_op jit(solution)/shard_map/convert_element_type | solution.py:148
  66.2 7.0 %all-to-all-start.2 = ((bf16[32,1,2,4096]{3,2,1,0:T(2,128)(2,1)}), bf16[32,1,2,4096]{3,2,1,0:T(2,128)(2,1)S(1)}, u32[]{:S(2)}, u32[]{:S(2)}) async-start(bf16[32,1,2,4096]{3,2,1,0:T(2,128)(2,1)} %copy.46), calls=%async_computation.2 | async-start | bytes 1048576 | tf_op jit(solution)/shard_map/all_to_all | solution.py:149
  73.2 0.0 copy-done.3
  73.3 11.7 %all-to-all-done.2 = bf16[32,1,2,4096]{3,2,1,0:T(2,128)(2,1)S(1)} async-done(((bf16[32,1,2,4096]{3,2,1,0:T(2,128)(2,1)}), bf16[32,1,2,4096]{3,2,1,0:T(2,128)(2,1)S(1)}, u32[]{:S(2)}, u32[]{:S(2)}) %all-to-all-start.2) | async-done | bytes 524320 | tf_op jit(solution)/shard_map/all_to_all | solution.py:149
  84.9 0.0 copy-start
  84.9 0.8 copy-done
  85.7 13.3 %shard_map.109 = bf16[32,2,4096]{2,1,0:T(2,128)(2,1)} custom-call(bf16[32,2,4096]{2,1,0:T(2,128)(2,1)} %bitcast.62, bf16[4096,768]{1,0:T(8,128)(2,1)} %bitcast.59, bf16[4096,768]{1,0:T(8,128)(2,1)} %bitcast.60, bf16[768,4096]{1,0:T(8,128)(2,1)} %bitcast.61), custom_call_target="tpu_custom_call" | custom-call | flops 1207959552 | bytes 19922944 | tf_op jit(solution)/shard_map/pallas_call | solution.py:52
  99.0 1.4 %reshape_reshape.3 = bf16[32,1,2,4,1024]{4,3,2,0,1:T(4,128)(2,1)S(1)} reshape(bf16[32,2,4096]{2,1,0:T(2,128)(2,1)} %shard_map.109) | data formatting | bytes 1048576 | tf_op jit(solution)/shard_map/reshape;reshape | solution.py:156
  100.4 1.3 %copy.47 = bf16[32,4,1,2,1024]{4,3,1,0,2:T(2,128)(2,1)} copy(bf16[32,4,1,2,1024]{4,1,3,0,2:T(4,128)(2,1)S(1)} %bitcast.63) | data formatting | bytes 1048576 | tf_op jit(solution)/shard_map/transpose | solution.py:157
  101.7 3.8 %all-to-all-start.3 = ((bf16[128,2,1024]{2,1,0:T(2,128)(2,1)}), bf16[128,2,1024]{2,1,0:T(2,128)(2,1)S(1)}, u32[]{:S(2)}, u32[]{:S(2)}) async-start(bf16[128,2,1024]{2,1,0:T(2,128)(2,1)} %bitcast.19), calls=%async_computation.3 | async-start | bytes 1048576 | tf_op jit(solution)/shard_map/all_to_all | solution.py:158
  105.5 0.1 copy.41
  105.6 0.1 select_reduce_fusion
  105.7 13.9 %all-to-all-done.3 = bf16[128,2,1024]{2,1,0:T(2,128)(2,1)S(1)} async-done(((bf16[128,2,1024]{2,1,0:T(2,128)(2,1)}), bf16[128,2,1024]{2,1,0:T(2,128)(2,1)S(1)}, u32[]{:S(2)}, u32[]{:S(2)}) %all-to-all-start.3) | async-done | bytes 524320 | tf_op jit(solution)/shard_map/all_to_all | solution.py:158
  119.6 1.0 fusion.18
  (13 shorter events, 0.2 us)
Async XLA Ops:
  10.0 8.6 %copy-start.1 = (bf16[2048,128]{1,0:T(8,128)(2,1)S(1)}, bf16[2048,128]{1,0:T(8,128)(2,1)}, u32[]{:S(2)}) copy-start(bf16[2048,128]{1,0:T(8,128)(2,1)} %param.16) | copy-start | bytes 1572868
  10.0 9.6 %copy-start.4 = (s32[24,8]{0,1:T(8,128)S(1)}, s32[24,8]{0,1:T(8,128)}, u32[]{:S(2)}) copy-start(s32[24,8]{0,1:T(8,128)} %param.17) | copy-start | bytes 2308
  10.0 29.3 %all-to-all-start = ((bf16[16,24,2048]{2,1,0:T(8,128)(2,1)}), bf16[16,24,2048]{2,1,0:T(8,128)(2,1)S(1)}, u32[]{:S(2)}, u32[]{:S(2)}) async-start(bf16[16,24,2048]{2,1,0:T(8,128)(2,1)} %broadcast_in_dim.66), calls=%async_computation | async-start | bytes 3145728 | tf_op jit(solution)/shard_map/all_to_all | solution.py:119
  18.6 2.6 %collective-permute-start = (bf16[2048,128]{1,0:T(8,128)(2,1)S(1)}, bf16[2048,128]{1,0:T(8,128)(2,1)S(1)}, u32[]{:S(2)}, u32[]{:S(2)}) collective-permute-start(bf16[2048,128]{1,0:T(8,128)(2,1)S(1)} %copy-done.1), channel_id=1, source_target_pairs={{0,4},{4,0},{1,5},{5,1},{2,6},{6,2},{3,7},{7,3},{8,12},{12,8},{9,1... | collective-permute-start | bytes 1572872 | tf_op jit(solution)/shard_map/ppermute | solution.py:114
  41.9 22.2 %all-to-all-start.1 = ((bf16[64,24,256]{2,1,0:T(8,128)(2,1)}), bf16[64,24,256]{2,1,0:T(8,128)(2,1)S(1)}, u32[]{:S(2)}, u32[]{:S(2)}) async-start(bf16[64,24,256]{2,1,0:T(8,128)(2,1)} %bitcast.3), calls=%async_computation.1 | async-start | bytes 1572864 | tf_op jit(solution)/shard_map/all_to_all | solution.py:126
  50.8 13.5 %copy-start.2 = (bf16[24,4096]{1,0:T(8,128)(2,1)S(1)}, bf16[24,4096]{1,0:T(8,128)(2,1)}, u32[]{:S(2)}) copy-start(bf16[24,4096]{1,0:T(8,128)(2,1)} %param.11) | copy-start | bytes 589828
  64.5 8.8 %copy-start.3 = (f32[24,8]{0,1:T(8,128)S(1)}, f32[24,8]{0,1:T(8,128)}, u32[]{:S(2)}) copy-start(f32[24,8]{0,1:T(8,128)} %param.18) | copy-start | bytes 2308
  66.2 18.8 %all-to-all-start.2 = ((bf16[32,1,2,4096]{3,2,1,0:T(2,128)(2,1)}), bf16[32,1,2,4096]{3,2,1,0:T(2,128)(2,1)S(1)}, u32[]{:S(2)}, u32[]{:S(2)}) async-start(bf16[32,1,2,4096]{3,2,1,0:T(2,128)(2,1)} %copy.46), calls=%async_computation.2 | async-start | bytes 1048576 | tf_op jit(solution)/shard_map/all_to_all | solution.py:149
  84.9 0.8 copy-start
  101.7 17.9 %all-to-all-start.3 = ((bf16[128,2,1024]{2,1,0:T(2,128)(2,1)}), bf16[128,2,1024]{2,1,0:T(2,128)(2,1)S(1)}, u32[]{:S(2)}, u32[]{:S(2)}) async-start(bf16[128,2,1024]{2,1,0:T(2,128)(2,1)} %bitcast.19), calls=%async_computation.3 | async-start | bytes 1048576 | tf_op jit(solution)/shard_map/all_to_all | solution.py:158

commit v9 on v8

--- a/solution.py
+++ b/solution.py
@@ -24,31 +24,34 @@
     return (residual, normed)
 
 
-def ffn_kernel(x_ref, wg_ref, wu_ref, wd_ref, o_ref, acc_ref):
+def ffn_kernel(x_ref, wg_ref, wu_ref, wd_ref, o_ref, acc_ref, out_ref):
     step = pl.program_id(0)
+    sources, slots, _ = x_ref.shape
+    parts = o_ref.shape[1]
+    share = o_ref.shape[3]
 
     @pl.when(step == 0)
     def _():
         acc_ref[...] = jnp.zeros_like(acc_ref)
 
-    wg = wg_ref[...]
-    wu = wu_ref[...]
-    wd = wd_ref[...]
-    for c in range(x_ref.shape[1]):
-        x = x_ref[:, c, :]
-        gate = jnp.dot(x, wg, preferred_element_type=jnp.float32)
-        up = jnp.dot(x, wu, preferred_element_type=jnp.float32)
-        activated = (gate / (1.0 + jnp.exp(-gate)) * up).astype(jnp.bfloat16)
-        acc_ref[:, c, :] += jnp.dot(activated, wd, preferred_element_type=jnp.float32)
+    x = jnp.concatenate([x_ref[:, c, :] for c in range(slots)], axis=0)
+    gate = jnp.dot(x, wg_ref[...], preferred_element_type=jnp.float32)
+    up = jnp.dot(x, wu_ref[...], preferred_element_type=jnp.float32)
+    activated = (gate / (1.0 + jnp.exp(-gate)) * up).astype(jnp.bfloat16)
+    acc_ref[...] += jnp.dot(activated, wd_ref[...], preferred_element_type=jnp.float32)
 
     @pl.when(step == pl.num_programs(0) - 1)
     def _():
-        o_ref[...] = acc_ref[...].astype(o_ref.dtype)
-
-
-def expert_ffn(x, wg, wu, wd, chunk=256):
+        for t in range(parts):
+            for c in range(slots):
+                out_ref[:, t, c, :] = acc_ref[c * sources : (c + 1) * sources, t * share : (t + 1) * share]
+        o_ref[...] = out_ref[...].astype(o_ref.dtype)
+
+
+def expert_ffn(x, wg, wu, wd, parts, chunk=256):
     sources, slots, width = x.shape
     ff = wg.shape[1]
+    share = width // parts
     return pl.pallas_call(
         ffn_kernel,
         grid=(ff // chunk,),
@@ -58,9 +61,12 @@
             pl.BlockSpec((width, chunk), lambda f: (0, f)),
             pl.BlockSpec((chunk, width), lambda f: (f, 0)),
         ],
-        out_specs=pl.BlockSpec((sources, slots, width), lambda f: (0, 0, 0)),
-        out_shape=jax.ShapeDtypeStruct((sources, slots, width), jnp.bfloat16),
-        scratch_shapes=[pltpu.VMEM((sources, slots, width), jnp.float32)],
+        out_specs=pl.BlockSpec((sources, parts, slots, share), lambda f: (0, 0, 0, 0)),
+        out_shape=jax.ShapeDtypeStruct((sources, parts, slots, share), jnp.bfloat16),
+        scratch_shapes=[
+            pltpu.VMEM((slots * sources, width), jnp.float32),
+            pltpu.VMEM((sources, parts, slots, share), jnp.float32),
+        ],
         compiler_params=pltpu.CompilerParams(vmem_limit_bytes=60 * 1024 * 1024),
         cost_estimate=pl.CostEstimate(
             flops=6 * sources * slots * width * ff,
@@ -148,13 +154,11 @@
     ).astype(jnp.bfloat16)
     arrived_slots = lax.all_to_all(outgoing, DP, 0, 0, tiled=True)
     assert exp_dev == 1
-    expert_out = expert_ffn(
-        arrived_slots.reshape(dp_count, CAP, model_width), w_gate[0], w_up[0], w_down[0]
-    ).reshape(dp_count, exp_dev, CAP, model_width)
-
     width_share = model_width // tp_count
-    back = expert_out.reshape(dp_count, exp_dev, CAP, tp_count, width_share)
-    back = back.transpose(0, 3, 1, 2, 4).reshape(n_all, exp_dev * CAP, width_share)
+    back = expert_ffn(
+        arrived_slots.reshape(dp_count, CAP, model_width), w_gate[0], w_up[0], w_down[0], tp_count
+    ).reshape(n_all, exp_dev * CAP, width_share)
+
     results = lax.all_to_all(back, ALL, 0, 0, tiled=True)
     combine_table = jnp.where(slot_hit, all_weight[:, :, None], 0.0)
     mixture = jnp.einsum(

time: 121 us -> 117 us (0.967)
  local copies, waits for them, and re-layouts: 8.61 us -> 5.93 us
  Pallas kernels: 13.3 us -> 11.6 us
    pallas_call x1, Pallas kernels: 13.3 us -> 11.6 us  [expert_ffn(): pl.pallas_call(ffn_kernel, grid=(ff // chunk,), in_specs=[pl.BlockSpec((s...]
    another operation x1 -> x0, local copies, waits for them, and re-layouts: 1.37 us -> none  [local(): back = expert_out.reshape(dp_count, exp_dev, CAP, tp_count, width_share)]
    transpose x1 -> x0, local copies, waits for them, and re-layouts: 1.31 us -> none  [local(): back.transpose(0, 3, 1, 2, 4).reshape(n_all, exp_dev * CAP, width_share)]
  transfers between devices with their start and end apart: 5 -> 5, of which waited for: 5 -> 5; matrix products, arithmetic and copies ran while one was open for 1% -> 2% of each run, Pallas kernels for 0% -> 0%
where the time goes in v9:
time: 117 us; the launch traced here: 116 us
  waiting for transfers between devices  57 us (49%)
  starting transfers between devices  29.3 us (25%)
  Pallas kernels  11.6 us (10%)
  matrix products  10 us (9%)
  local copies, waits for them, and re-layouts  5.93 us (5%)
  other arithmetic  2.27 us (2%)
    all_to_all x1, waiting for transfers between devices, local(): mine = lax.all_to_all(sent, ('x', 'z'), 0, 0, tiled=True)  17.3 us
    all_to_all x1, waiting for transfers between devices, local(): results = lax.all_to_all(back, ALL, 0, 0, tiled=True)  13.9 us
    all_to_all x1, waiting for transfers between devices, local(): lax.all_to_all(sent.reshape(n_xz * tp_count, rows_dev, pair_cols), ('x',...  12.7 us
    all_to_all x1, waiting for transfers between devices, local(): arrived_slots = lax.all_to_all(outgoing, DP, 0, 0, tiled=True)  11.7 us
    pallas_call x1, Pallas kernels, expert_ffn(): pl.pallas_call(ffn_kernel, grid=(ff // chunk,), in_specs=[pl.BlockSpec((s...  11.6 us
    all_to_all x1, starting transfers between devices, local(): lax.all_to_all(sent.reshape(n_xz * tp_count, rows_dev, pair_cols), ('x',...  8.83 us
    all_to_all x1, starting transfers between devices, local(): mine = lax.all_to_all(sent, ('x', 'z'), 0, 0, tiled=True)  8.55 us
    all_to_all x1, starting transfers between devices, local(): arrived_slots = lax.all_to_all(outgoing, DP, 0, 0, tiled=True)  7.04 us
  transfers between devices with their start and end apart: 5, of which 5 were waited for; matrix products, arithmetic and copies ran while one was open for 2% of the time, Pallas kernels for 0%

profile of v9, /device:TPU:1, one launch (start us, length us, event | category | flops | bytes accessed | tf_op | source)
XLA Modules:
  0.0 116.3 jit_solution(3326259193994059368)
XLA Ops:
  0.0 0.9 copy.48
  0.9 0.7 iota_compare_fusion.1
  1.7 3.8 %fusion.42 = (f32[24,16]{1,0:T(8,128)S(1)}, f32[24,16,768]{2,1,0:T(8,128)S(1)}) fusion(bf16[24,16,128]{2,1,0:T(8,128)(2,1)S(1)} %bitcast.67, bf16[24,1,768,128]{3,2,1,0:T(8,128)(2,1)} %param.13, pred[24,768]{1,0:T(8,128)(4,1)S(1)} %iota_compare_fusion.1), kind=kOutput, calls=%fused_computation.58 | convolution fusion | flops 76677888 | bytes 6016512 | tf_op jit(solution)/shard_map/sub | solution.py:113
  5.5 3.2 %fusion.14 = bf16[24,16,128]{2,1,0:T(8,128)(2,1)S(1)} fusion(bf16[24,1,768,128]{3,2,1,0:T(8,128)(2,1)} %param.14, f32[24,16,768]{2,1,0:T(8,128)S(1)} %get-tuple-element.10, f32[24,16]{1,0:T(8,128)S(1)} %get-tuple-element.9), kind=kOutput, calls=%fused_computation.13 | convolution fusion | flops 76136448 | bytes 5998080 | tf_op jit(solution)/shard_map/rhgl,rhld->rhgd/dot_general | solution.py:115
  8.7 1.3 %broadcast_in_dim.66 = bf16[16,24,2048]{2,1,0:T(8,128)(2,1)} broadcast(bf16[24,2048]{1,0:T(8,128)(2,1)S(1)} %bitcast.66), dimensions={1,2} | broadcast | bytes 1671168 | tf_op jit(solution)/shard_map/broadcast_in_dim | solution.py:124
  10.0 0.0 copy-start.1
  10.0 0.0 copy-start.4
  10.0 8.5 %all-to-all-start = ((bf16[16,24,2048]{2,1,0:T(8,128)(2,1)}), bf16[16,24,2048]{2,1,0:T(8,128)(2,1)S(1)}, u32[]{:S(2)}, u32[]{:S(2)}) async-start(bf16[16,24,2048]{2,1,0:T(8,128)(2,1)} %broadcast_in_dim.66), calls=%async_computation | async-start | bytes 3145728 | tf_op jit(solution)/shard_map/all_to_all | solution.py:125
  18.6 0.0 copy-done.1
  18.6 1.0 collective-permute-start
  19.6 0.0 copy-done.4
  19.6 0.1 copy.38
  19.7 1.5 %collective-permute-done = bf16[2048,128]{1,0:T(8,128)(2,1)S(1)} collective-permute-done((bf16[2048,128]{1,0:T(8,128)(2,1)S(1)}, bf16[2048,128]{1,0:T(8,128)(2,1)S(1)}, u32[]{:S(2)}, u32[]{:S(2)}) %collective-permute-start) | collective-permute-done | bytes 524320 | tf_op jit(solution)/shard_map/ppermute | solution.py:120
  21.2 0.9 broadcast_select_fusion.1
  22.1 17.3 %all-to-all-done = bf16[16,24,2048]{2,1,0:T(8,128)(2,1)S(1)} async-done(((bf16[16,24,2048]{2,1,0:T(8,128)(2,1)}), bf16[16,24,2048]{2,1,0:T(8,128)(2,1)S(1)}, u32[]{:S(2)}, u32[]{:S(2)}) %all-to-all-start) | async-done | bytes 1572896 | tf_op jit(solution)/shard_map/all_to_all | solution.py:125
  39.3 1.7 %convolution_convert_fusion.1 = bf16[16,24,256]{2,1,0:T(8,128)(2,1)S(1)} fusion(bf16[16,24,2048]{2,1,0:T(8,128)(2,1)S(1)} %all-to-all-done, bf16[2048,128]{1,0:T(8,128)(2,1)} %get-tuple-element.8, bf16[2048,128]{1,0:T(8,128)(2,1)S(1)} %get-tuple-element.7), kind=kOutput, calls=%fused_computation.12 | convolution fusion | flops 404848640 | bytes 2818048 | tf_op jit(solution)/shard_map/ird,dc->irc/dot_general | solution.py:126
  41.0 0.9 broadcast_in_dim.67
  41.9 8.8 %all-to-all-start.1 = ((bf16[64,24,256]{2,1,0:T(8,128)(2,1)}), bf16[64,24,256]{2,1,0:T(8,128)(2,1)S(1)}, u32[]{:S(2)}, u32[]{:S(2)}) async-start(bf16[64,24,256]{2,1,0:T(8,128)(2,1)} %bitcast.3), calls=%async_computation.1 | async-start | bytes 1572864 | tf_op jit(solution)/shard_map/all_to_all | solution.py:132
  50.8 0.0 copy-start.2
  50.8 0.1 convert_reduce_fusion
  50.9 0.1 copy.42
  51.0 0.1 copy.41
  51.1 0.1 copy.43
  51.3 0.1 copy.44
  51.4 12.7 %all-to-all-done.1 = bf16[64,24,256]{2,1,0:T(8,128)(2,1)S(1)} async-done(((bf16[64,24,256]{2,1,0:T(8,128)(2,1)}), bf16[64,24,256]{2,1,0:T(8,128)(2,1)S(1)}, u32[]{:S(2)}, u32[]{:S(2)}) %all-to-all-start.1) | async-done | bytes 786464 | tf_op jit(solution)/shard_map/all_to_all | solution.py:132
  64.1 0.1 bitcast_reduce_fusion
  64.3 0.0 copy-done.2
  64.3 0.2 fusion.23
  64.5 0.0 copy-start.3
  64.5 0.4 fusion.5
  64.8 1.3 %copy.45 = bf16[32,1,2,4096]{3,2,1,0:T(2,128)(2,1)} copy(bf16[32,1,2,4096]{3,0,2,1:T(8,128)(2,1)S(1)} %fusion.5) | data formatting | bytes 1048576 | tf_op jit(solution)/shard_map/convert_element_type | solution.py:154
  66.2 7.0 %all-to-all-start.2 = ((bf16[32,1,2,4096]{3,2,1,0:T(2,128)(2,1)}), bf16[32,1,2,4096]{3,2,1,0:T(2,128)(2,1)S(1)}, u32[]{:S(2)}, u32[]{:S(2)}) async-start(bf16[32,1,2,4096]{3,2,1,0:T(2,128)(2,1)} %copy.45), calls=%async_computation.2 | async-start | bytes 1048576 | tf_op jit(solution)/shard_map/all_to_all | solution.py:155
  73.2 0.0 copy-done.3
  73.3 11.7 %all-to-all-done.2 = bf16[32,1,2,4096]{3,2,1,0:T(2,128)(2,1)S(1)} async-done(((bf16[32,1,2,4096]{3,2,1,0:T(2,128)(2,1)}), bf16[32,1,2,4096]{3,2,1,0:T(2,128)(2,1)S(1)}, u32[]{:S(2)}, u32[]{:S(2)}) %all-to-all-start.2) | async-done | bytes 524320 | tf_op jit(solution)/shard_map/all_to_all | solution.py:155
  84.9 0.0 copy-start
  84.9 0.8 copy-done
  85.7 11.6 %shard_map.109 = bf16[32,4,2,1024]{3,2,1,0:T(2,128)(2,1)} custom-call(bf16[32,2,4096]{2,1,0:T(2,128)(2,1)} %bitcast.62, bf16[4096,768]{1,0:T(8,128)(2,1)} %bitcast.58, bf16[4096,768]{1,0:T(8,128)(2,1)} %bitcast.59, bf16[768,4096]{1,0:T(8,128)(2,1)} %bitcast.60), custom_call_target="tpu_custom_call" | custom-call | flops 1207959552 | bytes 19922944 | tf_op jit(solution)/shard_map/pallas_call | solution.py:55
  97.3 3.8 %all-to-all-start.3 = ((bf16[128,2,1024]{2,1,0:T(2,128)(2,1)}), bf16[128,2,1024]{2,1,0:T(2,128)(2,1)S(1)}, u32[]{:S(2)}, u32[]{:S(2)}) async-start(bf16[128,2,1024]{2,1,0:T(2,128)(2,1)} %bitcast.61), calls=%async_computation.3 | async-start | bytes 1048576 | tf_op jit(solution)/shard_map/all_to_all | solution.py:162
  101.2 0.1 copy.40
  101.3 0.1 select_reduce_fusion
  101.4 13.9 %all-to-all-done.3 = bf16[128,2,1024]{2,1,0:T(2,128)(2,1)S(1)} async-done(((bf16[128,2,1024]{2,1,0:T(2,128)(2,1)}), bf16[128,2,1024]{2,1,0:T(2,128)(2,1)S(1)}, u32[]{:S(2)}, u32[]{:S(2)}) %all-to-all-start.3) | async-done | bytes 524320 | tf_op jit(solution)/shard_map/all_to_all | solution.py:162
  115.3 1.0 fusion.18
  (13 shorter events, 0.2 us)
Async XLA Ops:
  10.0 8.6 %copy-start.1 = (bf16[2048,128]{1,0:T(8,128)(2,1)S(1)}, bf16[2048,128]{1,0:T(8,128)(2,1)}, u32[]{:S(2)}) copy-start(bf16[2048,128]{1,0:T(8,128)(2,1)} %param.16) | copy-start | bytes 1572868
  10.0 9.6 %copy-start.4 = (s32[24,8]{0,1:T(8,128)S(1)}, s32[24,8]{0,1:T(8,128)}, u32[]{:S(2)}) copy-start(s32[24,8]{0,1:T(8,128)} %param.17) | copy-start | bytes 2308
  10.0 29.3 %all-to-all-start = ((bf16[16,24,2048]{2,1,0:T(8,128)(2,1)}), bf16[16,24,2048]{2,1,0:T(8,128)(2,1)S(1)}, u32[]{:S(2)}, u32[]{:S(2)}) async-start(bf16[16,24,2048]{2,1,0:T(8,128)(2,1)} %broadcast_in_dim.66), calls=%async_computation | async-start | bytes 3145728 | tf_op jit(solution)/shard_map/all_to_all | solution.py:125
  18.6 2.6 %collective-permute-start = (bf16[2048,128]{1,0:T(8,128)(2,1)S(1)}, bf16[2048,128]{1,0:T(8,128)(2,1)S(1)}, u32[]{:S(2)}, u32[]{:S(2)}) collective-permute-start(bf16[2048,128]{1,0:T(8,128)(2,1)S(1)} %copy-done.1), channel_id=1, source_target_pairs={{0,4},{4,0},{1,5},{5,1},{2,6},{6,2},{3,7},{7,3},{8,12},{12,8},{9,1... | collective-permute-start | bytes 1572872 | tf_op jit(solution)/shard_map/ppermute | solution.py:120
  41.9 22.2 %all-to-all-start.1 = ((bf16[64,24,256]{2,1,0:T(8,128)(2,1)}), bf16[64,24,256]{2,1,0:T(8,128)(2,1)S(1)}, u32[]{:S(2)}, u32[]{:S(2)}) async-start(bf16[64,24,256]{2,1,0:T(8,128)(2,1)} %bitcast.3), calls=%async_computation.1 | async-start | bytes 1572864 | tf_op jit(solution)/shard_map/all_to_all | solution.py:132
  50.8 13.5 %copy-start.2 = (bf16[24,4096]{1,0:T(8,128)(2,1)S(1)}, bf16[24,4096]{1,0:T(8,128)(2,1)}, u32[]{:S(2)}) copy-start(bf16[24,4096]{1,0:T(8,128)(2,1)} %param.11) | copy-start | bytes 589828
  64.5 8.8 %copy-start.3 = (f32[24,8]{0,1:T(8,128)S(1)}, f32[24,8]{0,1:T(8,128)}, u32[]{:S(2)}) copy-start(f32[24,8]{0,1:T(8,128)} %param.18) | copy-start | bytes 2308
  66.2 18.8 %all-to-all-start.2 = ((bf16[32,1,2,4096]{3,2,1,0:T(2,128)(2,1)}), bf16[32,1,2,4096]{3,2,1,0:T(2,128)(2,1)S(1)}, u32[]{:S(2)}, u32[]{:S(2)}) async-start(bf16[32,1,2,4096]{3,2,1,0:T(2,128)(2,1)} %copy.45), calls=%async_computation.2 | async-start | bytes 1048576 | tf_op jit(solution)/shard_map/all_to_all | solution.py:155
  84.9 0.8 copy-start
  97.3 17.9 %all-to-all-start.3 = ((bf16[128,2,1024]{2,1,0:T(2,128)(2,1)}), bf16[128,2,1024]{2,1,0:T(2,128)(2,1)S(1)}, u32[]{:S(2)}, u32[]{:S(2)}) async-start(bf16[128,2,1024]{2,1,0:T(2,128)(2,1)} %bitcast.61), calls=%async_computation.3 | async-start | bytes 1048576 | tf_op jit(solution)/shard_map/all_to_all | solution.py:162

commit v10 on v9

--- a/solution.py
+++ b/solution.py
@@ -24,7 +24,8 @@
     return (residual, normed)
 
 
-def ffn_kernel(x_ref, wg_ref, wu_ref, wd_ref, o_ref, acc_ref, out_ref):
+def ffn_kernel(x_ref, *refs):
+    *w_refs, o_ref, acc_ref, out_ref = refs
     step = pl.program_id(0)
     sources, slots, _ = x_ref.shape
     parts = o_ref.shape[1]
@@ -35,10 +36,11 @@
         acc_ref[...] = jnp.zeros_like(acc_ref)
 
     x = jnp.concatenate([x_ref[:, c, :] for c in range(slots)], axis=0)
-    gate = jnp.dot(x, wg_ref[...], preferred_element_type=jnp.float32)
-    up = jnp.dot(x, wu_ref[...], preferred_element_type=jnp.float32)
-    activated = (gate / (1.0 + jnp.exp(-gate)) * up).astype(jnp.bfloat16)
-    acc_ref[...] += jnp.dot(activated, wd_ref[...], preferred_element_type=jnp.float32)
+    for wg_ref, wu_ref, wd_ref in zip(w_refs[0::3], w_refs[1::3], w_refs[2::3]):
+        gate = jnp.dot(x, wg_ref[...], preferred_element_type=jnp.float32)
+        up = jnp.dot(x, wu_ref[...], preferred_element_type=jnp.float32)
+        activated = (gate / (1.0 + jnp.exp(-gate)) * up).astype(jnp.bfloat16)
+        acc_ref[...] += jnp.dot(activated, wd_ref[...], preferred_element_type=jnp.float32)
 
     @pl.when(step == pl.num_programs(0) - 1)
     def _():
@@ -48,18 +50,22 @@
         o_ref[...] = out_ref[...].astype(o_ref.dtype)
 
 
-def expert_ffn(x, wg, wu, wd, parts, chunk=256):
+def expert_ffn(x, wg, wu, wd, parts, chunk=256, split=2):
     sources, slots, width = x.shape
     ff = wg.shape[1]
     share = width // parts
     return pl.pallas_call(
         ffn_kernel,
         grid=(ff // chunk,),
-        in_specs=[
-            pl.BlockSpec((sources, slots, width), lambda f: (0, 0, 0)),
-            pl.BlockSpec((width, chunk), lambda f: (0, f)),
-            pl.BlockSpec((width, chunk), lambda f: (0, f)),
-            pl.BlockSpec((chunk, width), lambda f: (f, 0)),
+        in_specs=[pl.BlockSpec((sources, slots, width), lambda f: (0, 0, 0))]
+        + [
+            spec
+            for h in range(split)
+            for spec in (
+                pl.BlockSpec((width, chunk // split), lambda f, h=h: (0, f * split + h)),
+                pl.BlockSpec((width, chunk // split), lambda f, h=h: (0, f * split + h)),
+                pl.BlockSpec((chunk // split, width), lambda f, h=h: (f * split + h, 0)),
+            )
         ],
         out_specs=pl.BlockSpec((sources, parts, slots, share), lambda f: (0, 0, 0, 0)),
         out_shape=jax.ShapeDtypeStruct((sources, parts, slots, share), jnp.bfloat16),
@@ -73,7 +79,7 @@
             transcendentals=sources * slots * ff,
             bytes_accessed=2 * (3 * width * ff + 2 * sources * slots * width),
         ),
-    )(x, wg, wu, wd)
+    )(x, *([wg, wu, wd] * split))
 
 
 def local(

time: 117 us -> 118 us (level)
  no operation moved by 1% of the time
where the time goes in v10:
time: 118 us; the launch traced here: 117 us
  waiting for transfers between devices  57 us (48%)
  starting transfers between devices  29.3 us (25%)
  Pallas kernels  12.7 us (11%)
  matrix products  10 us (8%)
  local copies, waits for them, and re-layouts  5.93 us (5%)
  other arithmetic  2.27 us (2%)
    all_to_all x1, waiting for transfers between devices, local(): mine = lax.all_to_all(sent, ('x', 'z'), 0, 0, tiled=True)  17.3 us
    all_to_all x1, waiting for transfers between devices, local(): results = lax.all_to_all(back, ALL, 0, 0, tiled=True)  13.9 us
    pallas_call x1, Pallas kernels, expert_ffn(): pl.pallas_call(ffn_kernel, grid=(ff // chunk,), in_specs=[pl.BlockSpec((s...  12.7 us
    all_to_all x1, waiting for transfers between devices, local(): lax.all_to_all(sent.reshape(n_xz * tp_count, rows_dev, pair_cols), ('x',...  12.7 us
    all_to_all x1, waiting for transfers between devices, local(): arrived_slots = lax.all_to_all(outgoing, DP, 0, 0, tiled=True)  11.7 us
    all_to_all x1, starting transfers between devices, local(): lax.all_to_all(sent.reshape(n_xz * tp_count, rows_dev, pair_cols), ('x',...  8.83 us
    all_to_all x1, starting transfers between devices, local(): mine = lax.all_to_all(sent, ('x', 'z'), 0, 0, tiled=True)  8.55 us
    all_to_all x1, starting transfers between devices, local(): arrived_slots = lax.all_to_all(outgoing, DP, 0, 0, tiled=True)  7.04 us
  transfers between devices with their start and end apart: 5, of which 5 were waited for; matrix products, arithmetic and copies ran while one was open for 2% of the time, Pallas kernels for 0%

profile of v10, /device:TPU:1, one launch (start us, length us, event | category | flops | bytes accessed | tf_op | source)
XLA Modules:
  0.0 117.4 jit_solution(9393886821566919561)
XLA Ops:
  0.0 0.9 copy.48
  0.9 0.7 iota_compare_fusion.1
  1.7 3.8 %fusion.42 = (f32[24,16]{1,0:T(8,128)S(1)}, f32[24,16,768]{2,1,0:T(8,128)S(1)}) fusion(bf16[24,16,128]{2,1,0:T(8,128)(2,1)S(1)} %bitcast.70, bf16[24,1,768,128]{3,2,1,0:T(8,128)(2,1)} %param.13, pred[24,768]{1,0:T(8,128)(4,1)S(1)} %iota_compare_fusion.1), kind=kOutput, calls=%fused_computation.58 | convolution fusion | flops 76677888 | bytes 6016512 | tf_op jit(solution)/shard_map/sub | solution.py:119
  5.5 3.2 %fusion.14 = bf16[24,16,128]{2,1,0:T(8,128)(2,1)S(1)} fusion(bf16[24,1,768,128]{3,2,1,0:T(8,128)(2,1)} %param.14, f32[24,16,768]{2,1,0:T(8,128)S(1)} %get-tuple-element.10, f32[24,16]{1,0:T(8,128)S(1)} %get-tuple-element.9), kind=kOutput, calls=%fused_computation.13 | convolution fusion | flops 76136448 | bytes 5998080 | tf_op jit(solution)/shard_map/rhgl,rhld->rhgd/dot_general | solution.py:121
  8.7 1.3 %broadcast_in_dim.66 = bf16[16,24,2048]{2,1,0:T(8,128)(2,1)} broadcast(bf16[24,2048]{1,0:T(8,128)(2,1)S(1)} %bitcast.69), dimensions={1,2} | broadcast | bytes 1671168 | tf_op jit(solution)/shard_map/broadcast_in_dim | solution.py:130
  10.0 0.0 copy-start.1
  10.0 0.0 copy-start.4
  10.0 8.5 %all-to-all-start = ((bf16[16,24,2048]{2,1,0:T(8,128)(2,1)}), bf16[16,24,2048]{2,1,0:T(8,128)(2,1)S(1)}, u32[]{:S(2)}, u32[]{:S(2)}) async-start(bf16[16,24,2048]{2,1,0:T(8,128)(2,1)} %broadcast_in_dim.66), calls=%async_computation | async-start | bytes 3145728 | tf_op jit(solution)/shard_map/all_to_all | solution.py:131
  18.6 0.0 copy-done.1
  18.6 1.0 collective-permute-start
  19.6 0.0 copy-done.4
  19.6 0.1 copy.38
  19.7 1.5 %collective-permute-done = bf16[2048,128]{1,0:T(8,128)(2,1)S(1)} collective-permute-done((bf16[2048,128]{1,0:T(8,128)(2,1)S(1)}, bf16[2048,128]{1,0:T(8,128)(2,1)S(1)}, u32[]{:S(2)}, u32[]{:S(2)}) %collective-permute-start) | collective-permute-done | bytes 524320 | tf_op jit(solution)/shard_map/ppermute | solution.py:126
  21.2 0.9 broadcast_select_fusion.1
  22.1 17.3 %all-to-all-done = bf16[16,24,2048]{2,1,0:T(8,128)(2,1)S(1)} async-done(((bf16[16,24,2048]{2,1,0:T(8,128)(2,1)}), bf16[16,24,2048]{2,1,0:T(8,128)(2,1)S(1)}, u32[]{:S(2)}, u32[]{:S(2)}) %all-to-all-start) | async-done | bytes 1572896 | tf_op jit(solution)/shard_map/all_to_all | solution.py:131
  39.3 1.7 %convolution_convert_fusion.1 = bf16[16,24,256]{2,1,0:T(8,128)(2,1)S(1)} fusion(bf16[16,24,2048]{2,1,0:T(8,128)(2,1)S(1)} %all-to-all-done, bf16[2048,128]{1,0:T(8,128)(2,1)} %get-tuple-element.8, bf16[2048,128]{1,0:T(8,128)(2,1)S(1)} %get-tuple-element.7), kind=kOutput, calls=%fused_computation.12 | convolution fusion | flops 404848640 | bytes 2818048 | tf_op jit(solution)/shard_map/ird,dc->irc/dot_general | solution.py:132
  41.0 0.9 broadcast_in_dim.67
  41.9 8.8 %all-to-all-start.1 = ((bf16[64,24,256]{2,1,0:T(8,128)(2,1)}), bf16[64,24,256]{2,1,0:T(8,128)(2,1)S(1)}, u32[]{:S(2)}, u32[]{:S(2)}) async-start(bf16[64,24,256]{2,1,0:T(8,128)(2,1)} %bitcast.3), calls=%async_computation.1 | async-start | bytes 1572864 | tf_op jit(solution)/shard_map/all_to_all | solution.py:138
  50.8 0.0 copy-start.2
  50.8 0.1 convert_reduce_fusion
  50.9 0.1 copy.42
  51.0 0.1 copy.41
  51.1 0.1 copy.43
  51.3 0.1 copy.44
  51.4 12.7 %all-to-all-done.1 = bf16[64,24,256]{2,1,0:T(8,128)(2,1)S(1)} async-done(((bf16[64,24,256]{2,1,0:T(8,128)(2,1)}), bf16[64,24,256]{2,1,0:T(8,128)(2,1)S(1)}, u32[]{:S(2)}, u32[]{:S(2)}) %all-to-all-start.1) | async-done | bytes 786464 | tf_op jit(solution)/shard_map/all_to_all | solution.py:138
  64.1 0.1 bitcast_reduce_fusion
  64.3 0.0 copy-done.2
  64.3 0.2 fusion.23
  64.5 0.0 copy-start.3
  64.5 0.4 fusion.5
  64.8 1.3 %copy.45 = bf16[32,1,2,4096]{3,2,1,0:T(2,128)(2,1)} copy(bf16[32,1,2,4096]{3,0,2,1:T(8,128)(2,1)S(1)} %fusion.5) | data formatting | bytes 1048576 | tf_op jit(solution)/shard_map/convert_element_type | solution.py:160
  66.2 7.0 %all-to-all-start.2 = ((bf16[32,1,2,4096]{3,2,1,0:T(2,128)(2,1)}), bf16[32,1,2,4096]{3,2,1,0:T(2,128)(2,1)S(1)}, u32[]{:S(2)}, u32[]{:S(2)}) async-start(bf16[32,1,2,4096]{3,2,1,0:T(2,128)(2,1)} %copy.45), calls=%async_computation.2 | async-start | bytes 1048576 | tf_op jit(solution)/shard_map/all_to_all | solution.py:161
  73.2 0.0 copy-done.3
  73.3 11.7 %all-to-all-done.2 = bf16[32,1,2,4096]{3,2,1,0:T(2,128)(2,1)S(1)} async-done(((bf16[32,1,2,4096]{3,2,1,0:T(2,128)(2,1)}), bf16[32,1,2,4096]{3,2,1,0:T(2,128)(2,1)S(1)}, u32[]{:S(2)}, u32[]{:S(2)}) %all-to-all-start.2) | async-done | bytes 524320 | tf_op jit(solution)/shard_map/all_to_all | solution.py:161
  84.9 0.0 copy-start
  84.9 0.8 copy-done
  85.7 12.7 %shard_map.109 = bf16[32,4,2,1024]{3,2,1,0:T(2,128)(2,1)} custom-call(bf16[32,2,4096]{2,1,0:T(2,128)(2,1)} %bitcast.65, bf16[4096,768]{1,0:T(8,128)(2,1)} %bitcast.58, bf16[4096,768]{1,0:T(8,128)(2,1)} %bitcast.60, bf16[768,4096]{1,0:T(8,128)(2,1)} %bitcast.62, bf16[4096,768]{1,0:T(8,128)(2,1)} %bitcast.59, bf16[4096,768]{1,0:T(8,128)(2,1)} %bitcast.61, ...), custom_call_target="tpu_custom_call" | custom-call | flops 1207959552 | bytes 19922944 | tf_op jit(solution)/shard_map/pallas_call | solution.py:57
  98.4 3.8 %all-to-all-start.3 = ((bf16[128,2,1024]{2,1,0:T(2,128)(2,1)}), bf16[128,2,1024]{2,1,0:T(2,128)(2,1)S(1)}, u32[]{:S(2)}, u32[]{:S(2)}) async-start(bf16[128,2,1024]{2,1,0:T(2,128)(2,1)} %bitcast.64), calls=%async_computation.3 | async-start | bytes 1048576 | tf_op jit(solution)/shard_map/all_to_all | solution.py:168
  102.3 0.1 copy.40
  102.3 0.1 select_reduce_fusion
  102.5 13.9 %all-to-all-done.3 = bf16[128,2,1024]{2,1,0:T(2,128)(2,1)S(1)} async-done(((bf16[128,2,1024]{2,1,0:T(2,128)(2,1)}), bf16[128,2,1024]{2,1,0:T(2,128)(2,1)S(1)}, u32[]{:S(2)}, u32[]{:S(2)}) %all-to-all-start.3) | async-done | bytes 524320 | tf_op jit(solution)/shard_map/all_to_all | solution.py:168
  116.4 1.0 fusion.18
  (13 shorter events, 0.2 us)
Async XLA Ops:
  10.0 8.6 %copy-start.1 = (bf16[2048,128]{1,0:T(8,128)(2,1)S(1)}, bf16[2048,128]{1,0:T(8,128)(2,1)}, u32[]{:S(2)}) copy-start(bf16[2048,128]{1,0:T(8,128)(2,1)} %param.16) | copy-start | bytes 1572868
  10.0 9.6 %copy-start.4 = (s32[24,8]{0,1:T(8,128)S(1)}, s32[24,8]{0,1:T(8,128)}, u32[]{:S(2)}) copy-start(s32[24,8]{0,1:T(8,128)} %param.17) | copy-start | bytes 2308
  10.0 29.3 %all-to-all-start = ((bf16[16,24,2048]{2,1,0:T(8,128)(2,1)}), bf16[16,24,2048]{2,1,0:T(8,128)(2,1)S(1)}, u32[]{:S(2)}, u32[]{:S(2)}) async-start(bf16[16,24,2048]{2,1,0:T(8,128)(2,1)} %broadcast_in_dim.66), calls=%async_computation | async-start | bytes 3145728 | tf_op jit(solution)/shard_map/all_to_all | solution.py:131
  18.6 2.6 %collective-permute-start = (bf16[2048,128]{1,0:T(8,128)(2,1)S(1)}, bf16[2048,128]{1,0:T(8,128)(2,1)S(1)}, u32[]{:S(2)}, u32[]{:S(2)}) collective-permute-start(bf16[2048,128]{1,0:T(8,128)(2,1)S(1)} %copy-done.1), channel_id=1, source_target_pairs={{0,4},{4,0},{1,5},{5,1},{2,6},{6,2},{3,7},{7,3},{8,12},{12,8},{9,1... | collective-permute-start | bytes 1572872 | tf_op jit(solution)/shard_map/ppermute | solution.py:126
  41.9 22.2 %all-to-all-start.1 = ((bf16[64,24,256]{2,1,0:T(8,128)(2,1)}), bf16[64,24,256]{2,1,0:T(8,128)(2,1)S(1)}, u32[]{:S(2)}, u32[]{:S(2)}) async-start(bf16[64,24,256]{2,1,0:T(8,128)(2,1)} %bitcast.3), calls=%async_computation.1 | async-start | bytes 1572864 | tf_op jit(solution)/shard_map/all_to_all | solution.py:138
  50.8 13.5 %copy-start.2 = (bf16[24,4096]{1,0:T(8,128)(2,1)S(1)}, bf16[24,4096]{1,0:T(8,128)(2,1)}, u32[]{:S(2)}) copy-start(bf16[24,4096]{1,0:T(8,128)(2,1)} %param.11) | copy-start | bytes 589828
  64.5 8.8 %copy-start.3 = (f32[24,8]{0,1:T(8,128)S(1)}, f32[24,8]{0,1:T(8,128)}, u32[]{:S(2)}) copy-start(f32[24,8]{0,1:T(8,128)} %param.18) | copy-start | bytes 2308
  66.2 18.8 %all-to-all-start.2 = ((bf16[32,1,2,4096]{3,2,1,0:T(2,128)(2,1)}), bf16[32,1,2,4096]{3,2,1,0:T(2,128)(2,1)S(1)}, u32[]{:S(2)}, u32[]{:S(2)}) async-start(bf16[32,1,2,4096]{3,2,1,0:T(2,128)(2,1)} %copy.45), calls=%async_computation.2 | async-start | bytes 1048576 | tf_op jit(solution)/shard_map/all_to_all | solution.py:161
  84.9 0.8 copy-start
  98.4 17.9 %all-to-all-start.3 = ((bf16[128,2,1024]{2,1,0:T(2,128)(2,1)}), bf16[128,2,1024]{2,1,0:T(2,128)(2,1)S(1)}, u32[]{:S(2)}, u32[]{:S(2)}) async-start(bf16[128,2,1024]{2,1,0:T(2,128)(2,1)} %bitcast.64), calls=%async_computation.3 | async-start | bytes 1048576 | tf_op jit(solution)/shard_map/all_to_all | solution.py:168

commit v11 on v9

--- a/solution.py
+++ b/solution.py
@@ -48,7 +48,7 @@
         o_ref[...] = out_ref[...].astype(o_ref.dtype)
 
 
-def expert_ffn(x, wg, wu, wd, parts, chunk=256):
+def expert_ffn(x, wg, wu, wd, parts, chunk=384):
     sources, slots, width = x.shape
     ff = wg.shape[1]
     share = width // parts

time: 117 us -> 117 us (level)
  no operation moved by 1% of the time
where the time goes in v11:
time: 117 us; the launch traced here: 116 us
  waiting for transfers between devices  57 us (49%)
  starting transfers between devices  29.3 us (25%)
  Pallas kernels  11.6 us (10%)
  matrix products  10 us (9%)
  local copies, waits for them, and re-layouts  5.93 us (5%)
  other arithmetic  2.27 us (2%)
    all_to_all x1, waiting for transfers between devices, local(): mine = lax.all_to_all(sent, ('x', 'z'), 0, 0, tiled=True)  17.3 us
    all_to_all x1, waiting for transfers between devices, local(): results = lax.all_to_all(back, ALL, 0, 0, tiled=True)  13.9 us
    all_to_all x1, waiting for transfers between devices, local(): lax.all_to_all(sent.reshape(n_xz * tp_count, rows_dev, pair_cols), ('x',...  12.7 us
    all_to_all x1, waiting for transfers between devices, local(): arrived_slots = lax.all_to_all(outgoing, DP, 0, 0, tiled=True)  11.7 us
    pallas_call x1, Pallas kernels, expert_ffn(): pl.pallas_call(ffn_kernel, grid=(ff // chunk,), in_specs=[pl.BlockSpec((s...  11.6 us
    all_to_all x1, starting transfers between devices, local(): lax.all_to_all(sent.reshape(n_xz * tp_count, rows_dev, pair_cols), ('x',...  8.83 us
    all_to_all x1, starting transfers between devices, local(): mine = lax.all_to_all(sent, ('x', 'z'), 0, 0, tiled=True)  8.55 us
    all_to_all x1, starting transfers between devices, local(): arrived_slots = lax.all_to_all(outgoing, DP, 0, 0, tiled=True)  7.04 us
  transfers between devices with their start and end apart: 5, of which 5 were waited for; matrix products, arithmetic and copies ran while one was open for 2% of the time, Pallas kernels for 0%

profile of v11, /device:TPU:1, one launch (start us, length us, event | category | flops | bytes accessed | tf_op | source)
XLA Modules:
  0.0 116.2 jit_solution(2200410245036911565)
XLA Ops:
  0.0 0.9 copy.48
  0.9 0.7 iota_compare_fusion.1
  1.7 3.8 %fusion.42 = (f32[24,16]{1,0:T(8,128)S(1)}, f32[24,16,768]{2,1,0:T(8,128)S(1)}) fusion(bf16[24,16,128]{2,1,0:T(8,128)(2,1)S(1)} %bitcast.67, bf16[24,1,768,128]{3,2,1,0:T(8,128)(2,1)} %param.13, pred[24,768]{1,0:T(8,128)(4,1)S(1)} %iota_compare_fusion.1), kind=kOutput, calls=%fused_computation.58 | convolution fusion | flops 76677888 | bytes 6016512 | tf_op jit(solution)/shard_map/sub | solution.py:113
  5.5 3.2 %fusion.14 = bf16[24,16,128]{2,1,0:T(8,128)(2,1)S(1)} fusion(bf16[24,1,768,128]{3,2,1,0:T(8,128)(2,1)} %param.14, f32[24,16,768]{2,1,0:T(8,128)S(1)} %get-tuple-element.10, f32[24,16]{1,0:T(8,128)S(1)} %get-tuple-element.9), kind=kOutput, calls=%fused_computation.13 | convolution fusion | flops 76136448 | bytes 5998080 | tf_op jit(solution)/shard_map/rhgl,rhld->rhgd/dot_general | solution.py:115
  8.7 1.3 %broadcast_in_dim.66 = bf16[16,24,2048]{2,1,0:T(8,128)(2,1)} broadcast(bf16[24,2048]{1,0:T(8,128)(2,1)S(1)} %bitcast.66), dimensions={1,2} | broadcast | bytes 1671168 | tf_op jit(solution)/shard_map/broadcast_in_dim | solution.py:124
  10.0 0.0 copy-start.1
  10.0 0.0 copy-start.4
  10.0 8.5 %all-to-all-start = ((bf16[16,24,2048]{2,1,0:T(8,128)(2,1)}), bf16[16,24,2048]{2,1,0:T(8,128)(2,1)S(1)}, u32[]{:S(2)}, u32[]{:S(2)}) async-start(bf16[16,24,2048]{2,1,0:T(8,128)(2,1)} %broadcast_in_dim.66), calls=%async_computation | async-start | bytes 3145728 | tf_op jit(solution)/shard_map/all_to_all | solution.py:125
  18.6 0.0 copy-done.1
  18.6 1.0 collective-permute-start
  19.6 0.0 copy-done.4
  19.6 0.1 copy.38
  19.7 1.5 %collective-permute-done = bf16[2048,128]{1,0:T(8,128)(2,1)S(1)} collective-permute-done((bf16[2048,128]{1,0:T(8,128)(2,1)S(1)}, bf16[2048,128]{1,0:T(8,128)(2,1)S(1)}, u32[]{:S(2)}, u32[]{:S(2)}) %collective-permute-start) | collective-permute-done | bytes 524320 | tf_op jit(solution)/shard_map/ppermute | solution.py:120
  21.2 0.9 broadcast_select_fusion.1
  22.1 17.3 %all-to-all-done = bf16[16,24,2048]{2,1,0:T(8,128)(2,1)S(1)} async-done(((bf16[16,24,2048]{2,1,0:T(8,128)(2,1)}), bf16[16,24,2048]{2,1,0:T(8,128)(2,1)S(1)}, u32[]{:S(2)}, u32[]{:S(2)}) %all-to-all-start) | async-done | bytes 1572896 | tf_op jit(solution)/shard_map/all_to_all | solution.py:125
  39.3 1.7 %convolution_convert_fusion.1 = bf16[16,24,256]{2,1,0:T(8,128)(2,1)S(1)} fusion(bf16[16,24,2048]{2,1,0:T(8,128)(2,1)S(1)} %all-to-all-done, bf16[2048,128]{1,0:T(8,128)(2,1)} %get-tuple-element.8, bf16[2048,128]{1,0:T(8,128)(2,1)S(1)} %get-tuple-element.7), kind=kOutput, calls=%fused_computation.12 | convolution fusion | flops 404848640 | bytes 2818048 | tf_op jit(solution)/shard_map/ird,dc->irc/dot_general | solution.py:126
  41.0 0.9 broadcast_in_dim.67
  41.9 8.8 %all-to-all-start.1 = ((bf16[64,24,256]{2,1,0:T(8,128)(2,1)}), bf16[64,24,256]{2,1,0:T(8,128)(2,1)S(1)}, u32[]{:S(2)}, u32[]{:S(2)}) async-start(bf16[64,24,256]{2,1,0:T(8,128)(2,1)} %bitcast.3), calls=%async_computation.1 | async-start | bytes 1572864 | tf_op jit(solution)/shard_map/all_to_all | solution.py:132
  50.8 0.0 copy-start.2
  50.8 0.1 convert_reduce_fusion
  50.9 0.1 copy.42
  51.0 0.1 copy.41
  51.1 0.1 copy.43
  51.3 0.1 copy.44
  51.4 12.7 %all-to-all-done.1 = bf16[64,24,256]{2,1,0:T(8,128)(2,1)S(1)} async-done(((bf16[64,24,256]{2,1,0:T(8,128)(2,1)}), bf16[64,24,256]{2,1,0:T(8,128)(2,1)S(1)}, u32[]{:S(2)}, u32[]{:S(2)}) %all-to-all-start.1) | async-done | bytes 786464 | tf_op jit(solution)/shard_map/all_to_all | solution.py:132
  64.1 0.1 bitcast_reduce_fusion
  64.3 0.0 copy-done.2
  64.3 0.2 fusion.23
  64.5 0.0 copy-start.3
  64.5 0.4 fusion.5
  64.8 1.3 %copy.45 = bf16[32,1,2,4096]{3,2,1,0:T(2,128)(2,1)} copy(bf16[32,1,2,4096]{3,0,2,1:T(8,128)(2,1)S(1)} %fusion.5) | data formatting | bytes 1048576 | tf_op jit(solution)/shard_map/convert_element_type | solution.py:154
  66.2 7.0 %all-to-all-start.2 = ((bf16[32,1,2,4096]{3,2,1,0:T(2,128)(2,1)}), bf16[32,1,2,4096]{3,2,1,0:T(2,128)(2,1)S(1)}, u32[]{:S(2)}, u32[]{:S(2)}) async-start(bf16[32,1,2,4096]{3,2,1,0:T(2,128)(2,1)} %copy.45), calls=%async_computation.2 | async-start | bytes 1048576 | tf_op jit(solution)/shard_map/all_to_all | solution.py:155
  73.2 0.0 copy-done.3
  73.3 11.7 %all-to-all-done.2 = bf16[32,1,2,4096]{3,2,1,0:T(2,128)(2,1)S(1)} async-done(((bf16[32,1,2,4096]{3,2,1,0:T(2,128)(2,1)}), bf16[32,1,2,4096]{3,2,1,0:T(2,128)(2,1)S(1)}, u32[]{:S(2)}, u32[]{:S(2)}) %all-to-all-start.2) | async-done | bytes 524320 | tf_op jit(solution)/shard_map/all_to_all | solution.py:155
  84.9 0.0 copy-start
  84.9 0.8 copy-done
  85.7 11.6 %shard_map.109 = bf16[32,4,2,1024]{3,2,1,0:T(2,128)(2,1)} custom-call(bf16[32,2,4096]{2,1,0:T(2,128)(2,1)} %bitcast.62, bf16[4096,768]{1,0:T(8,128)(2,1)} %bitcast.58, bf16[4096,768]{1,0:T(8,128)(2,1)} %bitcast.59, bf16[768,4096]{1,0:T(8,128)(2,1)} %bitcast.60), custom_call_target="tpu_custom_call" | custom-call | flops 1207959552 | bytes 19922944 | tf_op jit(solution)/shard_map/pallas_call | solution.py:55
  97.3 3.8 %all-to-all-start.3 = ((bf16[128,2,1024]{2,1,0:T(2,128)(2,1)}), bf16[128,2,1024]{2,1,0:T(2,128)(2,1)S(1)}, u32[]{:S(2)}, u32[]{:S(2)}) async-start(bf16[128,2,1024]{2,1,0:T(2,128)(2,1)} %bitcast.61), calls=%async_computation.3 | async-start | bytes 1048576 | tf_op jit(solution)/shard_map/all_to_all | solution.py:162
  101.1 0.1 copy.40
  101.2 0.1 select_reduce_fusion
  101.3 13.9 %all-to-all-done.3 = bf16[128,2,1024]{2,1,0:T(2,128)(2,1)S(1)} async-done(((bf16[128,2,1024]{2,1,0:T(2,128)(2,1)}), bf16[128,2,1024]{2,1,0:T(2,128)(2,1)S(1)}, u32[]{:S(2)}, u32[]{:S(2)}) %all-to-all-start.3) | async-done | bytes 524320 | tf_op jit(solution)/shard_map/all_to_all | solution.py:162
  115.2 1.0 fusion.18
  (13 shorter events, 0.2 us)
Async XLA Ops:
  10.0 8.6 %copy-start.1 = (bf16[2048,128]{1,0:T(8,128)(2,1)S(1)}, bf16[2048,128]{1,0:T(8,128)(2,1)}, u32[]{:S(2)}) copy-start(bf16[2048,128]{1,0:T(8,128)(2,1)} %param.16) | copy-start | bytes 1572868
  10.0 9.6 %copy-start.4 = (s32[24,8]{0,1:T(8,128)S(1)}, s32[24,8]{0,1:T(8,128)}, u32[]{:S(2)}) copy-start(s32[24,8]{0,1:T(8,128)} %param.17) | copy-start | bytes 2308
  10.0 29.3 %all-to-all-start = ((bf16[16,24,2048]{2,1,0:T(8,128)(2,1)}), bf16[16,24,2048]{2,1,0:T(8,128)(2,1)S(1)}, u32[]{:S(2)}, u32[]{:S(2)}) async-start(bf16[16,24,2048]{2,1,0:T(8,128)(2,1)} %broadcast_in_dim.66), calls=%async_computation | async-start | bytes 3145728 | tf_op jit(solution)/shard_map/all_to_all | solution.py:125
  18.6 2.6 %collective-permute-start = (bf16[2048,128]{1,0:T(8,128)(2,1)S(1)}, bf16[2048,128]{1,0:T(8,128)(2,1)S(1)}, u32[]{:S(2)}, u32[]{:S(2)}) collective-permute-start(bf16[2048,128]{1,0:T(8,128)(2,1)S(1)} %copy-done.1), channel_id=1, source_target_pairs={{0,4},{4,0},{1,5},{5,1},{2,6},{6,2},{3,7},{7,3},{8,12},{12,8},{9,1... | collective-permute-start | bytes 1572872 | tf_op jit(solution)/shard_map/ppermute | solution.py:120
  41.9 22.2 %all-to-all-start.1 = ((bf16[64,24,256]{2,1,0:T(8,128)(2,1)}), bf16[64,24,256]{2,1,0:T(8,128)(2,1)S(1)}, u32[]{:S(2)}, u32[]{:S(2)}) async-start(bf16[64,24,256]{2,1,0:T(8,128)(2,1)} %bitcast.3), calls=%async_computation.1 | async-start | bytes 1572864 | tf_op jit(solution)/shard_map/all_to_all | solution.py:132
  50.8 13.5 %copy-start.2 = (bf16[24,4096]{1,0:T(8,128)(2,1)S(1)}, bf16[24,4096]{1,0:T(8,128)(2,1)}, u32[]{:S(2)}) copy-start(bf16[24,4096]{1,0:T(8,128)(2,1)} %param.11) | copy-start | bytes 589828
  64.5 8.8 %copy-start.3 = (f32[24,8]{0,1:T(8,128)S(1)}, f32[24,8]{0,1:T(8,128)}, u32[]{:S(2)}) copy-start(f32[24,8]{0,1:T(8,128)} %param.18) | copy-start | bytes 2308
  66.2 18.8 %all-to-all-start.2 = ((bf16[32,1,2,4096]{3,2,1,0:T(2,128)(2,1)}), bf16[32,1,2,4096]{3,2,1,0:T(2,128)(2,1)S(1)}, u32[]{:S(2)}, u32[]{:S(2)}) async-start(bf16[32,1,2,4096]{3,2,1,0:T(2,128)(2,1)} %copy.45), calls=%async_computation.2 | async-start | bytes 1048576 | tf_op jit(solution)/shard_map/all_to_all | solution.py:155
  84.9 0.8 copy-start
  97.3 17.9 %all-to-all-start.3 = ((bf16[128,2,1024]{2,1,0:T(2,128)(2,1)}), bf16[128,2,1024]{2,1,0:T(2,128)(2,1)S(1)}, u32[]{:S(2)}, u32[]{:S(2)}) async-start(bf16[128,2,1024]{2,1,0:T(2,128)(2,1)} %bitcast.61), calls=%async_computation.3 | async-start | bytes 1048576 | tf_op jit(solution)/shard_map/all_to_all | solution.py:162

commit v12 on v9

--- a/solution.py
+++ b/solution.py
@@ -161,12 +161,12 @@
 
     results = lax.all_to_all(back, ALL, 0, 0, tiled=True)
     combine_table = jnp.where(slot_hit, all_weight[:, :, None], 0.0)
+    table_hi = combine_table.astype(jnp.bfloat16)
+    table_lo = (combine_table - table_hi.astype(jnp.float32)).astype(jnp.bfloat16)
+    arrived_out = results.reshape(n_exp, CAP, width_share)
     mixture = jnp.einsum(
-        "rmc,mcd->rd",
-        combine_table,
-        results.reshape(n_exp, CAP, width_share).astype(jnp.float32),
-        precision=lax.Precision.HIGHEST,
-    )
+        "rmc,mcd->rd", table_hi, arrived_out, preferred_element_type=jnp.float32
+    ) + jnp.einsum("rmc,mcd->rd", table_lo, arrived_out, preferred_element_type=jnp.float32)
     residual_own = lax.dynamic_slice_in_dim(residual, tp_rank * width_share, width_share, 1)
     return (residual_own.astype(jnp.float32) + mixture).astype(jnp.bfloat16)
 

time: 117 us -> 117 us (level)
  no operation moved by 1% of the time
where the time goes in v12:
time: 117 us; the launch traced here: 116 us
  waiting for transfers between devices  57 us (49%)
  starting transfers between devices  29.3 us (25%)
  Pallas kernels  11.6 us (10%)
  matrix products  10.1 us (9%)
  local copies, waits for them, and re-layouts  5.93 us (5%)
  other arithmetic  2.27 us (2%)
    all_to_all x1, waiting for transfers between devices, local(): mine = lax.all_to_all(sent, ('x', 'z'), 0, 0, tiled=True)  17.3 us
    all_to_all x1, waiting for transfers between devices, local(): results = lax.all_to_all(back, ALL, 0, 0, tiled=True)  13.9 us
    all_to_all x1, waiting for transfers between devices, local(): lax.all_to_all(sent.reshape(n_xz * tp_count, rows_dev, pair_cols), ('x',...  12.7 us
    all_to_all x1, waiting for transfers between devices, local(): arrived_slots = lax.all_to_all(outgoing, DP, 0, 0, tiled=True)  11.7 us
    pallas_call x1, Pallas kernels, expert_ffn(): pl.pallas_call(ffn_kernel, grid=(ff // chunk,), in_specs=[pl.BlockSpec((s...  11.6 us
    all_to_all x1, starting transfers between devices, local(): lax.all_to_all(sent.reshape(n_xz * tp_count, rows_dev, pair_cols), ('x',...  8.83 us
    all_to_all x1, starting transfers between devices, local(): mine = lax.all_to_all(sent, ('x', 'z'), 0, 0, tiled=True)  8.55 us
    all_to_all x1, starting transfers between devices, local(): arrived_slots = lax.all_to_all(outgoing, DP, 0, 0, tiled=True)  7.04 us
  transfers between devices with their start and end apart: 5, of which 5 were waited for; matrix products, arithmetic and copies ran while one was open for 2% of the time, Pallas kernels for 0%

profile of v12, /device:TPU:1, one launch (start us, length us, event | category | flops | bytes accessed | tf_op | source)
XLA Modules:
  0.0 116.3 jit_solution(14554458752556059846)
XLA Ops:
  0.0 0.9 copy.50
  0.9 0.7 iota_compare_fusion.1
  1.7 3.8 %fusion.49 = (f32[24,16]{1,0:T(8,128)S(1)}, f32[24,16,768]{2,1,0:T(8,128)S(1)}) fusion(bf16[24,16,128]{2,1,0:T(8,128)(2,1)S(1)} %bitcast.71, bf16[24,1,768,128]{3,2,1,0:T(8,128)(2,1)} %param.13, pred[24,768]{1,0:T(8,128)(4,1)S(1)} %iota_compare_fusion.1), kind=kOutput, calls=%fused_computation.68 | convolution fusion | flops 76677888 | bytes 6016512 | tf_op jit(solution)/shard_map/sub | solution.py:113
  5.5 3.2 %fusion.14 = bf16[24,16,128]{2,1,0:T(8,128)(2,1)S(1)} fusion(bf16[24,1,768,128]{3,2,1,0:T(8,128)(2,1)} %param.14, f32[24,16,768]{2,1,0:T(8,128)S(1)} %get-tuple-element.10, f32[24,16]{1,0:T(8,128)S(1)} %get-tuple-element.9), kind=kOutput, calls=%fused_computation.13 | convolution fusion | flops 76136448 | bytes 5998080 | tf_op jit(solution)/shard_map/rhgl,rhld->rhgd/dot_general | solution.py:115
  8.7 1.3 %broadcast_in_dim.66 = bf16[16,24,2048]{2,1,0:T(8,128)(2,1)} broadcast(bf16[24,2048]{1,0:T(8,128)(2,1)S(1)} %bitcast.70), dimensions={1,2} | broadcast | bytes 1671168 | tf_op jit(solution)/shard_map/broadcast_in_dim | solution.py:124
  10.0 0.0 copy-start.1
  10.0 0.0 copy-start.4
  10.0 8.5 %all-to-all-start = ((bf16[16,24,2048]{2,1,0:T(8,128)(2,1)}), bf16[16,24,2048]{2,1,0:T(8,128)(2,1)S(1)}, u32[]{:S(2)}, u32[]{:S(2)}) async-start(bf16[16,24,2048]{2,1,0:T(8,128)(2,1)} %broadcast_in_dim.66), calls=%async_computation | async-start | bytes 3145728 | tf_op jit(solution)/shard_map/all_to_all | solution.py:125
  18.6 0.0 copy-done.1
  18.6 1.0 collective-permute-start
  19.6 0.0 copy-done.4
  19.6 0.1 copy.39
  19.7 1.5 %collective-permute-done = bf16[2048,128]{1,0:T(8,128)(2,1)S(1)} collective-permute-done((bf16[2048,128]{1,0:T(8,128)(2,1)S(1)}, bf16[2048,128]{1,0:T(8,128)(2,1)S(1)}, u32[]{:S(2)}, u32[]{:S(2)}) %collective-permute-start) | collective-permute-done | bytes 524320 | tf_op jit(solution)/shard_map/ppermute | solution.py:120
  21.2 0.9 broadcast_select_fusion.1
  22.1 17.3 %all-to-all-done = bf16[16,24,2048]{2,1,0:T(8,128)(2,1)S(1)} async-done(((bf16[16,24,2048]{2,1,0:T(8,128)(2,1)}), bf16[16,24,2048]{2,1,0:T(8,128)(2,1)S(1)}, u32[]{:S(2)}, u32[]{:S(2)}) %all-to-all-start) | async-done | bytes 1572896 | tf_op jit(solution)/shard_map/all_to_all | solution.py:125
  39.3 1.7 %convolution_convert_fusion.1 = bf16[16,24,256]{2,1,0:T(8,128)(2,1)S(1)} fusion(bf16[16,24,2048]{2,1,0:T(8,128)(2,1)S(1)} %all-to-all-done, bf16[2048,128]{1,0:T(8,128)(2,1)} %get-tuple-element.8, bf16[2048,128]{1,0:T(8,128)(2,1)S(1)} %get-tuple-element.7), kind=kOutput, calls=%fused_computation.12 | convolution fusion | flops 404848640 | bytes 2818048 | tf_op jit(solution)/shard_map/ird,dc->irc/dot_general | solution.py:126
  41.0 0.9 broadcast_in_dim.67
  41.9 8.8 %all-to-all-start.1 = ((bf16[64,24,256]{2,1,0:T(8,128)(2,1)}), bf16[64,24,256]{2,1,0:T(8,128)(2,1)S(1)}, u32[]{:S(2)}, u32[]{:S(2)}) async-start(bf16[64,24,256]{2,1,0:T(8,128)(2,1)} %bitcast.3), calls=%async_computation.1 | async-start | bytes 1572864 | tf_op jit(solution)/shard_map/all_to_all | solution.py:132
  50.8 0.0 copy-start.2
  50.8 0.1 convert_reduce_fusion
  50.9 0.1 copy.43
  51.0 0.1 copy.42
  51.1 0.1 copy.44
  51.3 0.1 copy.45
  51.4 12.7 %all-to-all-done.1 = bf16[64,24,256]{2,1,0:T(8,128)(2,1)S(1)} async-done(((bf16[64,24,256]{2,1,0:T(8,128)(2,1)}), bf16[64,24,256]{2,1,0:T(8,128)(2,1)S(1)}, u32[]{:S(2)}, u32[]{:S(2)}) %all-to-all-start.1) | async-done | bytes 786464 | tf_op jit(solution)/shard_map/all_to_all | solution.py:132
  64.1 0.1 bitcast_reduce_fusion
  64.3 0.0 copy-done.2
  64.3 0.2 fusion.25
  64.5 0.0 copy-start.3
  64.5 0.4 fusion.5
  64.8 1.3 %copy.46 = bf16[32,1,2,4096]{3,2,1,0:T(2,128)(2,1)} copy(bf16[32,1,2,4096]{3,0,2,1:T(8,128)(2,1)S(1)} %fusion.5) | data formatting | bytes 1048576 | tf_op jit(solution)/shard_map/convert_element_type | solution.py:154
  66.2 7.0 %all-to-all-start.2 = ((bf16[32,1,2,4096]{3,2,1,0:T(2,128)(2,1)}), bf16[32,1,2,4096]{3,2,1,0:T(2,128)(2,1)S(1)}, u32[]{:S(2)}, u32[]{:S(2)}) async-start(bf16[32,1,2,4096]{3,2,1,0:T(2,128)(2,1)} %copy.46), calls=%async_computation.2 | async-start | bytes 1048576 | tf_op jit(solution)/shard_map/all_to_all | solution.py:155
  73.2 0.0 copy-done.3
  73.3 11.7 %all-to-all-done.2 = bf16[32,1,2,4096]{3,2,1,0:T(2,128)(2,1)S(1)} async-done(((bf16[32,1,2,4096]{3,2,1,0:T(2,128)(2,1)}), bf16[32,1,2,4096]{3,2,1,0:T(2,128)(2,1)S(1)}, u32[]{:S(2)}, u32[]{:S(2)}) %all-to-all-start.2) | async-done | bytes 524320 | tf_op jit(solution)/shard_map/all_to_all | solution.py:155
  84.9 0.0 copy-start
  84.9 0.8 copy-done
  85.7 11.6 %shard_map.109 = bf16[32,4,2,1024]{3,2,1,0:T(2,128)(2,1)} custom-call(bf16[32,2,4096]{2,1,0:T(2,128)(2,1)} %bitcast.66, bf16[4096,768]{1,0:T(8,128)(2,1)} %bitcast.62, bf16[4096,768]{1,0:T(8,128)(2,1)} %bitcast.63, bf16[768,4096]{1,0:T(8,128)(2,1)} %bitcast.64), custom_call_target="tpu_custom_call" | custom-call | flops 1207959552 | bytes 19922944 | tf_op jit(solution)/shard_map/pallas_call | solution.py:55
  97.3 3.8 %all-to-all-start.3 = ((bf16[128,2,1024]{2,1,0:T(2,128)(2,1)}), bf16[128,2,1024]{2,1,0:T(2,128)(2,1)S(1)}, u32[]{:S(2)}, u32[]{:S(2)}) async-start(bf16[128,2,1024]{2,1,0:T(2,128)(2,1)} %bitcast.65), calls=%async_computation.3 | async-start | bytes 1048576 | tf_op jit(solution)/shard_map/all_to_all | solution.py:162
  101.2 0.1 copy.41
  101.3 0.1 select_reduce_fusion
  101.4 13.9 %all-to-all-done.3 = bf16[128,2,1024]{2,1,0:T(2,128)(2,1)S(1)} async-done(((bf16[128,2,1024]{2,1,0:T(2,128)(2,1)}), bf16[128,2,1024]{2,1,0:T(2,128)(2,1)S(1)}, u32[]{:S(2)}, u32[]{:S(2)}) %all-to-all-start.3) | async-done | bytes 524320 | tf_op jit(solution)/shard_map/all_to_all | solution.py:162
  115.3 0.2 convolution_bitcast_fusion.1
  115.5 0.9 fusion.19
  (13 shorter events, 0.2 us)
Async XLA Ops:
  10.0 8.6 %copy-start.1 = (bf16[2048,128]{1,0:T(8,128)(2,1)S(1)}, bf16[2048,128]{1,0:T(8,128)(2,1)}, u32[]{:S(2)}) copy-start(bf16[2048,128]{1,0:T(8,128)(2,1)} %param.16) | copy-start | bytes 1572868
  10.0 9.6 %copy-start.4 = (s32[24,8]{0,1:T(8,128)S(1)}, s32[24,8]{0,1:T(8,128)}, u32[]{:S(2)}) copy-start(s32[24,8]{0,1:T(8,128)} %param.17) | copy-start | bytes 2308
  10.0 29.3 %all-to-all-start = ((bf16[16,24,2048]{2,1,0:T(8,128)(2,1)}), bf16[16,24,2048]{2,1,0:T(8,128)(2,1)S(1)}, u32[]{:S(2)}, u32[]{:S(2)}) async-start(bf16[16,24,2048]{2,1,0:T(8,128)(2,1)} %broadcast_in_dim.66), calls=%async_computation | async-start | bytes 3145728 | tf_op jit(solution)/shard_map/all_to_all | solution.py:125
  18.6 2.6 %collective-permute-start = (bf16[2048,128]{1,0:T(8,128)(2,1)S(1)}, bf16[2048,128]{1,0:T(8,128)(2,1)S(1)}, u32[]{:S(2)}, u32[]{:S(2)}) collective-permute-start(bf16[2048,128]{1,0:T(8,128)(2,1)S(1)} %copy-done.1), channel_id=1, source_target_pairs={{0,4},{4,0},{1,5},{5,1},{2,6},{6,2},{3,7},{7,3},{8,12},{12,8},{9,1... | collective-permute-start | bytes 1572872 | tf_op jit(solution)/shard_map/ppermute | solution.py:120
  41.9 22.2 %all-to-all-start.1 = ((bf16[64,24,256]{2,1,0:T(8,128)(2,1)}), bf16[64,24,256]{2,1,0:T(8,128)(2,1)S(1)}, u32[]{:S(2)}, u32[]{:S(2)}) async-start(bf16[64,24,256]{2,1,0:T(8,128)(2,1)} %bitcast.3), calls=%async_computation.1 | async-start | bytes 1572864 | tf_op jit(solution)/shard_map/all_to_all | solution.py:132
  50.8 13.5 %copy-start.2 = (bf16[24,4096]{1,0:T(8,128)(2,1)S(1)}, bf16[24,4096]{1,0:T(8,128)(2,1)}, u32[]{:S(2)}) copy-start(bf16[24,4096]{1,0:T(8,128)(2,1)} %param.11) | copy-start | bytes 589828
  64.5 8.8 %copy-start.3 = (f32[24,8]{0,1:T(8,128)S(1)}, f32[24,8]{0,1:T(8,128)}, u32[]{:S(2)}) copy-start(f32[24,8]{0,1:T(8,128)} %param.18) | copy-start | bytes 2308
  66.2 18.8 %all-to-all-start.2 = ((bf16[32,1,2,4096]{3,2,1,0:T(2,128)(2,1)}), bf16[32,1,2,4096]{3,2,1,0:T(2,128)(2,1)S(1)}, u32[]{:S(2)}, u32[]{:S(2)}) async-start(bf16[32,1,2,4096]{3,2,1,0:T(2,128)(2,1)} %copy.46), calls=%async_computation.2 | async-start | bytes 1048576 | tf_op jit(solution)/shard_map/all_to_all | solution.py:155
  84.9 0.8 copy-start
  97.3 17.9 %all-to-all-start.3 = ((bf16[128,2,1024]{2,1,0:T(2,128)(2,1)}), bf16[128,2,1024]{2,1,0:T(2,128)(2,1)S(1)}, u32[]{:S(2)}, u32[]{:S(2)}) async-start(bf16[128,2,1024]{2,1,0:T(2,128)(2,1)} %bitcast.65), calls=%async_computation.3 | async-start | bytes 1048576 | tf_op jit(solution)/shard_map/all_to_all | solution.py:162

commit v13 on v9

--- a/solution.py
+++ b/solution.py
@@ -24,7 +24,7 @@
     return (residual, normed)
 
 
-def ffn_kernel(x_ref, wg_ref, wu_ref, wd_ref, o_ref, acc_ref, out_ref):
+def ffn_kernel(x_ref, wg_ref, wu_ref, wd_ref, o_ref, acc_ref):
     step = pl.program_id(0)
     sources, slots, _ = x_ref.shape
     parts = o_ref.shape[1]
@@ -44,8 +44,9 @@
     def _():
         for t in range(parts):
             for c in range(slots):
-                out_ref[:, t, c, :] = acc_ref[c * sources : (c + 1) * sources, t * share : (t + 1) * share]
-        o_ref[...] = out_ref[...].astype(o_ref.dtype)
+                o_ref[:, t, c, :] = acc_ref[
+                    c * sources : (c + 1) * sources, t * share : (t + 1) * share
+                ].astype(o_ref.dtype)
 
 
 def expert_ffn(x, wg, wu, wd, parts, chunk=256):
@@ -65,7 +66,6 @@
         out_shape=jax.ShapeDtypeStruct((sources, parts, slots, share), jnp.bfloat16),
         scratch_shapes=[
             pltpu.VMEM((slots * sources, width), jnp.float32),
-            pltpu.VMEM((sources, parts, slots, share), jnp.float32),
         ],
         compiler_params=pltpu.CompilerParams(vmem_limit_bytes=60 * 1024 * 1024),
         cost_estimate=pl.CostEstimate(

time: 117 us -> 116 us (level)
  no operation moved by 1% of the time
where the time goes in v13:
time: 116 us
  waiting for transfers between devices  57 us (49%)
  starting transfers between devices  29.3 us (25%)
  Pallas kernels  11.3 us (10%)
  matrix products  10 us (9%)
  local copies, waits for them, and re-layouts  5.93 us (5%)
  other arithmetic  2.27 us (2%)
    all_to_all x1, waiting for transfers between devices, local(): mine = lax.all_to_all(sent, ('x', 'z'), 0, 0, tiled=True)  17.3 us
    all_to_all x1, waiting for transfers between devices, local(): results = lax.all_to_all(back, ALL, 0, 0, tiled=True)  13.9 us
    all_to_all x1, waiting for transfers between devices, local(): lax.all_to_all(sent.reshape(n_xz * tp_count, rows_dev, pair_cols), ('x',...  12.7 us
    all_to_all x1, waiting for transfers between devices, local(): arrived_slots = lax.all_to_all(outgoing, DP, 0, 0, tiled=True)  11.7 us
    pallas_call x1, Pallas kernels, expert_ffn(): pl.pallas_call(ffn_kernel, grid=(ff // chunk,), in_specs=[pl.BlockSpec((s...  11.3 us
    all_to_all x1, starting transfers between devices, local(): lax.all_to_all(sent.reshape(n_xz * tp_count, rows_dev, pair_cols), ('x',...  8.83 us
    all_to_all x1, starting transfers between devices, local(): mine = lax.all_to_all(sent, ('x', 'z'), 0, 0, tiled=True)  8.55 us
    all_to_all x1, starting transfers between devices, local(): arrived_slots = lax.all_to_all(outgoing, DP, 0, 0, tiled=True)  7.04 us
  transfers between devices with their start and end apart: 5, of which 5 were waited for; matrix products, arithmetic and copies ran while one was open for 2% of the time, Pallas kernels for 0%

profile of v13, /device:TPU:1, one launch (start us, length us, event | category | flops | bytes accessed | tf_op | source)
XLA Modules:
  0.0 115.9 jit_solution(5533651179740632011)
XLA Ops:
  0.0 0.9 copy.48
  0.9 0.7 iota_compare_fusion.1
  1.7 3.8 %fusion.42 = (f32[24,16]{1,0:T(8,128)S(1)}, f32[24,16,768]{2,1,0:T(8,128)S(1)}) fusion(bf16[24,16,128]{2,1,0:T(8,128)(2,1)S(1)} %bitcast.67, bf16[24,1,768,128]{3,2,1,0:T(8,128)(2,1)} %param.13, pred[24,768]{1,0:T(8,128)(4,1)S(1)} %iota_compare_fusion.1), kind=kOutput, calls=%fused_computation.58 | convolution fusion | flops 76677888 | bytes 6016512 | tf_op jit(solution)/shard_map/sub | solution.py:113
  5.5 3.2 %fusion.14 = bf16[24,16,128]{2,1,0:T(8,128)(2,1)S(1)} fusion(bf16[24,1,768,128]{3,2,1,0:T(8,128)(2,1)} %param.14, f32[24,16,768]{2,1,0:T(8,128)S(1)} %get-tuple-element.10, f32[24,16]{1,0:T(8,128)S(1)} %get-tuple-element.9), kind=kOutput, calls=%fused_computation.13 | convolution fusion | flops 76136448 | bytes 5998080 | tf_op jit(solution)/shard_map/rhgl,rhld->rhgd/dot_general | solution.py:115
  8.7 1.3 %broadcast_in_dim.66 = bf16[16,24,2048]{2,1,0:T(8,128)(2,1)} broadcast(bf16[24,2048]{1,0:T(8,128)(2,1)S(1)} %bitcast.66), dimensions={1,2} | broadcast | bytes 1671168 | tf_op jit(solution)/shard_map/broadcast_in_dim | solution.py:124
  10.0 0.0 copy-start.1
  10.0 0.0 copy-start.4
  10.0 8.5 %all-to-all-start = ((bf16[16,24,2048]{2,1,0:T(8,128)(2,1)}), bf16[16,24,2048]{2,1,0:T(8,128)(2,1)S(1)}, u32[]{:S(2)}, u32[]{:S(2)}) async-start(bf16[16,24,2048]{2,1,0:T(8,128)(2,1)} %broadcast_in_dim.66), calls=%async_computation | async-start | bytes 3145728 | tf_op jit(solution)/shard_map/all_to_all | solution.py:125
  18.6 0.0 copy-done.1
  18.6 1.0 collective-permute-start
  19.6 0.0 copy-done.4
  19.6 0.1 copy.38
  19.7 1.5 %collective-permute-done = bf16[2048,128]{1,0:T(8,128)(2,1)S(1)} collective-permute-done((bf16[2048,128]{1,0:T(8,128)(2,1)S(1)}, bf16[2048,128]{1,0:T(8,128)(2,1)S(1)}, u32[]{:S(2)}, u32[]{:S(2)}) %collective-permute-start) | collective-permute-done | bytes 524320 | tf_op jit(solution)/shard_map/ppermute | solution.py:120
  21.2 0.9 broadcast_select_fusion.1
  22.1 17.3 %all-to-all-done = bf16[16,24,2048]{2,1,0:T(8,128)(2,1)S(1)} async-done(((bf16[16,24,2048]{2,1,0:T(8,128)(2,1)}), bf16[16,24,2048]{2,1,0:T(8,128)(2,1)S(1)}, u32[]{:S(2)}, u32[]{:S(2)}) %all-to-all-start) | async-done | bytes 1572896 | tf_op jit(solution)/shard_map/all_to_all | solution.py:125
  39.3 1.7 %convolution_convert_fusion.1 = bf16[16,24,256]{2,1,0:T(8,128)(2,1)S(1)} fusion(bf16[16,24,2048]{2,1,0:T(8,128)(2,1)S(1)} %all-to-all-done, bf16[2048,128]{1,0:T(8,128)(2,1)} %get-tuple-element.8, bf16[2048,128]{1,0:T(8,128)(2,1)S(1)} %get-tuple-element.7), kind=kOutput, calls=%fused_computation.12 | convolution fusion | flops 404848640 | bytes 2818048 | tf_op jit(solution)/shard_map/ird,dc->irc/dot_general | solution.py:126
  41.0 0.9 broadcast_in_dim.67
  41.9 8.8 %all-to-all-start.1 = ((bf16[64,24,256]{2,1,0:T(8,128)(2,1)}), bf16[64,24,256]{2,1,0:T(8,128)(2,1)S(1)}, u32[]{:S(2)}, u32[]{:S(2)}) async-start(bf16[64,24,256]{2,1,0:T(8,128)(2,1)} %bitcast.3), calls=%async_computation.1 | async-start | bytes 1572864 | tf_op jit(solution)/shard_map/all_to_all | solution.py:132
  50.8 0.0 copy-start.2
  50.8 0.1 convert_reduce_fusion
  50.9 0.1 copy.42
  51.0 0.1 copy.41
  51.1 0.1 copy.43
  51.3 0.1 copy.44
  51.4 12.7 %all-to-all-done.1 = bf16[64,24,256]{2,1,0:T(8,128)(2,1)S(1)} async-done(((bf16[64,24,256]{2,1,0:T(8,128)(2,1)}), bf16[64,24,256]{2,1,0:T(8,128)(2,1)S(1)}, u32[]{:S(2)}, u32[]{:S(2)}) %all-to-all-start.1) | async-done | bytes 786464 | tf_op jit(solution)/shard_map/all_to_all | solution.py:132
  64.1 0.1 bitcast_reduce_fusion
  64.3 0.0 copy-done.2
  64.3 0.2 fusion.23
  64.5 0.0 copy-start.3
  64.5 0.4 fusion.5
  64.8 1.3 %copy.45 = bf16[32,1,2,4096]{3,2,1,0:T(2,128)(2,1)} copy(bf16[32,1,2,4096]{3,0,2,1:T(8,128)(2,1)S(1)} %fusion.5) | data formatting | bytes 1048576 | tf_op jit(solution)/shard_map/convert_element_type | solution.py:154
  66.2 7.0 %all-to-all-start.2 = ((bf16[32,1,2,4096]{3,2,1,0:T(2,128)(2,1)}), bf16[32,1,2,4096]{3,2,1,0:T(2,128)(2,1)S(1)}, u32[]{:S(2)}, u32[]{:S(2)}) async-start(bf16[32,1,2,4096]{3,2,1,0:T(2,128)(2,1)} %copy.45), calls=%async_computation.2 | async-start | bytes 1048576 | tf_op jit(solution)/shard_map/all_to_all | solution.py:155
  73.2 0.0 copy-done.3
  73.3 11.7 %all-to-all-done.2 = bf16[32,1,2,4096]{3,2,1,0:T(2,128)(2,1)S(1)} async-done(((bf16[32,1,2,4096]{3,2,1,0:T(2,128)(2,1)}), bf16[32,1,2,4096]{3,2,1,0:T(2,128)(2,1)S(1)}, u32[]{:S(2)}, u32[]{:S(2)}) %all-to-all-start.2) | async-done | bytes 524320 | tf_op jit(solution)/shard_map/all_to_all | solution.py:155
  84.9 0.0 copy-start
  84.9 0.8 copy-done
  85.7 11.3 %shard_map.109 = bf16[32,4,2,1024]{3,2,1,0:T(2,128)(2,1)} custom-call(bf16[32,2,4096]{2,1,0:T(2,128)(2,1)} %bitcast.62, bf16[4096,768]{1,0:T(8,128)(2,1)} %bitcast.58, bf16[4096,768]{1,0:T(8,128)(2,1)} %bitcast.59, bf16[768,4096]{1,0:T(8,128)(2,1)} %bitcast.60), custom_call_target="tpu_custom_call" | custom-call | flops 1207959552 | bytes 19922944 | tf_op jit(solution)/shard_map/pallas_call | solution.py:56
  97.0 3.8 %all-to-all-start.3 = ((bf16[128,2,1024]{2,1,0:T(2,128)(2,1)}), bf16[128,2,1024]{2,1,0:T(2,128)(2,1)S(1)}, u32[]{:S(2)}, u32[]{:S(2)}) async-start(bf16[128,2,1024]{2,1,0:T(2,128)(2,1)} %bitcast.61), calls=%async_computation.3 | async-start | bytes 1048576 | tf_op jit(solution)/shard_map/all_to_all | solution.py:162
  100.8 0.1 copy.40
  100.9 0.1 select_reduce_fusion
  101.0 13.9 %all-to-all-done.3 = bf16[128,2,1024]{2,1,0:T(2,128)(2,1)S(1)} async-done(((bf16[128,2,1024]{2,1,0:T(2,128)(2,1)}), bf16[128,2,1024]{2,1,0:T(2,128)(2,1)S(1)}, u32[]{:S(2)}, u32[]{:S(2)}) %all-to-all-start.3) | async-done | bytes 524320 | tf_op jit(solution)/shard_map/all_to_all | solution.py:162
  114.9 1.0 fusion.18
  (13 shorter events, 0.2 us)
Async XLA Ops:
  10.0 8.6 %copy-start.1 = (bf16[2048,128]{1,0:T(8,128)(2,1)S(1)}, bf16[2048,128]{1,0:T(8,128)(2,1)}, u32[]{:S(2)}) copy-start(bf16[2048,128]{1,0:T(8,128)(2,1)} %param.16) | copy-start | bytes 1572868
  10.0 9.6 %copy-start.4 = (s32[24,8]{0,1:T(8,128)S(1)}, s32[24,8]{0,1:T(8,128)}, u32[]{:S(2)}) copy-start(s32[24,8]{0,1:T(8,128)} %param.17) | copy-start | bytes 2308
  10.0 29.3 %all-to-all-start = ((bf16[16,24,2048]{2,1,0:T(8,128)(2,1)}), bf16[16,24,2048]{2,1,0:T(8,128)(2,1)S(1)}, u32[]{:S(2)}, u32[]{:S(2)}) async-start(bf16[16,24,2048]{2,1,0:T(8,128)(2,1)} %broadcast_in_dim.66), calls=%async_computation | async-start | bytes 3145728 | tf_op jit(solution)/shard_map/all_to_all | solution.py:125
  18.6 2.6 %collective-permute-start = (bf16[2048,128]{1,0:T(8,128)(2,1)S(1)}, bf16[2048,128]{1,0:T(8,128)(2,1)S(1)}, u32[]{:S(2)}, u32[]{:S(2)}) collective-permute-start(bf16[2048,128]{1,0:T(8,128)(2,1)S(1)} %copy-done.1), channel_id=1, source_target_pairs={{0,4},{4,0},{1,5},{5,1},{2,6},{6,2},{3,7},{7,3},{8,12},{12,8},{9,1... | collective-permute-start | bytes 1572872 | tf_op jit(solution)/shard_map/ppermute | solution.py:120
  41.9 22.2 %all-to-all-start.1 = ((bf16[64,24,256]{2,1,0:T(8,128)(2,1)}), bf16[64,24,256]{2,1,0:T(8,128)(2,1)S(1)}, u32[]{:S(2)}, u32[]{:S(2)}) async-start(bf16[64,24,256]{2,1,0:T(8,128)(2,1)} %bitcast.3), calls=%async_computation.1 | async-start | bytes 1572864 | tf_op jit(solution)/shard_map/all_to_all | solution.py:132
  50.8 13.5 %copy-start.2 = (bf16[24,4096]{1,0:T(8,128)(2,1)S(1)}, bf16[24,4096]{1,0:T(8,128)(2,1)}, u32[]{:S(2)}) copy-start(bf16[24,4096]{1,0:T(8,128)(2,1)} %param.11) | copy-start | bytes 589828
  64.5 8.8 %copy-start.3 = (f32[24,8]{0,1:T(8,128)S(1)}, f32[24,8]{0,1:T(8,128)}, u32[]{:S(2)}) copy-start(f32[24,8]{0,1:T(8,128)} %param.18) | copy-start | bytes 2308
  66.2 18.8 %all-to-all-start.2 = ((bf16[32,1,2,4096]{3,2,1,0:T(2,128)(2,1)}), bf16[32,1,2,4096]{3,2,1,0:T(2,128)(2,1)S(1)}, u32[]{:S(2)}, u32[]{:S(2)}) async-start(bf16[32,1,2,4096]{3,2,1,0:T(2,128)(2,1)} %copy.45), calls=%async_computation.2 | async-start | bytes 1048576 | tf_op jit(solution)/shard_map/all_to_all | solution.py:155
  84.9 0.8 copy-start
  97.0 17.9 %all-to-all-start.3 = ((bf16[128,2,1024]{2,1,0:T(2,128)(2,1)}), bf16[128,2,1024]{2,1,0:T(2,128)(2,1)S(1)}, u32[]{:S(2)}, u32[]{:S(2)}) async-start(bf16[128,2,1024]{2,1,0:T(2,128)(2,1)} %bitcast.61), calls=%async_computation.3 | async-start | bytes 1048576 | tf_op jit(solution)/shard_map/all_to_all | solution.py:162
